TPU v7x, 512 devices: a whole 4x8x8 slice. The times are simulated.
512 devices in a mesh: ind: 64 (over y, z), snp: 8 (over x, core).
Axes of the slice: x: 4, y: 8, z: 8, core: 2. Of those that a mesh axis runs over, the one named last changes fastest.
Arguments:
- genotypes: int32 [4096, 16384], P('ind', 'snp'), may hold values from 0 to 2
- observed: int32 [4096, 16384], P('ind', 'snp'), may hold values from 0 to 1
- ancestry: float32 [4096, 32], P('ind'), may hold values from 0.018 to 54.6, as said below
- freqs: float32 [16384, 32], P(('snp', 'ind')), may hold values from 0.05 to 0.95
Outputs:
- ancestry_out: float32 [4096, 32], P('ind')
- freqs_out: float32 [16384, 32], P(('snp', 'ind'))
Inputs may be any that keep to these rules, and one draw needn't show every extreme that they name: `ancestry`: positive weights.
All inputs are finite; a program needn't handle non-finite values.
Results may differ from a plain program's by a relative error of at most 0.0003.
Values sent between devices are 32-bit elements; how exact they have to be, the bound alone decides.
No kernel may reach another device: no remote copies, remote signals or barrier semaphores. Data moves between devices by JAX's collectives and lax.ppermute only.
A program may use at most 64 MiB of HBM per device.

v0:
```python
import jax
import jax.numpy as jnp
from jax import lax
from jax.sharding import PartitionSpec as P

STEPS = 3


clip_low = 1e-05
high = lax.Precision.HIGHEST


def over_rows(left, right):
    return lax.dot_general(
        left, right, (((0,), (0,)), ((), ())), precision=high, preferred_element_type=jnp.float32
    )


def per_device(genotypes, observed, ancestry, freqs):
    ind_count = lax.axis_size("ind")
    snp_count = lax.axis_size("snp")
    geno = genotypes.astype(jnp.float32)
    seen = observed.astype(jnp.float32)
    hits = seen * geno
    misses = seen * (2.0 - geno)
    own_rows = freqs.shape[0]
    q_zero = ancestry / jnp.sum(ancestry, axis=1, keepdims=True)
    f_zero = lax.all_gather(freqs, "ind", axis=0, tiled=True)
    f_weight = 1.0 / ind_count
    q_weight = 1.0 / snp_count

    def em_map(q_rows, f_state):
        prob = jnp.dot(q_rows, f_state.T, precision=high, preferred_element_type=jnp.float32)
        ratio_a = hits / prob
        ratio_b = misses / (1.0 - prob)
        sum_a = jnp.dot(ratio_a, f_state, precision=high, preferred_element_type=jnp.float32)
        sum_b = jnp.dot(ratio_b, 1.0 - f_state, precision=high, preferred_element_type=jnp.float32)
        c_part = over_rows(ratio_a, q_rows)
        d_part = over_rows(ratio_b, q_rows)
        sum_a, sum_b = lax.psum((sum_a, sum_b), "snp")
        q_next = q_rows * (sum_a + sum_b)
        q_next = q_next / jnp.sum(q_next, axis=1, keepdims=True)
        c_total, d_total = lax.psum((c_part, d_part), "ind")
        f_next = f_state * c_total / (f_state * c_total + (1.0 - f_state) * d_total)
        return (q_next, f_next)

    for step in range(STEPS):
        q_one, f_one = em_map(q_zero, f_zero)
        rq = q_one - q_zero
        rf = f_one - f_zero
        first_local = q_weight * jnp.sum(rq * rq) + f_weight * jnp.sum(rf * rf)
        q_two, f_two = em_map(q_one, f_one)
        vq = q_two - 2.0 * q_one + q_zero
        vf = f_two - 2.0 * f_one + f_zero
        second_local = q_weight * jnp.sum(vq * vq) + f_weight * jnp.sum(vf * vf)
        first, second = lax.psum((first_local, second_local), ("ind", "snp"))
        alpha = -jnp.sqrt(first / (second + 1e-20))
        q_ext = jnp.clip(q_zero - 2.0 * alpha * rq + alpha * alpha * vq, clip_low, 1.0 - clip_low)
        q_zero = q_ext / jnp.sum(q_ext, axis=1, keepdims=True)
        f_zero = jnp.clip(f_zero - 2.0 * alpha * rf + alpha * alpha * vf, clip_low, 1.0 - clip_low)
    f_final = lax.dynamic_slice_in_dim(f_zero, lax.axis_index("ind") * own_rows, own_rows, 0)
    return (q_zero, f_final)


def solution(mesh):
    in_specs = (P("ind", "snp"), P("ind", "snp"), P("ind", None), P(("snp", "ind"), None))
    out_specs = (P("ind", None), P(("snp", "ind"), None))
    return jax.shard_map(
        per_device, mesh=mesh, in_specs=in_specs, out_specs=out_specs, check_vma=False
    )
```

profile of v0, /device:TPU:1, one launch (start us, length us, event | category | flops | bytes accessed | tf_op | source)
XLA Modules:
  0.0 1308.1 jit_solution(10451656634871468365)
XLA Ops:
  7.2 47.0 %all_gather.3 = f32[2048,32]{1,0:T(8,128)S(1)} all-gather(f32[32,32]{1,0:T(8,128)} %param.7), channel_id=1, replica_groups=mesh['ind'=64,'snp'=8] {'ind'}, dimensions={0}, use_global_device_ids=true | all-gather | bytes 266240 | tf_op jit(solution)/shard_map/all_gather | solution.py:28
  54.3 1.3 fusion.48
  55.6 0.1 convert_multiply_fusion
  55.7 1.2 fusion.46
  56.9 1.2 fusion.45
  58.2 0.0 all-reduce.24.cloned.1.call-start
  58.2 0.3 copy.8
  58.5 0.6 fusion.11
  59.1 1.8 convolution_add_fusion
  60.9 32.1 %psum.240 = f32[64,32]{0,1:T(8,128)S(1)} all-reduce(f32[64,32]{0,1:T(8,128)S(1)} %convolution_add_fusion), channel_id=1, replica_groups=mesh['ind'=64,'snp'=8] {'snp'}, use_global_device_ids=true, to_apply=%region_1.0 | all-reduce | flops 2048 | bytes 16384 | tf_op jit(solution)/shard_map/psum | solution.py:40
  93.0 123.9 %all-reduce.26.cloned.1.call-done = (f32[2048,32]{0,1:T(8,128)}, f32[2048,32]{0,1:T(8,128)}) async-done(((f32[2048,32]{0,1:T(8,128)}, f32[2048,32]{0,1:T(8,128)}), (f32[2048,32]{0,1:T(8,128)}, f32[2048,32]{0,1:T(8,128)})) %all-reduce.26.cloned.1.call-update) | async-done | bytes 524304 | tf_op jit(solution)/shard_map/psum | solution.py:43
  216.9 1.7 multiply_reduce_fusion.5
  218.6 0.6 fusion.30
  219.2 1.2 fusion.27
  220.4 1.2 fusion.28
  221.7 0.6 fusion.72
  222.3 0.6 convolution_add_fusion.5
  222.9 24.9 %psum.241 = f32[64,32]{0,1:T(8,128)S(1)} all-reduce(f32[64,32]{0,1:T(8,128)S(1)} %convolution_add_fusion.5), channel_id=1, replica_groups=mesh['ind'=64,'snp'=8] {'snp'}, use_global_device_ids=true, to_apply=%region_9.0 | all-reduce | flops 2048 | bytes 16384 | tf_op jit(solution)/shard_map/psum | solution.py:40
  247.8 0.7 multiply_reduce_fusion.10
  250.5 123.8 %all-reduce.24.cloned.1.call-done = (f32[2048,32]{0,1:T(8,128)}, f32[2048,32]{0,1:T(8,128)}) async-done(((f32[2048,32]{0,1:T(8,128)}, f32[2048,32]{0,1:T(8,128)}), (f32[2048,32]{0,1:T(8,128)}, f32[2048,32]{0,1:T(8,128)})) %all-reduce.24.cloned.1.call-update) | async-done | bytes 524304 | tf_op jit(solution)/shard_map/psum | solution.py:43
  374.3 1.7 multiply_reduce_fusion.4
  376.7 99.3 %all-reduce.2 = (f32[]{:T(128)}, f32[]{:T(128)}) all-reduce(f32[]{:T(128)S(6)} %add.164, f32[]{:T(128)S(6)} %add.169), channel_id=1, replica_groups=mesh['ind'=64,'snp'=8] {'ind','snp'}, use_global_device_ids=true, to_apply=%region_8.0 | all-reduce | flops 2 | bytes 16 | tf_op jit(solution)/shard_map/psum | solution.py:56
  477.4 0.1 add_clamp_fusion.1
  477.5 0.6 fusion.52
  478.1 1.2 fusion.49
  479.3 1.2 fusion.50
  480.6 0.0 all-reduce.20.cloned.1.call-start
  480.6 0.6 fusion.69
  481.2 0.6 convolution_add_fusion.4
  481.8 20.9 %psum.242 = f32[64,32]{0,1:T(8,128)S(1)} all-reduce(f32[64,32]{0,1:T(8,128)S(1)} %convolution_add_fusion.4), channel_id=1, replica_groups=mesh['ind'=64,'snp'=8] {'snp'}, use_global_device_ids=true, to_apply=%region_18.19 | all-reduce | flops 2048 | bytes 16384 | tf_op jit(solution)/shard_map/psum | solution.py:40
  502.7 125.4 %all-reduce.22.cloned.1.call-done = (f32[2048,32]{0,1:T(8,128)}, f32[2048,32]{0,1:T(8,128)}) async-done(((f32[2048,32]{0,1:T(8,128)}, f32[2048,32]{0,1:T(8,128)}), (f32[2048,32]{0,1:T(8,128)}, f32[2048,32]{0,1:T(8,128)})) %all-reduce.22.cloned.1.call-update) | async-done | bytes 524304 | tf_op jit(solution)/shard_map/psum | solution.py:43
  628.1 1.7 multiply_reduce_fusion.3
  629.8 0.6 fusion.36
  630.4 1.2 fusion.33
  631.7 1.2 fusion.34
  633.0 0.6 fusion.66
  634.2 0.6 convolution_add_fusion.3
  634.8 24.9 %psum.243 = f32[64,32]{0,1:T(8,128)S(1)} all-reduce(f32[64,32]{0,1:T(8,128)S(1)} %convolution_add_fusion.3), channel_id=1, replica_groups=mesh['ind'=64,'snp'=8] {'snp'}, use_global_device_ids=true, to_apply=%region_26.27 | all-reduce | flops 2048 | bytes 16384 | tf_op jit(solution)/shard_map/psum | solution.py:40
  659.7 0.6 multiply_reduce_fusion.8
  661.6 123.9 %all-reduce.20.cloned.1.call-done = (f32[2048,32]{0,1:T(8,128)}, f32[2048,32]{0,1:T(8,128)}) async-done(((f32[2048,32]{0,1:T(8,128)}, f32[2048,32]{0,1:T(8,128)}), (f32[2048,32]{0,1:T(8,128)}, f32[2048,32]{0,1:T(8,128)})) %all-reduce.20.cloned.1.call-update) | async-done | bytes 524304 | tf_op jit(solution)/shard_map/psum | solution.py:43
  785.6 1.7 multiply_reduce_fusion.2
  787.9 99.4 %all-reduce.1 = (f32[]{:T(128)}, f32[]{:T(128)}) all-reduce(f32[]{:T(128)S(6)} %add.175, f32[]{:T(128)S(6)} %add.180), channel_id=1, replica_groups=mesh['ind'=64,'snp'=8] {'ind','snp'}, use_global_device_ids=true, to_apply=%region_25.26 | all-reduce | flops 2 | bytes 16 | tf_op jit(solution)/shard_map/psum | solution.py:56
  888.7 0.1 add_clamp_fusion
  888.7 0.6 fusion.56
  889.4 1.2 fusion.53
  890.6 1.2 fusion.54
  891.9 0.6 fusion.63
  892.5 0.6 convolution_add_fusion.2
  893.1 20.8 %psum.244 = f32[64,32]{0,1:T(8,128)S(1)} all-reduce(f32[64,32]{0,1:T(8,128)S(1)} %convolution_add_fusion.2), channel_id=1, replica_groups=mesh['ind'=64,'snp'=8] {'snp'}, use_global_device_ids=true, to_apply=%region_35.36 | all-reduce | flops 2048 | bytes 16384 | tf_op jit(solution)/shard_map/psum | solution.py:40
  913.9 125.4 %all-reduce.18.cloned.1.call-done = (f32[2048,32]{0,1:T(8,128)}, f32[2048,32]{0,1:T(8,128)}) async-done(((f32[2048,32]{0,1:T(8,128)}, f32[2048,32]{0,1:T(8,128)}), (f32[2048,32]{0,1:T(8,128)}, f32[2048,32]{0,1:T(8,128)})) %all-reduce.18.cloned.1.call-update) | async-done | bytes 524304 | tf_op jit(solution)/shard_map/psum | solution.py:43
  1039.3 1.7 multiply_reduce_fusion.1
  1041.0 0.6 fusion.42
  1041.6 1.2 fusion.40
  1042.9 1.2 fusion.39
  1044.1 0.6 fusion.60
  1045.3 0.6 convolution_add_fusion.1
  1045.9 24.9 %psum.245 = f32[64,32]{0,1:T(8,128)S(1)} all-reduce(f32[64,32]{0,1:T(8,128)S(1)} %convolution_add_fusion.1), channel_id=1, replica_groups=mesh['ind'=64,'snp'=8] {'snp'}, use_global_device_ids=true, to_apply=%region_43.44 | all-reduce | flops 2048 | bytes 16384 | tf_op jit(solution)/shard_map/psum | solution.py:40
  1070.9 0.6 multiply_reduce_fusion.6
  1072.8 124.0 %all-reduce.16.cloned.1.call-done = (f32[2048,32]{0,1:T(8,128)}, f32[2048,32]{0,1:T(8,128)}) async-done(((f32[2048,32]{0,1:T(8,128)}, f32[2048,32]{0,1:T(8,128)}), (f32[2048,32]{0,1:T(8,128)}, f32[2048,32]{0,1:T(8,128)})) %all-reduce.16.cloned.1.call-update) | async-done | bytes 524304 | tf_op jit(solution)/shard_map/psum | solution.py:43
  1196.8 1.7 multiply_reduce_fusion
  1199.2 99.3 %all-reduce = (f32[]{:T(128)}, f32[]{:T(128)}) all-reduce(f32[]{:T(128)S(6)} %add.186, f32[]{:T(128)S(6)} %add.191), channel_id=1, replica_groups=mesh['ind'=64,'snp'=8] {'ind','snp'}, use_global_device_ids=true, to_apply=%region_42.43 | all-reduce | flops 2 | bytes 16 | tf_op jit(solution)/shard_map/psum | solution.py:56
  1299.9 0.1 fusion.20
  1300.0 0.7 copy.13
  1300.7 0.6 broadcast_divide_fusion
  (26 shorter events, 0.6 us)
Async XLA Ops:
  7.2 47.0 %copy-start.2 = (f32[64,32]{0,1:T(8,128)S(1)}, f32[64,32]{0,1:T(8,128)}, u32[]{:S(2)}) copy-start(f32[64,32]{0,1:T(8,128)} %param.6) | copy-start | bytes 24580
  7.2 209.7 %all-reduce.26.cloned.1.call-start = ((), (), s32[]{:S(2)}) async-start(), calls=%async_computation.5 | async-start | bytes 1048576 | tf_op jit(solution)/shard_map/psum | solution.py:43
  54.2 1.3 copy-start
  54.2 1.3 copy-start.1
  58.2 316.1 %all-reduce.24.cloned.1.call-start = ((), (), s32[]{:S(2)}) async-start(), calls=%async_computation.4 | async-start | bytes 1048576 | tf_op jit(solution)/shard_map/psum | solution.py:43
  221.7 406.4 %all-reduce.22.cloned.1.call-start = ((), (), s32[]{:S(2)}) async-start(), calls=%async_computation.3 | async-start | bytes 1048576 | tf_op jit(solution)/shard_map/psum | solution.py:43
  480.6 305.0 %all-reduce.20.cloned.1.call-start = ((), (), s32[]{:S(2)}) async-start(), calls=%async_computation.2 | async-start | bytes 1048576 | tf_op jit(solution)/shard_map/psum | solution.py:43
  632.9 406.4 %all-reduce.18.cloned.1.call-start = ((), (), s32[]{:S(2)}) async-start(), calls=%async_computation.1 | async-start | bytes 1048576 | tf_op jit(solution)/shard_map/psum | solution.py:43
  891.8 304.9 %all-reduce.16.cloned.1.call-start = ((), (), s32[]{:S(2)}) async-start(), calls=%async_computation | async-start | bytes 1048576 | tf_op jit(solution)/shard_map/psum | solution.py:43
Sparse Core Ops, SparseCore 0:
  58.3 158.5 all-reduce.25
  221.8 152.4 all-reduce.23
  480.7 147.3 all-reduce.21
  633.0 152.4 all-reduce.19
  892.0 147.2 all-reduce.17
  1044.2 152.5 all-reduce.15
where the time goes:
time: 1310 us
  waiting for transfers between devices  746 us (57%)
  blocking collectives  494 us (38%)
  matrix products  27.2 us (2%)
  between operations  26.2 us (2%)
  other arithmetic  13.5 us (1%)
    psum x6, waiting for transfers between devices, em_map(): c_total, d_total = lax.psum((c_part, d_part), 'ind')  746 us
    psum x3, blocking collectives, per_device(): first, second = lax.psum((first_local, second_local), ('ind', 'snp'))  298 us
    psum x6, blocking collectives, em_map(): sum_a, sum_b = lax.psum((sum_a, sum_b), 'snp')  148 us
    all_gather x1, blocking collectives, per_device(): f_zero = lax.all_gather(freqs, 'ind', axis=0, tiled=True)  47 us
  transfers between devices with their start and end apart: 6, of which 6 were waited for; matrix products, arithmetic and copies ran while one was open for 1% of the time, Pallas kernels for 0%

commit v1 on v0

v1 whole, which is shorter than its diff:
```python
import jax
import jax.numpy as jnp
from jax import lax
from jax.sharding import Mesh
from jax.sharding import PartitionSpec as P

STEPS = 3


clip_low = 1e-05
high = lax.Precision.HIGHEST

IND_AXES = ("yh", "yl", "z")
SNP_AXES = ("x", "c")
ROW_GROUP = ("yl", "z")
COL_GROUP = ("c", "x", "yh")


def doubling_sum(value, axes):
    for name in axes:
        size = lax.axis_size(name)
        step = 1
        while step < size:
            pairs = [(j, j ^ step) for j in range(size)]
            value = value + lax.ppermute(value, name, pairs)
            step *= 2
    return value


def per_device(genotypes, observed, ancestry, freqs):
    quarter = lax.axis_size("yh")
    geno = genotypes.astype(jnp.float32)
    seen = observed.astype(jnp.float32)
    counts = jnp.stack([seen * geno, seen * (2.0 - geno)])
    counts = lax.all_to_all(counts, "yh", 2, 1, tiled=True)
    hits, misses = counts[0], counts[1]
    own_rows = ancestry.shape[0]
    own_snps = freqs.shape[0]
    q_own = ancestry / jnp.sum(ancestry, axis=1, keepdims=True)
    q_zero = lax.all_gather(q_own, "yh", axis=0, tiled=True)
    f_zero = lax.all_gather(freqs, ROW_GROUP, axis=0, tiled=True)

    def em_map(q_rows, f_state):
        prob = jnp.dot(q_rows, f_state.T, precision=high, preferred_element_type=jnp.float32)
        ratio_a = hits / prob
        ratio_b = misses / (1.0 - prob)
        sum_a = jnp.dot(ratio_a, f_state, precision=high, preferred_element_type=jnp.float32)
        sum_b = jnp.dot(ratio_b, 1.0 - f_state, precision=high, preferred_element_type=jnp.float32)
        c_part = lax.dot_general(
            ratio_a, q_rows, (((0,), (0,)), ((), ())), precision=high, preferred_element_type=jnp.float32
        )
        d_part = lax.dot_general(
            ratio_b, q_rows, (((0,), (0,)), ((), ())), precision=high, preferred_element_type=jnp.float32
        )
        q_sum = doubling_sum(sum_a + sum_b, COL_GROUP)
        cd_total = doubling_sum(jnp.concatenate([c_part, d_part], axis=1), ROW_GROUP)
        q_next = q_rows * q_sum
        q_next = q_next / jnp.sum(q_next, axis=1, keepdims=True)
        width = f_state.shape[1]
        c_total, d_total = cd_total[:, :width], cd_total[:, width:]
        f_next = f_state * c_total / (f_state * c_total + (1.0 - f_state) * d_total)
        return (q_next, f_next)

    for step in range(STEPS):
        q_one, f_one = em_map(q_zero, f_zero)
        q_two, f_two = em_map(q_one, f_one)
        rq = q_one - q_zero
        rf = f_one - f_zero
        vq = q_two - 2.0 * q_one + q_zero
        vf = f_two - 2.0 * f_one + f_zero
        q_parts = doubling_sum(jnp.stack([jnp.sum(rq * rq), jnp.sum(vq * vq)]), ROW_GROUP)
        f_parts = doubling_sum(jnp.stack([jnp.sum(rf * rf), jnp.sum(vf * vf)]), COL_GROUP)
        first = q_parts[0] + f_parts[0]
        second = q_parts[1] + f_parts[1]
        alpha = -jnp.sqrt(first / (second + 1e-20))
        q_ext = jnp.clip(q_zero - 2.0 * alpha * rq + alpha * alpha * vq, clip_low, 1.0 - clip_low)
        q_zero = q_ext / jnp.sum(q_ext, axis=1, keepdims=True)
        f_zero = jnp.clip(f_zero - 2.0 * alpha * rf + alpha * alpha * vf, clip_low, 1.0 - clip_low)
    q_final = lax.dynamic_slice_in_dim(q_zero, lax.axis_index("yh") * own_rows, own_rows, 0)
    f_index = lax.axis_index("yl") * lax.axis_size("z") + lax.axis_index("z")
    f_final = lax.dynamic_slice_in_dim(f_zero, f_index * own_snps, own_snps, 0)
    del quarter
    return (q_final, f_final)


def solution(mesh):
    ind_size = mesh.shape["ind"]
    snp_size = mesh.shape["snp"]
    quarter = 4
    lanes = ind_size // quarter
    view = Mesh(
        mesh.devices.reshape(quarter, 2, lanes // 2, snp_size // 2, 2),
        ("yh", "yl", "z", "x", "c"),
    )
    in_specs = (
        P(IND_AXES, SNP_AXES),
        P(IND_AXES, SNP_AXES),
        P(IND_AXES, None),
        P(SNP_AXES + IND_AXES, None),
    )
    out_specs = (P(IND_AXES, None), P(SNP_AXES + IND_AXES, None))
    return jax.shard_map(
        per_device, mesh=view, in_specs=in_specs, out_specs=out_specs, check_vma=False
    )
```

time: 1310 us -> 614 us (0.47)
  waiting for transfers between devices: 746 us -> 109 us
  blocking collectives: 494 us -> 62 us
  starting transfers between devices: 0.25 us -> 356 us
  other arithmetic: 13.5 us -> 39.6 us
  between operations: 26.2 us -> 9.92 us
    psum x6 -> x0, waiting for transfers between devices: 746 us -> none  [em_map(): c_total, d_total = lax.psum((c_part, d_part), 'ind')]
    psum x9 -> x0, blocking collectives: 447 us -> none  [the longest x3 298 us: per_device(): first, second = lax.psum((first_local, second_local), ('ind', 'snp'))]
    ppermute x0 -> x81, starting transfers between devices: none -> 349 us  [doubling_sum(): value = value + lax.ppermute(value, name, pairs)]
    ppermute x0 -> x81, waiting for transfers between devices: none -> 109 us  [doubling_sum(): value = value + lax.ppermute(value, name, pairs)]
    add x0 -> x75, other arithmetic: none -> 16.6 us  [doubling_sum(): value = value + lax.ppermute(value, name, pairs)]
    all_gather x1 -> x2, blocking collectives: 47 us -> 62 us  [the longest x1 32 us: per_device(): q_zero = lax.all_gather(q_own, 'yh', axis=0, tiled=True)]
  transfers between devices with their start and end apart: 6 -> 82, of which waited for: 6 -> 55; matrix products, arithmetic and copies ran while one was open for 1% -> 4% of each run, Pallas kernels for 0% -> 0%
where the time goes in v1:
time: 614 us; the launch traced here: 607 us
  starting transfers between devices  356 us (58%)
  waiting for transfers between devices  109 us (18%)
  blocking collectives  62 us (10%)
  other arithmetic  39.6 us (6%)
  matrix products  16.2 us (3%)
  local copies, waits for them, and re-layouts  13.5 us (2%)
  between operations  9.92 us (2%)
    ppermute x81, starting transfers between devices, doubling_sum(): value = value + lax.ppermute(value, name, pairs)  349 us
    ppermute x81, waiting for transfers between devices, doubling_sum(): value = value + lax.ppermute(value, name, pairs)  109 us
    all_gather x1, blocking collectives, per_device(): q_zero = lax.all_gather(q_own, 'yh', axis=0, tiled=True)  32 us
    all_gather x1, blocking collectives, per_device(): f_zero = lax.all_gather(freqs, ROW_GROUP, axis=0, tiled=True)  30.1 us
    add x75, other arithmetic, doubling_sum(): value = value + lax.ppermute(value, name, pairs)  16.6 us
  transfers between devices with their start and end apart: 82, of which 55 were waited for; matrix products, arithmetic and copies ran while one was open for 4% of the time, Pallas kernels for 0%

profile of v1, /device:TPU:1, one launch (start us, length us, event | category | flops | bytes accessed | tf_op | source)
XLA Modules:
  0.0 606.9 jit_solution(14223782295887713590)
XLA Ops:
  9.1 7.6 %all-to-all-start = ((f32[4,1,65536]{2,1,0:T(1,128)}), f32[4,1,65536]{2,1,0:T(1,128)S(1)}, u32[]{:S(2)}, u32[]{:S(2)}) async-start(f32[4,1,65536]{2,1,0:T(1,128)} %reshape.50), calls=%async_computation | async-start | bytes 2097152 | tf_op jit(solution)/shard_map/all_to_all | solution.py:35
  16.8 32.0 %all-gather = f32[4,64,32]{1,2,0:T(8,128)S(1)} all-gather(f32[1,64,32]{1,2,0:T(8,128)S(1)} %divide_bitcast_fusion), channel_id=1, replica_groups=mesh['yh'=4,'yl'=2,'z'=8,'x'=4,'c'=2] {'yh'}, dimensions={0}, use_global_device_ids=true | all-gather | bytes 40960 | tf_op jit(solution)/shard_map/all_gather | solution.py:40
  48.9 30.1 %all_gather.7 = f32[512,32]{1,0:T(8,128)S(1)} all-gather(f32[32,32]{1,0:T(8,128)S(1)} %copy-done.1), channel_id=1, replica_groups=mesh['yh'=4,'yl'=2,'z'=8,'x'=4,'c'=2] {'yl','z'}, dimensions={0}, use_global_device_ids=true | all-gather | bytes 69632 | tf_op jit(solution)/shard_map/all_gather | solution.py:41
  79.6 3.7 reduce
  87.6 6.2 %collective-permute-start.5 = (f32[512,64]{0,1:T(8,128)S(1)}, f32[512,64]{0,1:T(8,128)S(1)}, u32[]{:S(2)}, u32[]{:S(2)}) collective-permute-start(f32[512,64]{0,1:T(8,128)S(1)} %pad_maximum_fusion.1), channel_id=1, source_target_pairs={{0,64},{64,0},{1,65},{65,1},{2,66},{66,2},{3,67},{67,3},{4,68},{68... | collective-permute-start | bytes 393224 | tf_op jit(solution)/shard_map/ppermute | solution.py:25
  94.9 12.8 %collective-permute-start = (f32[256,32]{0,1:T(8,128)S(1)}, f32[256,32]{0,1:T(8,128)S(1)}, u32[]{:S(2)}, u32[]{:S(2)}) collective-permute-start(f32[256,32]{0,1:T(8,128)S(1)} %convolution_add_fusion), channel_id=1, source_target_pairs={{0,1},{1,0},{2,3},{3,2},{4,5},{5,4},{6,7},{7,6},{8,9},{9,8},{10,11... | collective-permute-start | bytes 98312 | tf_op jit(solution)/shard_map/ppermute | solution.py:25
  109.6 3.1 collective-permute-start.1
  114.6 4.6 collective-permute-start.2
  120.8 3.8 collective-permute-start.3
  126.3 4.1 collective-permute-start.4
  135.0 3.8 collective-permute-done.7
  141.5 6.9 %collective-permute-done.8 = f32[512,64]{0,1:T(8,128)S(1)} collective-permute-done((f32[512,64]{0,1:T(8,128)S(1)}, f32[512,64]{0,1:T(8,128)S(1)}, u32[]{:S(2)}, u32[]{:S(2)}) %collective-permute-start.8) | collective-permute-done | bytes 131104 | tf_op jit(solution)/shard_map/ppermute | solution.py:25
  151.8 6.7 %collective-permute-start.9 = (f32[256,32]{0,1:T(8,128)S(1)}, f32[256,32]{0,1:T(8,128)S(1)}, u32[]{:S(2)}, u32[]{:S(2)}) collective-permute-start(f32[256,32]{0,1:T(8,128)S(1)} %convolution_add_fusion.5), channel_id=1, source_target_pairs={{0,1},{1,0},{2,3},{3,2},{4,5},{5,4},{6,7},{7,6},{8,9},{9,8},{10,11... | collective-permute-start | bytes 98312 | tf_op jit(solution)/shard_map/ppermute | solution.py:25
  161.7 3.1 collective-permute-start.10
  166.3 4.6 collective-permute-start.11
  172.5 4.2 collective-permute-start.12
  178.0 6.4 %collective-permute-start.13 = (f32[256,32]{0,1:T(8,128)S(1)}, f32[256,32]{0,1:T(8,128)S(1)}, u32[]{:S(2)}, u32[]{:S(2)}) collective-permute-start(f32[256,32]{0,1:T(8,128)S(1)} %add.375), channel_id=1, source_target_pairs={{0,256},{128,384},{256,0},{384,128},{1,257},{129,385},{257,1},{385... | collective-permute-start | bytes 98312 | tf_op jit(solution)/shard_map/ppermute | solution.py:25
  184.5 3.7 collective-permute-start.19
  210.0 6.1 %collective-permute-start.17 = (f32[2]{0:T(128)S(1)}, f32[2]{0:T(128)S(1)}, u32[]{:S(2)}, u32[]{:S(2)}) collective-permute-start(f32[2]{0:T(128)S(1)} %add.380), channel_id=1, source_target_pairs={{0,32},{8,40},{16,48},{24,56},{32,0},{40,8},{48,16},{56,24},{1,33}... | collective-permute-start | bytes 32 | tf_op jit(solution)/shard_map/ppermute | solution.py:25
  220.6 10.2 %collective-permute-start.22 = (f32[2]{0:T(128)S(1)}, f32[2]{0:T(128)S(1)}, u32[]{:S(2)}, u32[]{:S(2)}) collective-permute-start(f32[2]{0:T(128)S(1)} %pad_maximum_fusion.8), channel_id=1, source_target_pairs={{0,1},{1,0},{2,3},{3,2},{4,5},{5,4},{6,7},{7,6},{8,9},{9,8},{10,11... | collective-permute-start | bytes 32 | tf_op jit(solution)/shard_map/ppermute | solution.py:25
  238.5 4.6 collective-permute-start.24
  244.3 3.6 collective-permute-start.25
  249.4 4.9 collective-permute-start.26
  254.4 3.3 collective-permute-done.26
  266.2 7.1 %collective-permute-start.27 = (f32[256,32]{0,1:T(8,128)S(1)}, f32[256,32]{0,1:T(8,128)S(1)}, u32[]{:S(2)}, u32[]{:S(2)}) collective-permute-start(f32[256,32]{0,1:T(8,128)S(1)} %convolution_add_fusion.4), channel_id=1, source_target_pairs={{0,1},{1,0},{2,3},{3,2},{4,5},{5,4},{6,7},{7,6},{8,9},{9,8},{10,11... | collective-permute-start | bytes 98312 | tf_op jit(solution)/shard_map/ppermute | solution.py:25
  276.1 3.1 collective-permute-start.28
  281.1 4.6 collective-permute-start.29
  287.2 3.8 collective-permute-start.30
  293.0 5.3 collective-permute-start.31
  301.6 4.8 collective-permute-done.34
  306.4 7.2 %collective-permute-start.35 = (f32[512,64]{0,1:T(8,128)S(1)}, f32[512,64]{0,1:T(8,128)S(1)}, u32[]{:S(2)}, u32[]{:S(2)}) collective-permute-start(f32[512,64]{0,1:T(8,128)S(1)} %add.406), channel_id=1, source_target_pairs={{0,32},{8,40},{16,48},{24,56},{32,0},{40,8},{48,16},{56,24},{1,33}... | collective-permute-start | bytes 393224 | tf_op jit(solution)/shard_map/ppermute | solution.py:25
  319.4 8.8 %collective-permute-start.36 = (f32[256,32]{0,1:T(8,128)S(1)}, f32[256,32]{0,1:T(8,128)S(1)}, u32[]{:S(2)}, u32[]{:S(2)}) collective-permute-start(f32[256,32]{0,1:T(8,128)S(1)} %convolution_add_fusion.3), channel_id=1, source_target_pairs={{0,1},{1,0},{2,3},{3,2},{4,5},{5,4},{6,7},{7,6},{8,9},{9,8},{10,11... | collective-permute-start | bytes 98312 | tf_op jit(solution)/shard_map/ppermute | solution.py:25
  328.2 4.9 collective-permute-start.45
  337.9 4.6 collective-permute-start.38
  344.0 4.5 collective-permute-start.39
  350.1 4.0 collective-permute-start.40
  370.3 7.5 %collective-permute-start.48 = (f32[512,64]{0,1:T(8,128)S(1)}, f32[512,64]{0,1:T(8,128)S(1)}, u32[]{:S(2)}, u32[]{:S(2)}) collective-permute-start(f32[512,64]{0,1:T(8,128)S(1)} %add.422), channel_id=1, source_target_pairs={{0,32},{8,40},{16,48},{24,56},{32,0},{40,8},{48,16},{56,24},{1,33}... | collective-permute-start | bytes 393224 | tf_op jit(solution)/shard_map/ppermute | solution.py:25
  386.6 6.3 %collective-permute-done.44 = f32[2]{0:T(128)S(1)} collective-permute-done((f32[2]{0:T(128)S(1)}, f32[2]{0:T(128)S(1)}, u32[]{:S(2)}, u32[]{:S(2)}) %collective-permute-start.44) | collective-permute-done | bytes 40 | tf_op jit(solution)/shard_map/ppermute | solution.py:25
  395.4 9.5 %collective-permute-start.49 = (f32[2]{0:T(128)S(1)}, f32[2]{0:T(128)S(1)}, u32[]{:S(2)}, u32[]{:S(2)}) collective-permute-start(f32[2]{0:T(128)S(1)} %pad_maximum_fusion.10), channel_id=1, source_target_pairs={{0,1},{1,0},{2,3},{3,2},{4,5},{5,4},{6,7},{7,6},{8,9},{9,8},{10,11... | collective-permute-start | bytes 32 | tf_op jit(solution)/shard_map/ppermute | solution.py:25
  412.5 4.6 collective-permute-start.51
  418.2 4.5 collective-permute-start.52
  423.7 5.9 collective-permute-start.53
  437.3 5.2 collective-permute-start.59
  443.1 6.8 %collective-permute-start.54 = (f32[256,32]{0,1:T(8,128)S(1)}, f32[256,32]{0,1:T(8,128)S(1)}, u32[]{:S(2)}, u32[]{:S(2)}) collective-permute-start(f32[256,32]{0,1:T(8,128)S(1)} %convolution_add_fusion.2), channel_id=1, source_target_pairs={{0,1},{1,0},{2,3},{3,2},{4,5},{5,4},{6,7},{7,6},{8,9},{9,8},{10,11... | collective-permute-start | bytes 98312 | tf_op jit(solution)/shard_map/ppermute | solution.py:25
  451.9 3.1 collective-permute-start.55
  456.9 4.6 collective-permute-start.56
  463.0 4.5 collective-permute-start.57
  468.8 4.5 collective-permute-start.58
  473.4 3.6 collective-permute-start.61
  477.4 4.0 collective-permute-done.61
  483.4 7.7 %collective-permute-done.62 = f32[512,64]{0,1:T(8,128)S(1)} collective-permute-done((f32[512,64]{0,1:T(8,128)S(1)}, f32[512,64]{0,1:T(8,128)S(1)}, u32[]{:S(2)}, u32[]{:S(2)}) %collective-permute-start.62) | collective-permute-done | bytes 131104 | tf_op jit(solution)/shard_map/ppermute | solution.py:25
  494.4 7.2 %collective-permute-start.63 = (f32[256,32]{0,1:T(8,128)S(1)}, f32[256,32]{0,1:T(8,128)S(1)}, u32[]{:S(2)}, u32[]{:S(2)}) collective-permute-start(f32[256,32]{0,1:T(8,128)S(1)} %convolution_add_fusion.1), channel_id=1, source_target_pairs={{0,1},{1,0},{2,3},{3,2},{4,5},{5,4},{6,7},{7,6},{8,9},{9,8},{10,11... | collective-permute-start | bytes 98312 | tf_op jit(solution)/shard_map/ppermute | solution.py:25
  501.7 5.1 collective-permute-start.72
  506.9 3.1 collective-permute-start.64
  511.5 4.6 collective-permute-start.65
  517.7 4.3 collective-permute-start.66
  523.6 5.2 collective-permute-start.67
  550.2 3.3 collective-permute-done.70
  553.4 7.2 %collective-permute-start.71 = (f32[2]{0:T(128)S(1)}, f32[2]{0:T(128)S(1)}, u32[]{:S(2)}, u32[]{:S(2)}) collective-permute-start(f32[2]{0:T(128)S(1)} %add.456), channel_id=1, source_target_pairs={{0,32},{8,40},{16,48},{24,56},{32,0},{40,8},{48,16},{56,24},{1,33}... | collective-permute-start | bytes 32 | tf_op jit(solution)/shard_map/ppermute | solution.py:25
  564.4 10.9 %collective-permute-start.76 = (f32[2]{0:T(128)S(1)}, f32[2]{0:T(128)S(1)}, u32[]{:S(2)}, u32[]{:S(2)}) collective-permute-start(f32[2]{0:T(128)S(1)} %pad_maximum_fusion.12), channel_id=1, source_target_pairs={{0,1},{1,0},{2,3},{3,2},{4,5},{5,4},{6,7},{7,6},{8,9},{9,8},{10,11... | collective-permute-start | bytes 32 | tf_op jit(solution)/shard_map/ppermute | solution.py:25
  577.4 3.1 collective-permute-start.77
  582.9 4.6 collective-permute-start.78
  588.7 4.3 collective-permute-start.79
  593.9 5.2 collective-permute-start.80
  (271 shorter events, 203.6 us)
Async XLA Ops:
  9.1 70.0 %all-to-all-start = ((f32[4,1,65536]{2,1,0:T(1,128)}), f32[4,1,65536]{2,1,0:T(1,128)S(1)}, u32[]{:S(2)}, u32[]{:S(2)}) async-start(f32[4,1,65536]{2,1,0:T(1,128)} %reshape.50), calls=%async_computation | async-start | bytes 2097152 | tf_op jit(solution)/shard_map/all_to_all | solution.py:35
  87.6 20.1 %collective-permute-start.5 = (f32[512,64]{0,1:T(8,128)S(1)}, f32[512,64]{0,1:T(8,128)S(1)}, u32[]{:S(2)}, u32[]{:S(2)}) collective-permute-start(f32[512,64]{0,1:T(8,128)S(1)} %pad_maximum_fusion.1), channel_id=1, source_target_pairs={{0,64},{64,0},{1,65},{65,1},{2,66},{66,2},{3,67},{67,3},{4,68},{68... | collective-permute-start | bytes 393224 | tf_op jit(solution)/shard_map/ppermute | solution.py:25
  94.9 14.7 %collective-permute-start = (f32[256,32]{0,1:T(8,128)S(1)}, f32[256,32]{0,1:T(8,128)S(1)}, u32[]{:S(2)}, u32[]{:S(2)}) collective-permute-start(f32[256,32]{0,1:T(8,128)S(1)} %convolution_add_fusion), channel_id=1, source_target_pairs={{0,1},{1,0},{2,3},{3,2},{4,5},{5,4},{6,7},{7,6},{8,9},{9,8},{10,11... | collective-permute-start | bytes 98312 | tf_op jit(solution)/shard_map/ppermute | solution.py:25
  107.7 22.8 %collective-permute-start.6 = (f32[512,64]{0,1:T(8,128)S(1)}, f32[512,64]{0,1:T(8,128)S(1)}, u32[]{:S(2)}, u32[]{:S(2)}) collective-permute-start(f32[512,64]{0,1:T(8,128)S(1)} %fusion.41), channel_id=1, source_target_pairs={{0,8},{8,0},{16,24},{24,16},{32,40},{40,32},{48,56},{56,48},{1,9},... | collective-permute-start | bytes 393224 | tf_op jit(solution)/shard_map/ppermute | solution.py:25
  114.6 6.2 %collective-permute-start.2 = (f32[256,32]{0,1:T(8,128)S(1)}, f32[256,32]{0,1:T(8,128)S(1)}, u32[]{:S(2)}, u32[]{:S(2)}) collective-permute-start(f32[256,32]{0,1:T(8,128)S(1)} %add.362), channel_id=1, source_target_pairs={{0,4},{2,6},{4,0},{6,2},{1,5},{3,7},{5,1},{7,3},{8,12},{10,14},{12... | collective-permute-start | bytes 98312 | tf_op jit(solution)/shard_map/ppermute | solution.py:25
  120.8 5.5 collective-permute-start.3
  126.3 8.7 %collective-permute-start.4 = (f32[256,32]{0,1:T(8,128)S(1)}, f32[256,32]{0,1:T(8,128)S(1)}, u32[]{:S(2)}, u32[]{:S(2)}) collective-permute-start(f32[256,32]{0,1:T(8,128)S(1)} %add.364), channel_id=1, source_target_pairs={{0,256},{128,384},{256,0},{384,128},{1,257},{129,385},{257,1},{385... | collective-permute-start | bytes 98312 | tf_op jit(solution)/shard_map/ppermute | solution.py:25
  130.5 8.3 %collective-permute-start.7 = (f32[512,64]{0,1:T(8,128)S(1)}, f32[512,64]{0,1:T(8,128)S(1)}, u32[]{:S(2)}, u32[]{:S(2)}) collective-permute-start(f32[512,64]{0,1:T(8,128)S(1)} %add.367), channel_id=1, source_target_pairs={{0,16},{8,24},{16,0},{24,8},{32,48},{40,56},{48,32},{56,40},{1,17}... | collective-permute-start | bytes 393224 | tf_op jit(solution)/shard_map/ppermute | solution.py:25
  138.8 9.6 %collective-permute-start.8 = (f32[512,64]{0,1:T(8,128)S(1)}, f32[512,64]{0,1:T(8,128)S(1)}, u32[]{:S(2)}, u32[]{:S(2)}) collective-permute-start(f32[512,64]{0,1:T(8,128)S(1)} %add.368), channel_id=1, source_target_pairs={{0,32},{8,40},{16,48},{24,56},{32,0},{40,8},{48,16},{56,24},{1,33}... | collective-permute-start | bytes 393224 | tf_op jit(solution)/shard_map/ppermute | solution.py:25
  151.8 9.8 %collective-permute-start.9 = (f32[256,32]{0,1:T(8,128)S(1)}, f32[256,32]{0,1:T(8,128)S(1)}, u32[]{:S(2)}, u32[]{:S(2)}) collective-permute-start(f32[256,32]{0,1:T(8,128)S(1)} %convolution_add_fusion.5), channel_id=1, source_target_pairs={{0,1},{1,0},{2,3},{3,2},{4,5},{5,4},{6,7},{7,6},{8,9},{9,8},{10,11... | collective-permute-start | bytes 98312 | tf_op jit(solution)/shard_map/ppermute | solution.py:25
  158.6 25.8 %collective-permute-start.18 = (f32[512,64]{0,1:T(8,128)S(1)}, f32[512,64]{0,1:T(8,128)S(1)}, u32[]{:S(2)}, u32[]{:S(2)}) collective-permute-start(f32[512,64]{0,1:T(8,128)S(1)} %pad_maximum_fusion.2), channel_id=1, source_target_pairs={{0,64},{64,0},{1,65},{65,1},{2,66},{66,2},{3,67},{67,3},{4,68},{68... | collective-permute-start | bytes 393224 | tf_op jit(solution)/shard_map/ppermute | solution.py:25
  166.3 6.2 %collective-permute-start.11 = (f32[256,32]{0,1:T(8,128)S(1)}, f32[256,32]{0,1:T(8,128)S(1)}, u32[]{:S(2)}, u32[]{:S(2)}) collective-permute-start(f32[256,32]{0,1:T(8,128)S(1)} %add.373), channel_id=1, source_target_pairs={{0,4},{2,6},{4,0},{6,2},{1,5},{3,7},{5,1},{7,3},{8,12},{10,14},{12... | collective-permute-start | bytes 98312 | tf_op jit(solution)/shard_map/ppermute | solution.py:25
  172.5 5.5 collective-permute-start.12
  178.0 10.1 %collective-permute-start.13 = (f32[256,32]{0,1:T(8,128)S(1)}, f32[256,32]{0,1:T(8,128)S(1)}, u32[]{:S(2)}, u32[]{:S(2)}) collective-permute-start(f32[256,32]{0,1:T(8,128)S(1)} %add.375), channel_id=1, source_target_pairs={{0,256},{128,384},{256,0},{384,128},{1,257},{129,385},{257,1},{385... | collective-permute-start | bytes 98312 | tf_op jit(solution)/shard_map/ppermute | solution.py:25
  184.5 7.8 %collective-permute-start.19 = (f32[512,64]{0,1:T(8,128)S(1)}, f32[512,64]{0,1:T(8,128)S(1)}, u32[]{:S(2)}, u32[]{:S(2)}) collective-permute-start(f32[512,64]{0,1:T(8,128)S(1)} %fusion.40), channel_id=1, source_target_pairs={{0,8},{8,0},{16,24},{24,16},{32,40},{40,32},{48,56},{56,48},{1,9},... | collective-permute-start | bytes 393224 | tf_op jit(solution)/shard_map/ppermute | solution.py:25
  192.3 8.0 %collective-permute-start.20 = (f32[512,64]{0,1:T(8,128)S(1)}, f32[512,64]{0,1:T(8,128)S(1)}, u32[]{:S(2)}, u32[]{:S(2)}) collective-permute-start(f32[512,64]{0,1:T(8,128)S(1)} %add.383), channel_id=1, source_target_pairs={{0,16},{8,24},{16,0},{24,8},{32,48},{40,56},{48,32},{56,40},{1,17}... | collective-permute-start | bytes 393224 | tf_op jit(solution)/shard_map/ppermute | solution.py:25
  196.1 7.3 %collective-permute-start.15 = (f32[2]{0:T(128)S(1)}, f32[2]{0:T(128)S(1)}, u32[]{:S(2)}, u32[]{:S(2)}) collective-permute-start(f32[2]{0:T(128)S(1)} %fusion.127), channel_id=1, source_target_pairs={{0,8},{8,0},{16,24},{24,16},{32,40},{40,32},{48,56},{56,48},{1,9},... | collective-permute-start | bytes 32 | tf_op jit(solution)/shard_map/ppermute | solution.py:25
  200.3 18.4 %collective-permute-start.21 = (f32[512,64]{0,1:T(8,128)S(1)}, f32[512,64]{0,1:T(8,128)S(1)}, u32[]{:S(2)}, u32[]{:S(2)}) collective-permute-start(f32[512,64]{0,1:T(8,128)S(1)} %add.384), channel_id=1, source_target_pairs={{0,32},{8,40},{16,48},{24,56},{32,0},{40,8},{48,16},{56,24},{1,33}... | collective-permute-start | bytes 393224 | tf_op jit(solution)/shard_map/ppermute | solution.py:25
  210.0 8.2 %collective-permute-start.17 = (f32[2]{0:T(128)S(1)}, f32[2]{0:T(128)S(1)}, u32[]{:S(2)}, u32[]{:S(2)}) collective-permute-start(f32[2]{0:T(128)S(1)} %add.380), channel_id=1, source_target_pairs={{0,32},{8,40},{16,48},{24,56},{32,0},{40,8},{48,16},{56,24},{1,33}... | collective-permute-start | bytes 32 | tf_op jit(solution)/shard_map/ppermute | solution.py:25
  220.6 11.0 %collective-permute-start.22 = (f32[2]{0:T(128)S(1)}, f32[2]{0:T(128)S(1)}, u32[]{:S(2)}, u32[]{:S(2)}) collective-permute-start(f32[2]{0:T(128)S(1)} %pad_maximum_fusion.8), channel_id=1, source_target_pairs={{0,1},{1,0},{2,3},{3,2},{4,5},{5,4},{6,7},{7,6},{8,9},{9,8},{10,11... | collective-permute-start | bytes 32 | tf_op jit(solution)/shard_map/ppermute | solution.py:25
  238.5 5.8 collective-permute-start.24
  249.4 8.2 %collective-permute-start.26 = (f32[2]{0:T(128)S(1)}, f32[2]{0:T(128)S(1)}, u32[]{:S(2)}, u32[]{:S(2)}) collective-permute-start(f32[2]{0:T(128)S(1)} %add.391), channel_id=1, source_target_pairs={{0,256},{128,384},{256,0},{384,128},{1,257},{129,385},{257,1},{385... | collective-permute-start | bytes 32 | tf_op jit(solution)/shard_map/ppermute | solution.py:25
  263.1 10.2 %collective-permute-start.32 = (f32[512,64]{0,1:T(8,128)S(1)}, f32[512,64]{0,1:T(8,128)S(1)}, u32[]{:S(2)}, u32[]{:S(2)}) collective-permute-start(f32[512,64]{0,1:T(8,128)S(1)} %pad_maximum_fusion.3), channel_id=1, source_target_pairs={{0,64},{64,0},{1,65},{65,1},{2,66},{66,2},{3,67},{67,3},{4,68},{68... | collective-permute-start | bytes 393224 | tf_op jit(solution)/shard_map/ppermute | solution.py:25
  266.2 9.9 %collective-permute-start.27 = (f32[256,32]{0,1:T(8,128)S(1)}, f32[256,32]{0,1:T(8,128)S(1)}, u32[]{:S(2)}, u32[]{:S(2)}) collective-permute-start(f32[256,32]{0,1:T(8,128)S(1)} %convolution_add_fusion.4), channel_id=1, source_target_pairs={{0,1},{1,0},{2,3},{3,2},{4,5},{5,4},{6,7},{7,6},{8,9},{9,8},{10,11... | collective-permute-start | bytes 98312 | tf_op jit(solution)/shard_map/ppermute | solution.py:25
  273.3 24.9 %collective-permute-start.33 = (f32[512,64]{0,1:T(8,128)S(1)}, f32[512,64]{0,1:T(8,128)S(1)}, u32[]{:S(2)}, u32[]{:S(2)}) collective-permute-start(f32[512,64]{0,1:T(8,128)S(1)} %fusion.39), channel_id=1, source_target_pairs={{0,8},{8,0},{16,24},{24,16},{32,40},{40,32},{48,56},{56,48},{1,9},... | collective-permute-start | bytes 393224 | tf_op jit(solution)/shard_map/ppermute | solution.py:25
  281.1 6.2 %collective-permute-start.29 = (f32[256,32]{0,1:T(8,128)S(1)}, f32[256,32]{0,1:T(8,128)S(1)}, u32[]{:S(2)}, u32[]{:S(2)}) collective-permute-start(f32[256,32]{0,1:T(8,128)S(1)} %add.400), channel_id=1, source_target_pairs={{0,4},{2,6},{4,0},{6,2},{1,5},{3,7},{5,1},{7,3},{8,12},{10,14},{12... | collective-permute-start | bytes 98312 | tf_op jit(solution)/shard_map/ppermute | solution.py:25
  287.2 5.7 collective-permute-start.30
  293.0 8.6 %collective-permute-start.31 = (f32[256,32]{0,1:T(8,128)S(1)}, f32[256,32]{0,1:T(8,128)S(1)}, u32[]{:S(2)}, u32[]{:S(2)}) collective-permute-start(f32[256,32]{0,1:T(8,128)S(1)} %add.402), channel_id=1, source_target_pairs={{0,256},{128,384},{256,0},{384,128},{1,257},{129,385},{257,1},{385... | collective-permute-start | bytes 98312 | tf_op jit(solution)/shard_map/ppermute | solution.py:25
  298.3 8.1 %collective-permute-start.34 = (f32[512,64]{0,1:T(8,128)S(1)}, f32[512,64]{0,1:T(8,128)S(1)}, u32[]{:S(2)}, u32[]{:S(2)}) collective-permute-start(f32[512,64]{0,1:T(8,128)S(1)} %add.405), channel_id=1, source_target_pairs={{0,16},{8,24},{16,0},{24,8},{32,48},{40,56},{48,32},{56,40},{1,17}... | collective-permute-start | bytes 393224 | tf_op jit(solution)/shard_map/ppermute | solution.py:25
  306.4 9.6 %collective-permute-start.35 = (f32[512,64]{0,1:T(8,128)S(1)}, f32[512,64]{0,1:T(8,128)S(1)}, u32[]{:S(2)}, u32[]{:S(2)}) collective-permute-start(f32[512,64]{0,1:T(8,128)S(1)} %add.406), channel_id=1, source_target_pairs={{0,32},{8,40},{16,48},{24,56},{32,0},{40,8},{48,16},{56,24},{1,33}... | collective-permute-start | bytes 393224 | tf_op jit(solution)/shard_map/ppermute | solution.py:25
  319.4 13.8 %collective-permute-start.36 = (f32[256,32]{0,1:T(8,128)S(1)}, f32[256,32]{0,1:T(8,128)S(1)}, u32[]{:S(2)}, u32[]{:S(2)}) collective-permute-start(f32[256,32]{0,1:T(8,128)S(1)} %convolution_add_fusion.3), channel_id=1, source_target_pairs={{0,1},{1,0},{2,3},{3,2},{4,5},{5,4},{6,7},{7,6},{8,9},{9,8},{10,11... | collective-permute-start | bytes 98312 | tf_op jit(solution)/shard_map/ppermute | solution.py:25
  328.2 25.9 %collective-permute-start.45 = (f32[512,64]{0,1:T(8,128)S(1)}, f32[512,64]{0,1:T(8,128)S(1)}, u32[]{:S(2)}, u32[]{:S(2)}) collective-permute-start(f32[512,64]{0,1:T(8,128)S(1)} %pad_maximum_fusion.4), channel_id=1, source_target_pairs={{0,64},{64,0},{1,65},{65,1},{2,66},{66,2},{3,67},{67,3},{4,68},{68... | collective-permute-start | bytes 393224 | tf_op jit(solution)/shard_map/ppermute | solution.py:25
  337.9 6.2 %collective-permute-start.38 = (f32[256,32]{0,1:T(8,128)S(1)}, f32[256,32]{0,1:T(8,128)S(1)}, u32[]{:S(2)}, u32[]{:S(2)}) collective-permute-start(f32[256,32]{0,1:T(8,128)S(1)} %add.411), channel_id=1, source_target_pairs={{0,4},{2,6},{4,0},{6,2},{1,5},{3,7},{5,1},{7,3},{8,12},{10,14},{12... | collective-permute-start | bytes 98312 | tf_op jit(solution)/shard_map/ppermute | solution.py:25
  344.0 6.1 %collective-permute-start.39 = (f32[256,32]{0,1:T(8,128)S(1)}, f32[256,32]{0,1:T(8,128)S(1)}, u32[]{:S(2)}, u32[]{:S(2)}) collective-permute-start(f32[256,32]{0,1:T(8,128)S(1)} %add.412), channel_id=1, source_target_pairs={{0,128},{128,0},{256,384},{384,256},{1,129},{129,1},{257,385},{385... | collective-permute-start | bytes 98312 | tf_op jit(solution)/shard_map/ppermute | solution.py:25
  350.1 8.7 %collective-permute-start.40 = (f32[256,32]{0,1:T(8,128)S(1)}, f32[256,32]{0,1:T(8,128)S(1)}, u32[]{:S(2)}, u32[]{:S(2)}) collective-permute-start(f32[256,32]{0,1:T(8,128)S(1)} %add.413), channel_id=1, source_target_pairs={{0,256},{128,384},{256,0},{384,128},{1,257},{129,385},{257,1},{385... | collective-permute-start | bytes 98312 | tf_op jit(solution)/shard_map/ppermute | solution.py:25
  354.1 9.3 %collective-permute-start.46 = (f32[512,64]{0,1:T(8,128)S(1)}, f32[512,64]{0,1:T(8,128)S(1)}, u32[]{:S(2)}, u32[]{:S(2)}) collective-permute-start(f32[512,64]{0,1:T(8,128)S(1)} %fusion.38), channel_id=1, source_target_pairs={{0,8},{8,0},{16,24},{24,16},{32,40},{40,32},{48,56},{56,48},{1,9},... | collective-permute-start | bytes 393224 | tf_op jit(solution)/shard_map/ppermute | solution.py:25
  363.4 6.8 %collective-permute-start.47 = (f32[512,64]{0,1:T(8,128)S(1)}, f32[512,64]{0,1:T(8,128)S(1)}, u32[]{:S(2)}, u32[]{:S(2)}) collective-permute-start(f32[512,64]{0,1:T(8,128)S(1)} %add.421), channel_id=1, source_target_pairs={{0,16},{8,24},{16,0},{24,8},{32,48},{40,56},{48,32},{56,40},{1,17}... | collective-permute-start | bytes 393224 | tf_op jit(solution)/shard_map/ppermute | solution.py:25
  367.1 10.7 %collective-permute-start.42 = (f32[2]{0:T(128)S(1)}, f32[2]{0:T(128)S(1)}, u32[]{:S(2)}, u32[]{:S(2)}) collective-permute-start(f32[2]{0:T(128)S(1)} %fusion.125), channel_id=1, source_target_pairs={{0,8},{8,0},{16,24},{24,16},{32,40},{40,32},{48,56},{56,48},{1,9},... | collective-permute-start | bytes 32 | tf_op jit(solution)/shard_map/ppermute | solution.py:25
  370.3 23.2 %collective-permute-start.48 = (f32[512,64]{0,1:T(8,128)S(1)}, f32[512,64]{0,1:T(8,128)S(1)}, u32[]{:S(2)}, u32[]{:S(2)}) collective-permute-start(f32[512,64]{0,1:T(8,128)S(1)} %add.422), channel_id=1, source_target_pairs={{0,32},{8,40},{16,48},{24,56},{32,0},{40,8},{48,16},{56,24},{1,33}... | collective-permute-start | bytes 393224 | tf_op jit(solution)/shard_map/ppermute | solution.py:25
  384.7 8.2 %collective-permute-start.44 = (f32[2]{0:T(128)S(1)}, f32[2]{0:T(128)S(1)}, u32[]{:S(2)}, u32[]{:S(2)}) collective-permute-start(f32[2]{0:T(128)S(1)} %add.418), channel_id=1, source_target_pairs={{0,32},{8,40},{16,48},{24,56},{32,0},{40,8},{48,16},{56,24},{1,33}... | collective-permute-start | bytes 32 | tf_op jit(solution)/shard_map/ppermute | solution.py:25
  395.4 10.3 %collective-permute-start.49 = (f32[2]{0:T(128)S(1)}, f32[2]{0:T(128)S(1)}, u32[]{:S(2)}, u32[]{:S(2)}) collective-permute-start(f32[2]{0:T(128)S(1)} %pad_maximum_fusion.10), channel_id=1, source_target_pairs={{0,1},{1,0},{2,3},{3,2},{4,5},{5,4},{6,7},{7,6},{8,9},{9,8},{10,11... | collective-permute-start | bytes 32 | tf_op jit(solution)/shard_map/ppermute | solution.py:25
  412.5 5.8 collective-permute-start.51
  423.7 8.2 %collective-permute-start.53 = (f32[2]{0:T(128)S(1)}, f32[2]{0:T(128)S(1)}, u32[]{:S(2)}, u32[]{:S(2)}) collective-permute-start(f32[2]{0:T(128)S(1)} %add.429), channel_id=1, source_target_pairs={{0,256},{128,384},{256,0},{384,128},{1,257},{129,385},{257,1},{385... | collective-permute-start | bytes 32 | tf_op jit(solution)/shard_map/ppermute | solution.py:25
  437.3 12.6 %collective-permute-start.59 = (f32[512,64]{0,1:T(8,128)S(1)}, f32[512,64]{0,1:T(8,128)S(1)}, u32[]{:S(2)}, u32[]{:S(2)}) collective-permute-start(f32[512,64]{0,1:T(8,128)S(1)} %pad_maximum_fusion.5), channel_id=1, source_target_pairs={{0,64},{64,0},{1,65},{65,1},{2,66},{66,2},{3,67},{67,3},{4,68},{68... | collective-permute-start | bytes 393224 | tf_op jit(solution)/shard_map/ppermute | solution.py:25
  443.1 8.8 %collective-permute-start.54 = (f32[256,32]{0,1:T(8,128)S(1)}, f32[256,32]{0,1:T(8,128)S(1)}, u32[]{:S(2)}, u32[]{:S(2)}) collective-permute-start(f32[256,32]{0,1:T(8,128)S(1)} %convolution_add_fusion.2), channel_id=1, source_target_pairs={{0,1},{1,0},{2,3},{3,2},{4,5},{5,4},{6,7},{7,6},{8,9},{9,8},{10,11... | collective-permute-start | bytes 98312 | tf_op jit(solution)/shard_map/ppermute | solution.py:25
  449.9 23.4 %collective-permute-start.60 = (f32[512,64]{0,1:T(8,128)S(1)}, f32[512,64]{0,1:T(8,128)S(1)}, u32[]{:S(2)}, u32[]{:S(2)}) collective-permute-start(f32[512,64]{0,1:T(8,128)S(1)} %fusion.37), channel_id=1, source_target_pairs={{0,8},{8,0},{16,24},{24,16},{32,40},{40,32},{48,56},{56,48},{1,9},... | collective-permute-start | bytes 393224 | tf_op jit(solution)/shard_map/ppermute | solution.py:25
  456.9 6.2 %collective-permute-start.56 = (f32[256,32]{0,1:T(8,128)S(1)}, f32[256,32]{0,1:T(8,128)S(1)}, u32[]{:S(2)}, u32[]{:S(2)}) collective-permute-start(f32[256,32]{0,1:T(8,128)S(1)} %add.438), channel_id=1, source_target_pairs={{0,4},{2,6},{4,0},{6,2},{1,5},{3,7},{5,1},{7,3},{8,12},{10,14},{12... | collective-permute-start | bytes 98312 | tf_op jit(solution)/shard_map/ppermute | solution.py:25
  463.0 5.8 collective-permute-start.57
  468.8 8.6 %collective-permute-start.58 = (f32[256,32]{0,1:T(8,128)S(1)}, f32[256,32]{0,1:T(8,128)S(1)}, u32[]{:S(2)}, u32[]{:S(2)}) collective-permute-start(f32[256,32]{0,1:T(8,128)S(1)} %add.440), channel_id=1, source_target_pairs={{0,256},{128,384},{256,0},{384,128},{1,257},{129,385},{257,1},{385... | collective-permute-start | bytes 98312 | tf_op jit(solution)/shard_map/ppermute | solution.py:25
  473.4 8.0 %collective-permute-start.61 = (f32[512,64]{0,1:T(8,128)S(1)}, f32[512,64]{0,1:T(8,128)S(1)}, u32[]{:S(2)}, u32[]{:S(2)}) collective-permute-start(f32[512,64]{0,1:T(8,128)S(1)} %add.443), channel_id=1, source_target_pairs={{0,16},{8,24},{16,0},{24,8},{32,48},{40,56},{48,32},{56,40},{1,17}... | collective-permute-start | bytes 393224 | tf_op jit(solution)/shard_map/ppermute | solution.py:25
  481.4 9.6 %collective-permute-start.62 = (f32[512,64]{0,1:T(8,128)S(1)}, f32[512,64]{0,1:T(8,128)S(1)}, u32[]{:S(2)}, u32[]{:S(2)}) collective-permute-start(f32[512,64]{0,1:T(8,128)S(1)} %add.444), channel_id=1, source_target_pairs={{0,32},{8,40},{16,48},{24,56},{32,0},{40,8},{48,16},{56,24},{1,33}... | collective-permute-start | bytes 393224 | tf_op jit(solution)/shard_map/ppermute | solution.py:25
  494.4 12.4 %collective-permute-start.63 = (f32[256,32]{0,1:T(8,128)S(1)}, f32[256,32]{0,1:T(8,128)S(1)}, u32[]{:S(2)}, u32[]{:S(2)}) collective-permute-start(f32[256,32]{0,1:T(8,128)S(1)} %convolution_add_fusion.1), channel_id=1, source_target_pairs={{0,1},{1,0},{2,3},{3,2},{4,5},{5,4},{6,7},{7,6},{8,9},{9,8},{10,11... | collective-permute-start | bytes 98312 | tf_op jit(solution)/shard_map/ppermute | solution.py:25
  501.7 27.1 %collective-permute-start.72 = (f32[512,64]{0,1:T(8,128)S(1)}, f32[512,64]{0,1:T(8,128)S(1)}, u32[]{:S(2)}, u32[]{:S(2)}) collective-permute-start(f32[512,64]{0,1:T(8,128)S(1)} %pad_maximum_fusion.6), channel_id=1, source_target_pairs={{0,64},{64,0},{1,65},{65,1},{2,66},{66,2},{3,67},{67,3},{4,68},{68... | collective-permute-start | bytes 393224 | tf_op jit(solution)/shard_map/ppermute | solution.py:25
  511.5 6.2 %collective-permute-start.65 = (f32[256,32]{0,1:T(8,128)S(1)}, f32[256,32]{0,1:T(8,128)S(1)}, u32[]{:S(2)}, u32[]{:S(2)}) collective-permute-start(f32[256,32]{0,1:T(8,128)S(1)} %add.449), channel_id=1, source_target_pairs={{0,4},{2,6},{4,0},{6,2},{1,5},{3,7},{5,1},{7,3},{8,12},{10,14},{12... | collective-permute-start | bytes 98312 | tf_op jit(solution)/shard_map/ppermute | solution.py:25
  517.7 5.9 collective-permute-start.66
  523.6 8.7 %collective-permute-start.67 = (f32[256,32]{0,1:T(8,128)S(1)}, f32[256,32]{0,1:T(8,128)S(1)}, u32[]{:S(2)}, u32[]{:S(2)}) collective-permute-start(f32[256,32]{0,1:T(8,128)S(1)} %add.451), channel_id=1, source_target_pairs={{0,256},{128,384},{256,0},{384,128},{1,257},{129,385},{257,1},{385... | collective-permute-start | bytes 98312 | tf_op jit(solution)/shard_map/ppermute | solution.py:25
  528.9 8.0 %collective-permute-start.73 = (f32[512,64]{0,1:T(8,128)S(1)}, f32[512,64]{0,1:T(8,128)S(1)}, u32[]{:S(2)}, u32[]{:S(2)}) collective-permute-start(f32[512,64]{0,1:T(8,128)S(1)} %fusion.36), channel_id=1, source_target_pairs={{0,8},{8,0},{16,24},{24,16},{32,40},{40,32},{48,56},{56,48},{1,9},... | collective-permute-start | bytes 393224 | tf_op jit(solution)/shard_map/ppermute | solution.py:25
  536.9 7.9 %collective-permute-start.74 = (f32[512,64]{0,1:T(8,128)S(1)}, f32[512,64]{0,1:T(8,128)S(1)}, u32[]{:S(2)}, u32[]{:S(2)}) collective-permute-start(f32[512,64]{0,1:T(8,128)S(1)} %add.459), channel_id=1, source_target_pairs={{0,16},{8,24},{16,0},{24,8},{32,48},{40,56},{48,32},{56,40},{1,17}... | collective-permute-start | bytes 393224 | tf_op jit(solution)/shard_map/ppermute | solution.py:25
  541.1 5.6 collective-permute-start.69
  544.9 17.6 %collective-permute-start.75 = (f32[512,64]{0,1:T(8,128)S(1)}, f32[512,64]{0,1:T(8,128)S(1)}, u32[]{:S(2)}, u32[]{:S(2)}) collective-permute-start(f32[512,64]{0,1:T(8,128)S(1)} %add.460), channel_id=1, source_target_pairs={{0,32},{8,40},{16,48},{24,56},{32,0},{40,8},{48,16},{56,24},{1,33}... | collective-permute-start | bytes 393224 | tf_op jit(solution)/shard_map/ppermute | solution.py:25
  553.4 8.5 %collective-permute-start.71 = (f32[2]{0:T(128)S(1)}, f32[2]{0:T(128)S(1)}, u32[]{:S(2)}, u32[]{:S(2)}) collective-permute-start(f32[2]{0:T(128)S(1)} %add.456), channel_id=1, source_target_pairs={{0,32},{8,40},{16,48},{24,56},{32,0},{40,8},{48,16},{56,24},{1,33}... | collective-permute-start | bytes 32 | tf_op jit(solution)/shard_map/ppermute | solution.py:25
  564.4 11.7 %collective-permute-start.76 = (f32[2]{0:T(128)S(1)}, f32[2]{0:T(128)S(1)}, u32[]{:S(2)}, u32[]{:S(2)}) collective-permute-start(f32[2]{0:T(128)S(1)} %pad_maximum_fusion.12), channel_id=1, source_target_pairs={{0,1},{1,0},{2,3},{3,2},{4,5},{5,4},{6,7},{7,6},{8,9},{9,8},{10,11... | collective-permute-start | bytes 32 | tf_op jit(solution)/shard_map/ppermute | solution.py:25
  582.9 5.8 collective-permute-start.78
  593.9 8.2 %collective-permute-start.80 = (f32[2]{0:T(128)S(1)}, f32[2]{0:T(128)S(1)}, u32[]{:S(2)}, u32[]{:S(2)}) collective-permute-start(f32[2]{0:T(128)S(1)} %add.467), channel_id=1, source_target_pairs={{0,256},{128,384},{256,0},{384,128},{1,257},{129,385},{257,1},{385... | collective-permute-start | bytes 32 | tf_op jit(solution)/shard_map/ppermute | solution.py:25
  (20 other events, 140.6 us)

commit v2 on v1

--- a/solution.py
+++ b/solution.py
@@ -27,6 +27,20 @@
     return value
 
 
+def doubling_gather(value, axes):
+    for name in reversed(axes):
+        size = lax.axis_size(name)
+        me = lax.axis_index(name)
+        step = 1
+        while step < size:
+            pairs = [(j, j ^ step) for j in range(size)]
+            other = lax.ppermute(value, name, pairs)
+            upper = (me // step) % 2 == 1
+            value = jnp.where(upper, jnp.concatenate([other, value]), jnp.concatenate([value, other]))
+            step *= 2
+    return value
+
+
 def per_device(genotypes, observed, ancestry, freqs):
     quarter = lax.axis_size("yh")
     geno = genotypes.astype(jnp.float32)
@@ -37,8 +51,8 @@
     own_rows = ancestry.shape[0]
     own_snps = freqs.shape[0]
     q_own = ancestry / jnp.sum(ancestry, axis=1, keepdims=True)
-    q_zero = lax.all_gather(q_own, "yh", axis=0, tiled=True)
-    f_zero = lax.all_gather(freqs, ROW_GROUP, axis=0, tiled=True)
+    q_zero = doubling_gather(q_own, ("yh",))
+    f_zero = doubling_gather(freqs, ROW_GROUP)
 
     def em_map(q_rows, f_state):
         prob = jnp.dot(q_rows, f_state.T, precision=high, preferred_element_type=jnp.float32)

time: 614 us -> 586 us (0.954)
  blocking collectives: 62 us -> 0 us
  starting transfers between devices: 356 us -> 386 us
    all_gather x2 -> x0, blocking collectives: 62 us -> none  [the longest x1 32 us: per_device(): q_zero = lax.all_gather(q_own, 'yh', axis=0, tiled=True)]
    ppermute x0 -> x6, starting transfers between devices: none -> 29 us  [doubling_gather(): other = lax.ppermute(value, name, pairs)]
  transfers between devices with their start and end apart: 82 -> 88, of which waited for: 55 -> 51; matrix products, arithmetic and copies ran while one was open for 4% -> 5% of each run, Pallas kernels for 0% -> 0%
where the time goes in v2:
time: 586 us; the launch traced here: 578 us
  starting transfers between devices  386 us (66%)
  waiting for transfers between devices  112 us (19%)
  other arithmetic  40.3 us (7%)
  matrix products  16.2 us (3%)
  local copies, waits for them, and re-layouts  13.4 us (2%)
  between operations  10.3 us (2%)
    ppermute x81, starting transfers between devices, doubling_sum(): value = value + lax.ppermute(value, name, pairs)  349 us
    ppermute x81, waiting for transfers between devices, doubling_sum(): value = value + lax.ppermute(value, name, pairs)  108 us
    ppermute x6, starting transfers between devices, doubling_gather(): other = lax.ppermute(value, name, pairs)  29 us
    add x75, other arithmetic, doubling_sum(): value = value + lax.ppermute(value, name, pairs)  16.9 us
  transfers between devices with their start and end apart: 88, of which 51 were waited for; matrix products, arithmetic and copies ran while one was open for 5% of the time, Pallas kernels for 0%

profile of v2, /device:TPU:1, one launch (start us, length us, event | category | flops | bytes accessed | tf_op | source)
XLA Modules:
  0.0 577.6 jit_solution(4226420219177968923)
XLA Ops:
  9.1 7.6 %all-to-all-start = ((f32[4,1,65536]{2,1,0:T(1,128)}), f32[4,1,65536]{2,1,0:T(1,128)S(1)}, u32[]{:S(2)}, u32[]{:S(2)}) async-start(f32[4,1,65536]{2,1,0:T(1,128)} %reshape.48), calls=%async_computation | async-start | bytes 2097152 | tf_op jit(solution)/shard_map/all_to_all | solution.py:49
  16.8 4.0 collective-permute-start.2
  22.0 5.8 %collective-permute-start.3 = (f32[64,32]{0,1:T(8,128)S(1)}, f32[64,32]{0,1:T(8,128)S(1)}, u32[]{:S(2)}, u32[]{:S(2)}) collective-permute-start(f32[64,32]{0,1:T(8,128)S(1)} %maximum_select_fusion.4), channel_id=1, source_target_pairs={{0,16},{8,24},{16,0},{24,8},{32,48},{40,56},{48,32},{56,40},{1,17}... | collective-permute-start | bytes 24584 | tf_op jit(solution)/shard_map/ppermute | solution.py:37
  27.8 4.6 collective-permute-start
  32.6 8.2 %collective-permute-start.4 = (f32[128,32]{0,1:T(8,128)S(1)}, f32[128,32]{0,1:T(8,128)S(1)}, u32[]{:S(2)}, u32[]{:S(2)}) collective-permute-start(f32[128,32]{0,1:T(8,128)S(1)} %maximum_select_fusion.5), channel_id=1, source_target_pairs={{0,32},{8,40},{16,48},{24,56},{32,0},{40,8},{48,16},{56,24},{1,33}... | collective-permute-start | bytes 49160 | tf_op jit(solution)/shard_map/ppermute | solution.py:37
  43.6 4.5 collective-permute-start.1
  50.6 3.7 reduce
  58.6 3.4 collective-permute-start.11
  63.1 4.0 collective-permute-start.6
  67.2 4.0 collective-permute-start.12
  71.2 3.1 collective-permute-start.7
  75.9 4.6 collective-permute-start.8
  87.8 3.8 collective-permute-start.10
  91.6 5.8 %collective-permute-start.13 = (f32[512,64]{0,1:T(8,128)S(1)}, f32[512,64]{0,1:T(8,128)S(1)}, u32[]{:S(2)}, u32[]{:S(2)}) collective-permute-start(f32[512,64]{0,1:T(8,128)S(1)} %add.398), channel_id=1, source_target_pairs={{0,16},{8,24},{16,0},{24,8},{32,48},{40,56},{48,32},{56,40},{1,17}... | collective-permute-start | bytes 393224 | tf_op jit(solution)/shard_map/ppermute | solution.py:25
  97.4 3.7 collective-permute-done.13
  101.2 8.8 %collective-permute-start.14 = (f32[512,64]{0,1:T(8,128)S(1)}, f32[512,64]{0,1:T(8,128)S(1)}, u32[]{:S(2)}, u32[]{:S(2)}) collective-permute-start(f32[512,64]{0,1:T(8,128)S(1)} %add.399), channel_id=1, source_target_pairs={{0,32},{8,40},{16,48},{24,56},{32,0},{40,8},{48,16},{56,24},{1,33}... | collective-permute-start | bytes 393224 | tf_op jit(solution)/shard_map/ppermute | solution.py:25
  115.6 7.6 %collective-permute-start.15 = (f32[256,32]{0,1:T(8,128)S(1)}, f32[256,32]{0,1:T(8,128)S(1)}, u32[]{:S(2)}, u32[]{:S(2)}) collective-permute-start(f32[256,32]{0,1:T(8,128)S(1)} %convolution_add_fusion.4), channel_id=1, source_target_pairs={{0,1},{1,0},{2,3},{3,2},{4,5},{5,4},{6,7},{7,6},{8,9},{9,8},{10,11... | collective-permute-start | bytes 98312 | tf_op jit(solution)/shard_map/ppermute | solution.py:25
  123.2 4.8 collective-permute-start.24
  132.7 4.6 collective-permute-start.17
  140.8 4.0 collective-permute-done.18
  144.8 5.3 collective-permute-start.19
  162.4 4.4 collective-permute-start.21
  166.8 6.9 %collective-permute-start.27 = (f32[512,64]{0,1:T(8,128)S(1)}, f32[512,64]{0,1:T(8,128)S(1)}, u32[]{:S(2)}, u32[]{:S(2)}) collective-permute-start(f32[512,64]{0,1:T(8,128)S(1)} %add.415), channel_id=1, source_target_pairs={{0,32},{8,40},{16,48},{24,56},{32,0},{40,8},{48,16},{56,24},{1,33}... | collective-permute-start | bytes 393224 | tf_op jit(solution)/shard_map/ppermute | solution.py:25
  177.0 3.3 collective-permute-done.22
  182.6 5.8 %collective-permute-done.23 = f32[2]{0:T(128)S(1)} collective-permute-done((f32[2]{0:T(128)S(1)}, f32[2]{0:T(128)S(1)}, u32[]{:S(2)}, u32[]{:S(2)}) %collective-permute-start.23) | collective-permute-done | bytes 40 | tf_op jit(solution)/shard_map/ppermute | solution.py:25
  191.1 10.0 %collective-permute-start.28 = (f32[2]{0:T(128)S(1)}, f32[2]{0:T(128)S(1)}, u32[]{:S(2)}, u32[]{:S(2)}) collective-permute-start(f32[2]{0:T(128)S(1)} %pad_maximum_fusion.8), channel_id=1, source_target_pairs={{0,1},{1,0},{2,3},{3,2},{4,5},{5,4},{6,7},{7,6},{8,9},{9,8},{10,11... | collective-permute-start | bytes 32 | tf_op jit(solution)/shard_map/ppermute | solution.py:25
  208.9 4.6 collective-permute-start.30
  216.6 3.3 collective-permute-done.31
  219.9 6.6 %collective-permute-start.32 = (f32[2]{0:T(128)S(1)}, f32[2]{0:T(128)S(1)}, u32[]{:S(2)}, u32[]{:S(2)}) collective-permute-start(f32[2]{0:T(128)S(1)} %add.422), channel_id=1, source_target_pairs={{0,256},{128,384},{256,0},{384,128},{1,257},{129,385},{257,1},{385... | collective-permute-start | bytes 32 | tf_op jit(solution)/shard_map/ppermute | solution.py:25
  237.2 7.1 %collective-permute-start.33 = (f32[256,32]{0,1:T(8,128)S(1)}, f32[256,32]{0,1:T(8,128)S(1)}, u32[]{:S(2)}, u32[]{:S(2)}) collective-permute-start(f32[256,32]{0,1:T(8,128)S(1)} %convolution_add_fusion.3), channel_id=1, source_target_pairs={{0,1},{1,0},{2,3},{3,2},{4,5},{5,4},{6,7},{7,6},{8,9},{9,8},{10,11... | collective-permute-start | bytes 98312 | tf_op jit(solution)/shard_map/ppermute | solution.py:25
  252.0 4.6 collective-permute-start.35
  263.9 6.1 %collective-permute-start.37 = (f32[256,32]{0,1:T(8,128)S(1)}, f32[256,32]{0,1:T(8,128)S(1)}, u32[]{:S(2)}, u32[]{:S(2)}) collective-permute-start(f32[256,32]{0,1:T(8,128)S(1)} %add.433), channel_id=1, source_target_pairs={{0,256},{128,384},{256,0},{384,128},{1,257},{129,385},{257,1},{385... | collective-permute-start | bytes 98312 | tf_op jit(solution)/shard_map/ppermute | solution.py:25
  270.0 3.8 collective-permute-start.40
  273.8 4.2 collective-permute-done.40
  280.0 7.8 %collective-permute-done.41 = f32[512,64]{0,1:T(8,128)S(1)} collective-permute-done((f32[512,64]{0,1:T(8,128)S(1)}, f32[512,64]{0,1:T(8,128)S(1)}, u32[]{:S(2)}, u32[]{:S(2)}) %collective-permute-start.41) | collective-permute-done | bytes 131104 | tf_op jit(solution)/shard_map/ppermute | solution.py:25
  291.1 7.7 %collective-permute-start.42 = (f32[256,32]{0,1:T(8,128)S(1)}, f32[256,32]{0,1:T(8,128)S(1)}, u32[]{:S(2)}, u32[]{:S(2)}) collective-permute-start(f32[256,32]{0,1:T(8,128)S(1)} %convolution_add_fusion.2), channel_id=1, source_target_pairs={{0,1},{1,0},{2,3},{3,2},{4,5},{5,4},{6,7},{7,6},{8,9},{9,8},{10,11... | collective-permute-start | bytes 98312 | tf_op jit(solution)/shard_map/ppermute | solution.py:25
  298.8 4.4 collective-permute-start.51
  307.9 4.6 collective-permute-start.44
  314.0 4.0 collective-permute-start.45
  319.6 5.8 %collective-permute-start.46 = (f32[256,32]{0,1:T(8,128)S(1)}, f32[256,32]{0,1:T(8,128)S(1)}, u32[]{:S(2)}, u32[]{:S(2)}) collective-permute-start(f32[256,32]{0,1:T(8,128)S(1)} %add.444), channel_id=1, source_target_pairs={{0,256},{128,384},{256,0},{384,128},{1,257},{129,385},{257,1},{385... | collective-permute-start | bytes 98312 | tf_op jit(solution)/shard_map/ppermute | solution.py:25
  333.6 3.4 collective-permute-start.53
  347.0 3.1 collective-permute-done.49
  350.2 7.2 %collective-permute-start.50 = (f32[2]{0:T(128)S(1)}, f32[2]{0:T(128)S(1)}, u32[]{:S(2)}, u32[]{:S(2)}) collective-permute-start(f32[2]{0:T(128)S(1)} %add.449), channel_id=1, source_target_pairs={{0,32},{8,40},{16,48},{24,56},{32,0},{40,8},{48,16},{56,24},{1,33}... | collective-permute-start | bytes 32 | tf_op jit(solution)/shard_map/ppermute | solution.py:25
  361.3 11.3 %collective-permute-start.55 = (f32[2]{0:T(128)S(1)}, f32[2]{0:T(128)S(1)}, u32[]{:S(2)}, u32[]{:S(2)}) collective-permute-start(f32[2]{0:T(128)S(1)} %pad_maximum_fusion.10), channel_id=1, source_target_pairs={{0,1},{1,0},{2,3},{3,2},{4,5},{5,4},{6,7},{7,6},{8,9},{9,8},{10,11... | collective-permute-start | bytes 32 | tf_op jit(solution)/shard_map/ppermute | solution.py:25
  380.4 4.6 collective-permute-start.57
  386.2 3.9 collective-permute-start.58
  393.7 5.8 %collective-permute-done.59 = f32[2]{0:T(128)S(1)} collective-permute-done((f32[2]{0:T(128)S(1)}, f32[2]{0:T(128)S(1)}, u32[]{:S(2)}, u32[]{:S(2)}) %collective-permute-start.59) | collective-permute-done | bytes 40 | tf_op jit(solution)/shard_map/ppermute | solution.py:25
  408.5 7.1 %collective-permute-start.60 = (f32[256,32]{0,1:T(8,128)S(1)}, f32[256,32]{0,1:T(8,128)S(1)}, u32[]{:S(2)}, u32[]{:S(2)}) collective-permute-start(f32[256,32]{0,1:T(8,128)S(1)} %convolution_add_fusion.1), channel_id=1, source_target_pairs={{0,1},{1,0},{2,3},{3,2},{4,5},{5,4},{6,7},{7,6},{8,9},{9,8},{10,11... | collective-permute-start | bytes 98312 | tf_op jit(solution)/shard_map/ppermute | solution.py:25
  422.6 4.7 collective-permute-start.62
  428.7 3.6 collective-permute-start.63
  434.3 4.2 collective-permute-start.64
  438.5 4.2 collective-permute-start.67
  442.9 3.8 collective-permute-done.67
  446.8 7.6 %collective-permute-start.68 = (f32[512,64]{0,1:T(8,128)S(1)}, f32[512,64]{0,1:T(8,128)S(1)}, u32[]{:S(2)}, u32[]{:S(2)}) collective-permute-start(f32[512,64]{0,1:T(8,128)S(1)} %add.475), channel_id=1, source_target_pairs={{0,32},{8,40},{16,48},{24,56},{32,0},{40,8},{48,16},{56,24},{1,33}... | collective-permute-start | bytes 393224 | tf_op jit(solution)/shard_map/ppermute | solution.py:25
  460.3 7.7 %collective-permute-start.69 = (f32[256,32]{0,1:T(8,128)S(1)}, f32[256,32]{0,1:T(8,128)S(1)}, u32[]{:S(2)}, u32[]{:S(2)}) collective-permute-start(f32[256,32]{0,1:T(8,128)S(1)} %convolution_add_fusion), channel_id=1, source_target_pairs={{0,1},{1,0},{2,3},{3,2},{4,5},{5,4},{6,7},{7,6},{8,9},{9,8},{10,11... | collective-permute-start | bytes 98312 | tf_op jit(solution)/shard_map/ppermute | solution.py:25
  475.8 4.7 collective-permute-start.71
  487.5 5.9 %collective-permute-start.73 = (f32[256,32]{0,1:T(8,128)S(1)}, f32[256,32]{0,1:T(8,128)S(1)}, u32[]{:S(2)}, u32[]{:S(2)}) collective-permute-start(f32[256,32]{0,1:T(8,128)S(1)} %add.482), channel_id=1, source_target_pairs={{0,256},{128,384},{256,0},{384,128},{1,257},{129,385},{257,1},{385... | collective-permute-start | bytes 98312 | tf_op jit(solution)/shard_map/ppermute | solution.py:25
  501.9 4.1 collective-permute-start.80
  510.4 7.4 %collective-permute-start.81 = (f32[512,64]{0,1:T(8,128)S(1)}, f32[512,64]{0,1:T(8,128)S(1)}, u32[]{:S(2)}, u32[]{:S(2)}) collective-permute-start(f32[512,64]{0,1:T(8,128)S(1)} %add.491), channel_id=1, source_target_pairs={{0,32},{8,40},{16,48},{24,56},{32,0},{40,8},{48,16},{56,24},{1,33}... | collective-permute-start | bytes 393224 | tf_op jit(solution)/shard_map/ppermute | solution.py:25
  526.4 6.2 %collective-permute-done.77 = f32[2]{0:T(128)S(1)} collective-permute-done((f32[2]{0:T(128)S(1)}, f32[2]{0:T(128)S(1)}, u32[]{:S(2)}, u32[]{:S(2)}) %collective-permute-start.77) | collective-permute-done | bytes 40 | tf_op jit(solution)/shard_map/ppermute | solution.py:25
  535.2 10.3 %collective-permute-start.82 = (f32[2]{0:T(128)S(1)}, f32[2]{0:T(128)S(1)}, u32[]{:S(2)}, u32[]{:S(2)}) collective-permute-start(f32[2]{0:T(128)S(1)} %pad_maximum_fusion.12), channel_id=1, source_target_pairs={{0,1},{1,0},{2,3},{3,2},{4,5},{5,4},{6,7},{7,6},{8,9},{9,8},{10,11... | collective-permute-start | bytes 32 | tf_op jit(solution)/shard_map/ppermute | solution.py:25
  553.3 4.7 collective-permute-start.84
  559.0 3.6 collective-permute-start.85
  564.2 7.7 %collective-permute-start.86 = (f32[2]{0:T(128)S(1)}, f32[2]{0:T(128)S(1)}, u32[]{:S(2)}, u32[]{:S(2)}) collective-permute-start(f32[2]{0:T(128)S(1)} %add.498), channel_id=1, source_target_pairs={{0,256},{128,384},{256,0},{384,128},{1,257},{129,385},{257,1},{385... | collective-permute-start | bytes 32 | tf_op jit(solution)/shard_map/ppermute | solution.py:25
  (283 shorter events, 219.6 us)
Async XLA Ops:
  9.1 41.0 %all-to-all-start = ((f32[4,1,65536]{2,1,0:T(1,128)}), f32[4,1,65536]{2,1,0:T(1,128)S(1)}, u32[]{:S(2)}, u32[]{:S(2)}) async-start(f32[4,1,65536]{2,1,0:T(1,128)} %reshape.48), calls=%async_computation | async-start | bytes 2097152 | tf_op jit(solution)/shard_map/all_to_all | solution.py:49
  22.0 10.5 %collective-permute-start.3 = (f32[64,32]{0,1:T(8,128)S(1)}, f32[64,32]{0,1:T(8,128)S(1)}, u32[]{:S(2)}, u32[]{:S(2)}) collective-permute-start(f32[64,32]{0,1:T(8,128)S(1)} %maximum_select_fusion.4), channel_id=1, source_target_pairs={{0,16},{8,24},{16,0},{24,8},{32,48},{40,56},{48,32},{56,40},{1,17}... | collective-permute-start | bytes 24584 | tf_op jit(solution)/shard_map/ppermute | solution.py:37
  27.8 15.7 %collective-permute-start = (f32[64,32]{0,1:T(8,128)S(1)}, f32[64,32]{0,1:T(8,128)S(1)}, u32[]{:S(2)}, u32[]{:S(2)}) collective-permute-start(f32[64,32]{0,1:T(8,128)S(1)} %broadcast_divide_fusion.5), channel_id=1, source_target_pairs={{0,128},{128,0},{256,384},{384,256},{1,129},{129,1},{257,385},{385... | collective-permute-start | bytes 24584 | tf_op jit(solution)/shard_map/ppermute | solution.py:37
  32.6 15.5 %collective-permute-start.4 = (f32[128,32]{0,1:T(8,128)S(1)}, f32[128,32]{0,1:T(8,128)S(1)}, u32[]{:S(2)}, u32[]{:S(2)}) collective-permute-start(f32[128,32]{0,1:T(8,128)S(1)} %maximum_select_fusion.5), channel_id=1, source_target_pairs={{0,32},{8,40},{16,48},{24,56},{32,0},{40,8},{48,16},{56,24},{1,33}... | collective-permute-start | bytes 49160 | tf_op jit(solution)/shard_map/ppermute | solution.py:37
  43.6 13.4 %collective-permute-start.1 = (f32[128,32]{0,1:T(8,128)S(1)}, f32[128,32]{0,1:T(8,128)S(1)}, u32[]{:S(2)}, u32[]{:S(2)}) collective-permute-start(f32[128,32]{0,1:T(8,128)S(1)} %maximum_select_fusion.3), channel_id=1, source_target_pairs={{0,256},{128,384},{256,0},{384,128},{1,257},{129,385},{257,1},{385... | collective-permute-start | bytes 49160 | tf_op jit(solution)/shard_map/ppermute | solution.py:37
  48.2 8.8 %collective-permute-start.5 = (f32[256,32]{0,1:T(8,128)S(1)}, f32[256,32]{0,1:T(8,128)S(1)}, u32[]{:S(2)}, u32[]{:S(2)}) collective-permute-start(f32[256,32]{0,1:T(8,128)S(1)} %maximum_select_fusion.2), channel_id=1, source_target_pairs={{0,64},{64,0},{1,65},{65,1},{2,66},{66,2},{3,67},{67,3},{4,68},{68... | collective-permute-start | bytes 98312 | tf_op jit(solution)/shard_map/ppermute | solution.py:37
  58.6 8.5 %collective-permute-start.11 = (f32[512,64]{0,1:T(8,128)S(1)}, f32[512,64]{0,1:T(8,128)S(1)}, u32[]{:S(2)}, u32[]{:S(2)}) collective-permute-start(f32[512,64]{0,1:T(8,128)S(1)} %pad_maximum_fusion.1), channel_id=1, source_target_pairs={{0,64},{64,0},{1,65},{65,1},{2,66},{66,2},{3,67},{67,3},{4,68},{68... | collective-permute-start | bytes 393224 | tf_op jit(solution)/shard_map/ppermute | solution.py:25
  63.1 8.1 %collective-permute-start.6 = (f32[256,32]{0,1:T(8,128)S(1)}, f32[256,32]{0,1:T(8,128)S(1)}, u32[]{:S(2)}, u32[]{:S(2)}) collective-permute-start(f32[256,32]{0,1:T(8,128)S(1)} %convolution_add_fusion.5), channel_id=1, source_target_pairs={{0,1},{1,0},{2,3},{3,2},{4,5},{5,4},{6,7},{7,6},{8,9},{9,8},{10,11... | collective-permute-start | bytes 98312 | tf_op jit(solution)/shard_map/ppermute | solution.py:25
  67.2 24.4 %collective-permute-start.12 = (f32[512,64]{0,1:T(8,128)S(1)}, f32[512,64]{0,1:T(8,128)S(1)}, u32[]{:S(2)}, u32[]{:S(2)}) collective-permute-start(f32[512,64]{0,1:T(8,128)S(1)} %fusion.41), channel_id=1, source_target_pairs={{0,8},{8,0},{16,24},{24,16},{32,40},{40,32},{48,56},{56,48},{1,9},... | collective-permute-start | bytes 393224 | tf_op jit(solution)/shard_map/ppermute | solution.py:25
  75.9 6.2 %collective-permute-start.8 = (f32[256,32]{0,1:T(8,128)S(1)}, f32[256,32]{0,1:T(8,128)S(1)}, u32[]{:S(2)}, u32[]{:S(2)}) collective-permute-start(f32[256,32]{0,1:T(8,128)S(1)} %add.393), channel_id=1, source_target_pairs={{0,4},{2,6},{4,0},{6,2},{1,5},{3,7},{5,1},{7,3},{8,12},{10,14},{12... | collective-permute-start | bytes 98312 | tf_op jit(solution)/shard_map/ppermute | solution.py:25
  87.8 9.7 %collective-permute-start.10 = (f32[256,32]{0,1:T(8,128)S(1)}, f32[256,32]{0,1:T(8,128)S(1)}, u32[]{:S(2)}, u32[]{:S(2)}) collective-permute-start(f32[256,32]{0,1:T(8,128)S(1)} %add.395), channel_id=1, source_target_pairs={{0,256},{128,384},{256,0},{384,128},{1,257},{129,385},{257,1},{385... | collective-permute-start | bytes 98312 | tf_op jit(solution)/shard_map/ppermute | solution.py:25
  91.6 9.6 %collective-permute-start.13 = (f32[512,64]{0,1:T(8,128)S(1)}, f32[512,64]{0,1:T(8,128)S(1)}, u32[]{:S(2)}, u32[]{:S(2)}) collective-permute-start(f32[512,64]{0,1:T(8,128)S(1)} %add.398), channel_id=1, source_target_pairs={{0,16},{8,24},{16,0},{24,8},{32,48},{40,56},{48,32},{56,40},{1,17}... | collective-permute-start | bytes 393224 | tf_op jit(solution)/shard_map/ppermute | solution.py:25
  101.2 11.0 %collective-permute-start.14 = (f32[512,64]{0,1:T(8,128)S(1)}, f32[512,64]{0,1:T(8,128)S(1)}, u32[]{:S(2)}, u32[]{:S(2)}) collective-permute-start(f32[512,64]{0,1:T(8,128)S(1)} %add.399), channel_id=1, source_target_pairs={{0,32},{8,40},{16,48},{24,56},{32,0},{40,8},{48,16},{56,24},{1,33}... | collective-permute-start | bytes 393224 | tf_op jit(solution)/shard_map/ppermute | solution.py:25
  115.6 12.5 %collective-permute-start.15 = (f32[256,32]{0,1:T(8,128)S(1)}, f32[256,32]{0,1:T(8,128)S(1)}, u32[]{:S(2)}, u32[]{:S(2)}) collective-permute-start(f32[256,32]{0,1:T(8,128)S(1)} %convolution_add_fusion.4), channel_id=1, source_target_pairs={{0,1},{1,0},{2,3},{3,2},{4,5},{5,4},{6,7},{7,6},{8,9},{9,8},{10,11... | collective-permute-start | bytes 98312 | tf_op jit(solution)/shard_map/ppermute | solution.py:25
  123.2 26.9 %collective-permute-start.24 = (f32[512,64]{0,1:T(8,128)S(1)}, f32[512,64]{0,1:T(8,128)S(1)}, u32[]{:S(2)}, u32[]{:S(2)}) collective-permute-start(f32[512,64]{0,1:T(8,128)S(1)} %pad_maximum_fusion.2), channel_id=1, source_target_pairs={{0,64},{64,0},{1,65},{65,1},{2,66},{66,2},{3,67},{67,3},{4,68},{68... | collective-permute-start | bytes 393224 | tf_op jit(solution)/shard_map/ppermute | solution.py:25
  132.7 6.2 %collective-permute-start.17 = (f32[256,32]{0,1:T(8,128)S(1)}, f32[256,32]{0,1:T(8,128)S(1)}, u32[]{:S(2)}, u32[]{:S(2)}) collective-permute-start(f32[256,32]{0,1:T(8,128)S(1)} %add.404), channel_id=1, source_target_pairs={{0,4},{2,6},{4,0},{6,2},{1,5},{3,7},{5,1},{7,3},{8,12},{10,14},{12... | collective-permute-start | bytes 98312 | tf_op jit(solution)/shard_map/ppermute | solution.py:25
  138.9 5.9 %collective-permute-start.18 = (f32[256,32]{0,1:T(8,128)S(1)}, f32[256,32]{0,1:T(8,128)S(1)}, u32[]{:S(2)}, u32[]{:S(2)}) collective-permute-start(f32[256,32]{0,1:T(8,128)S(1)} %add.405), channel_id=1, source_target_pairs={{0,128},{128,0},{256,384},{384,256},{1,129},{129,1},{257,385},{385... | collective-permute-start | bytes 98312 | tf_op jit(solution)/shard_map/ppermute | solution.py:25
  144.8 8.6 %collective-permute-start.19 = (f32[256,32]{0,1:T(8,128)S(1)}, f32[256,32]{0,1:T(8,128)S(1)}, u32[]{:S(2)}, u32[]{:S(2)}) collective-permute-start(f32[256,32]{0,1:T(8,128)S(1)} %add.406), channel_id=1, source_target_pairs={{0,256},{128,384},{256,0},{384,128},{1,257},{129,385},{257,1},{385... | collective-permute-start | bytes 98312 | tf_op jit(solution)/shard_map/ppermute | solution.py:25
  150.1 8.2 %collective-permute-start.25 = (f32[512,64]{0,1:T(8,128)S(1)}, f32[512,64]{0,1:T(8,128)S(1)}, u32[]{:S(2)}, u32[]{:S(2)}) collective-permute-start(f32[512,64]{0,1:T(8,128)S(1)} %fusion.40), channel_id=1, source_target_pairs={{0,8},{8,0},{16,24},{24,16},{32,40},{40,32},{48,56},{56,48},{1,9},... | collective-permute-start | bytes 393224 | tf_op jit(solution)/shard_map/ppermute | solution.py:25
  158.4 8.4 %collective-permute-start.26 = (f32[512,64]{0,1:T(8,128)S(1)}, f32[512,64]{0,1:T(8,128)S(1)}, u32[]{:S(2)}, u32[]{:S(2)}) collective-permute-start(f32[512,64]{0,1:T(8,128)S(1)} %add.414), channel_id=1, source_target_pairs={{0,16},{8,24},{16,0},{24,8},{32,48},{40,56},{48,32},{56,40},{1,17}... | collective-permute-start | bytes 393224 | tf_op jit(solution)/shard_map/ppermute | solution.py:25
  162.4 11.3 %collective-permute-start.21 = (f32[2]{0:T(128)S(1)}, f32[2]{0:T(128)S(1)}, u32[]{:S(2)}, u32[]{:S(2)}) collective-permute-start(f32[2]{0:T(128)S(1)} %fusion.125), channel_id=1, source_target_pairs={{0,8},{8,0},{16,24},{24,16},{32,40},{40,32},{48,56},{56,48},{1,9},... | collective-permute-start | bytes 32 | tf_op jit(solution)/shard_map/ppermute | solution.py:25
  166.8 22.2 %collective-permute-start.27 = (f32[512,64]{0,1:T(8,128)S(1)}, f32[512,64]{0,1:T(8,128)S(1)}, u32[]{:S(2)}, u32[]{:S(2)}) collective-permute-start(f32[512,64]{0,1:T(8,128)S(1)} %add.415), channel_id=1, source_target_pairs={{0,32},{8,40},{16,48},{24,56},{32,0},{40,8},{48,16},{56,24},{1,33}... | collective-permute-start | bytes 393224 | tf_op jit(solution)/shard_map/ppermute | solution.py:25
  180.3 8.2 %collective-permute-start.23 = (f32[2]{0:T(128)S(1)}, f32[2]{0:T(128)S(1)}, u32[]{:S(2)}, u32[]{:S(2)}) collective-permute-start(f32[2]{0:T(128)S(1)} %add.411), channel_id=1, source_target_pairs={{0,32},{8,40},{16,48},{24,56},{32,0},{40,8},{48,16},{56,24},{1,33}... | collective-permute-start | bytes 32 | tf_op jit(solution)/shard_map/ppermute | solution.py:25
  191.1 10.8 %collective-permute-start.28 = (f32[2]{0:T(128)S(1)}, f32[2]{0:T(128)S(1)}, u32[]{:S(2)}, u32[]{:S(2)}) collective-permute-start(f32[2]{0:T(128)S(1)} %pad_maximum_fusion.8), channel_id=1, source_target_pairs={{0,1},{1,0},{2,3},{3,2},{4,5},{5,4},{6,7},{7,6},{8,9},{9,8},{10,11... | collective-permute-start | bytes 32 | tf_op jit(solution)/shard_map/ppermute | solution.py:25
  208.9 5.8 %collective-permute-start.30 = (f32[2]{0:T(128)S(1)}, f32[2]{0:T(128)S(1)}, u32[]{:S(2)}, u32[]{:S(2)}) collective-permute-start(f32[2]{0:T(128)S(1)} %fusion.130), channel_id=1, source_target_pairs={{0,4},{2,6},{4,0},{6,2},{1,5},{3,7},{5,1},{7,3},{8,12},{10,14},{12... | collective-permute-start | bytes 32 | tf_op jit(solution)/shard_map/ppermute | solution.py:25
  219.9 8.2 %collective-permute-start.32 = (f32[2]{0:T(128)S(1)}, f32[2]{0:T(128)S(1)}, u32[]{:S(2)}, u32[]{:S(2)}) collective-permute-start(f32[2]{0:T(128)S(1)} %add.422), channel_id=1, source_target_pairs={{0,256},{128,384},{256,0},{384,128},{1,257},{129,385},{257,1},{385... | collective-permute-start | bytes 32 | tf_op jit(solution)/shard_map/ppermute | solution.py:25
  233.5 10.8 %collective-permute-start.38 = (f32[512,64]{0,1:T(8,128)S(1)}, f32[512,64]{0,1:T(8,128)S(1)}, u32[]{:S(2)}, u32[]{:S(2)}) collective-permute-start(f32[512,64]{0,1:T(8,128)S(1)} %pad_maximum_fusion.3), channel_id=1, source_target_pairs={{0,64},{64,0},{1,65},{65,1},{2,66},{66,2},{3,67},{67,3},{4,68},{68... | collective-permute-start | bytes 393224 | tf_op jit(solution)/shard_map/ppermute | solution.py:25
  237.2 10.2 %collective-permute-start.33 = (f32[256,32]{0,1:T(8,128)S(1)}, f32[256,32]{0,1:T(8,128)S(1)}, u32[]{:S(2)}, u32[]{:S(2)}) collective-permute-start(f32[256,32]{0,1:T(8,128)S(1)} %convolution_add_fusion.3), channel_id=1, source_target_pairs={{0,1},{1,0},{2,3},{3,2},{4,5},{5,4},{6,7},{7,6},{8,9},{9,8},{10,11... | collective-permute-start | bytes 98312 | tf_op jit(solution)/shard_map/ppermute | solution.py:25
  244.3 25.6 %collective-permute-start.39 = (f32[512,64]{0,1:T(8,128)S(1)}, f32[512,64]{0,1:T(8,128)S(1)}, u32[]{:S(2)}, u32[]{:S(2)}) collective-permute-start(f32[512,64]{0,1:T(8,128)S(1)} %fusion.39), channel_id=1, source_target_pairs={{0,8},{8,0},{16,24},{24,16},{32,40},{40,32},{48,56},{56,48},{1,9},... | collective-permute-start | bytes 393224 | tf_op jit(solution)/shard_map/ppermute | solution.py:25
  252.0 6.2 %collective-permute-start.35 = (f32[256,32]{0,1:T(8,128)S(1)}, f32[256,32]{0,1:T(8,128)S(1)}, u32[]{:S(2)}, u32[]{:S(2)}) collective-permute-start(f32[256,32]{0,1:T(8,128)S(1)} %add.431), channel_id=1, source_target_pairs={{0,4},{2,6},{4,0},{6,2},{1,5},{3,7},{5,1},{7,3},{8,12},{10,14},{12... | collective-permute-start | bytes 98312 | tf_op jit(solution)/shard_map/ppermute | solution.py:25
  263.9 10.0 %collective-permute-start.37 = (f32[256,32]{0,1:T(8,128)S(1)}, f32[256,32]{0,1:T(8,128)S(1)}, u32[]{:S(2)}, u32[]{:S(2)}) collective-permute-start(f32[256,32]{0,1:T(8,128)S(1)} %add.433), channel_id=1, source_target_pairs={{0,256},{128,384},{256,0},{384,128},{1,257},{129,385},{257,1},{385... | collective-permute-start | bytes 98312 | tf_op jit(solution)/shard_map/ppermute | solution.py:25
  270.0 8.0 %collective-permute-start.40 = (f32[512,64]{0,1:T(8,128)S(1)}, f32[512,64]{0,1:T(8,128)S(1)}, u32[]{:S(2)}, u32[]{:S(2)}) collective-permute-start(f32[512,64]{0,1:T(8,128)S(1)} %add.436), channel_id=1, source_target_pairs={{0,16},{8,24},{16,0},{24,8},{32,48},{40,56},{48,32},{56,40},{1,17}... | collective-permute-start | bytes 393224 | tf_op jit(solution)/shard_map/ppermute | solution.py:25
  278.0 9.7 %collective-permute-start.41 = (f32[512,64]{0,1:T(8,128)S(1)}, f32[512,64]{0,1:T(8,128)S(1)}, u32[]{:S(2)}, u32[]{:S(2)}) collective-permute-start(f32[512,64]{0,1:T(8,128)S(1)} %add.437), channel_id=1, source_target_pairs={{0,32},{8,40},{16,48},{24,56},{32,0},{40,8},{48,16},{56,24},{1,33}... | collective-permute-start | bytes 393224 | tf_op jit(solution)/shard_map/ppermute | solution.py:25
  291.1 12.0 %collective-permute-start.42 = (f32[256,32]{0,1:T(8,128)S(1)}, f32[256,32]{0,1:T(8,128)S(1)}, u32[]{:S(2)}, u32[]{:S(2)}) collective-permute-start(f32[256,32]{0,1:T(8,128)S(1)} %convolution_add_fusion.2), channel_id=1, source_target_pairs={{0,1},{1,0},{2,3},{3,2},{4,5},{5,4},{6,7},{7,6},{8,9},{9,8},{10,11... | collective-permute-start | bytes 98312 | tf_op jit(solution)/shard_map/ppermute | solution.py:25
  298.8 26.6 %collective-permute-start.51 = (f32[512,64]{0,1:T(8,128)S(1)}, f32[512,64]{0,1:T(8,128)S(1)}, u32[]{:S(2)}, u32[]{:S(2)}) collective-permute-start(f32[512,64]{0,1:T(8,128)S(1)} %pad_maximum_fusion.4), channel_id=1, source_target_pairs={{0,64},{64,0},{1,65},{65,1},{2,66},{66,2},{3,67},{67,3},{4,68},{68... | collective-permute-start | bytes 393224 | tf_op jit(solution)/shard_map/ppermute | solution.py:25
  307.9 6.2 %collective-permute-start.44 = (f32[256,32]{0,1:T(8,128)S(1)}, f32[256,32]{0,1:T(8,128)S(1)}, u32[]{:S(2)}, u32[]{:S(2)}) collective-permute-start(f32[256,32]{0,1:T(8,128)S(1)} %add.442), channel_id=1, source_target_pairs={{0,4},{2,6},{4,0},{6,2},{1,5},{3,7},{5,1},{7,3},{8,12},{10,14},{12... | collective-permute-start | bytes 98312 | tf_op jit(solution)/shard_map/ppermute | solution.py:25
  319.6 8.6 %collective-permute-start.46 = (f32[256,32]{0,1:T(8,128)S(1)}, f32[256,32]{0,1:T(8,128)S(1)}, u32[]{:S(2)}, u32[]{:S(2)}) collective-permute-start(f32[256,32]{0,1:T(8,128)S(1)} %add.444), channel_id=1, source_target_pairs={{0,256},{128,384},{256,0},{384,128},{1,257},{129,385},{257,1},{385... | collective-permute-start | bytes 98312 | tf_op jit(solution)/shard_map/ppermute | solution.py:25
  325.4 8.1 %collective-permute-start.52 = (f32[512,64]{0,1:T(8,128)S(1)}, f32[512,64]{0,1:T(8,128)S(1)}, u32[]{:S(2)}, u32[]{:S(2)}) collective-permute-start(f32[512,64]{0,1:T(8,128)S(1)} %fusion.38), channel_id=1, source_target_pairs={{0,8},{8,0},{16,24},{24,16},{32,40},{40,32},{48,56},{56,48},{1,9},... | collective-permute-start | bytes 393224 | tf_op jit(solution)/shard_map/ppermute | solution.py:25
  330.8 6.2 %collective-permute-start.47 = (f32[2]{0:T(128)S(1)}, f32[2]{0:T(128)S(1)}, u32[]{:S(2)}, u32[]{:S(2)}) collective-permute-start(f32[2]{0:T(128)S(1)} %pad_maximum_fusion.9), channel_id=1, source_target_pairs={{0,64},{64,0},{1,65},{65,1},{2,66},{66,2},{3,67},{67,3},{4,68},{68... | collective-permute-start | bytes 32 | tf_op jit(solution)/shard_map/ppermute | solution.py:25
  333.6 8.0 %collective-permute-start.53 = (f32[512,64]{0,1:T(8,128)S(1)}, f32[512,64]{0,1:T(8,128)S(1)}, u32[]{:S(2)}, u32[]{:S(2)}) collective-permute-start(f32[512,64]{0,1:T(8,128)S(1)} %add.452), channel_id=1, source_target_pairs={{0,16},{8,24},{16,0},{24,8},{32,48},{40,56},{48,32},{56,40},{1,17}... | collective-permute-start | bytes 393224 | tf_op jit(solution)/shard_map/ppermute | solution.py:25
  341.6 17.6 %collective-permute-start.54 = (f32[512,64]{0,1:T(8,128)S(1)}, f32[512,64]{0,1:T(8,128)S(1)}, u32[]{:S(2)}, u32[]{:S(2)}) collective-permute-start(f32[512,64]{0,1:T(8,128)S(1)} %add.453), channel_id=1, source_target_pairs={{0,32},{8,40},{16,48},{24,56},{32,0},{40,8},{48,16},{56,24},{1,33}... | collective-permute-start | bytes 393224 | tf_op jit(solution)/shard_map/ppermute | solution.py:25
  350.2 8.5 %collective-permute-start.50 = (f32[2]{0:T(128)S(1)}, f32[2]{0:T(128)S(1)}, u32[]{:S(2)}, u32[]{:S(2)}) collective-permute-start(f32[2]{0:T(128)S(1)} %add.449), channel_id=1, source_target_pairs={{0,32},{8,40},{16,48},{24,56},{32,0},{40,8},{48,16},{56,24},{1,33}... | collective-permute-start | bytes 32 | tf_op jit(solution)/shard_map/ppermute | solution.py:25
  361.3 12.1 %collective-permute-start.55 = (f32[2]{0:T(128)S(1)}, f32[2]{0:T(128)S(1)}, u32[]{:S(2)}, u32[]{:S(2)}) collective-permute-start(f32[2]{0:T(128)S(1)} %pad_maximum_fusion.10), channel_id=1, source_target_pairs={{0,1},{1,0},{2,3},{3,2},{4,5},{5,4},{6,7},{7,6},{8,9},{9,8},{10,11... | collective-permute-start | bytes 32 | tf_op jit(solution)/shard_map/ppermute | solution.py:25
  380.4 5.8 %collective-permute-start.57 = (f32[2]{0:T(128)S(1)}, f32[2]{0:T(128)S(1)}, u32[]{:S(2)}, u32[]{:S(2)}) collective-permute-start(f32[2]{0:T(128)S(1)} %fusion.128), channel_id=1, source_target_pairs={{0,4},{2,6},{4,0},{6,2},{1,5},{3,7},{5,1},{7,3},{8,12},{10,14},{12... | collective-permute-start | bytes 32 | tf_op jit(solution)/shard_map/ppermute | solution.py:25
  391.3 8.2 %collective-permute-start.59 = (f32[2]{0:T(128)S(1)}, f32[2]{0:T(128)S(1)}, u32[]{:S(2)}, u32[]{:S(2)}) collective-permute-start(f32[2]{0:T(128)S(1)} %add.460), channel_id=1, source_target_pairs={{0,256},{128,384},{256,0},{384,128},{1,257},{129,385},{257,1},{385... | collective-permute-start | bytes 32 | tf_op jit(solution)/shard_map/ppermute | solution.py:25
  405.0 10.6 %collective-permute-start.65 = (f32[512,64]{0,1:T(8,128)S(1)}, f32[512,64]{0,1:T(8,128)S(1)}, u32[]{:S(2)}, u32[]{:S(2)}) collective-permute-start(f32[512,64]{0,1:T(8,128)S(1)} %pad_maximum_fusion.5), channel_id=1, source_target_pairs={{0,64},{64,0},{1,65},{65,1},{2,66},{66,2},{3,67},{67,3},{4,68},{68... | collective-permute-start | bytes 393224 | tf_op jit(solution)/shard_map/ppermute | solution.py:25
  408.5 9.1 %collective-permute-start.60 = (f32[256,32]{0,1:T(8,128)S(1)}, f32[256,32]{0,1:T(8,128)S(1)}, u32[]{:S(2)}, u32[]{:S(2)}) collective-permute-start(f32[256,32]{0,1:T(8,128)S(1)} %convolution_add_fusion.1), channel_id=1, source_target_pairs={{0,1},{1,0},{2,3},{3,2},{4,5},{5,4},{6,7},{7,6},{8,9},{9,8},{10,11... | collective-permute-start | bytes 98312 | tf_op jit(solution)/shard_map/ppermute | solution.py:25
  415.6 22.8 %collective-permute-start.66 = (f32[512,64]{0,1:T(8,128)S(1)}, f32[512,64]{0,1:T(8,128)S(1)}, u32[]{:S(2)}, u32[]{:S(2)}) collective-permute-start(f32[512,64]{0,1:T(8,128)S(1)} %fusion.37), channel_id=1, source_target_pairs={{0,8},{8,0},{16,24},{24,16},{32,40},{40,32},{48,56},{56,48},{1,9},... | collective-permute-start | bytes 393224 | tf_op jit(solution)/shard_map/ppermute | solution.py:25
  422.6 6.2 %collective-permute-start.62 = (f32[256,32]{0,1:T(8,128)S(1)}, f32[256,32]{0,1:T(8,128)S(1)}, u32[]{:S(2)}, u32[]{:S(2)}) collective-permute-start(f32[256,32]{0,1:T(8,128)S(1)} %add.469), channel_id=1, source_target_pairs={{0,4},{2,6},{4,0},{6,2},{1,5},{3,7},{5,1},{7,3},{8,12},{10,14},{12... | collective-permute-start | bytes 98312 | tf_op jit(solution)/shard_map/ppermute | solution.py:25
  434.3 8.6 %collective-permute-start.64 = (f32[256,32]{0,1:T(8,128)S(1)}, f32[256,32]{0,1:T(8,128)S(1)}, u32[]{:S(2)}, u32[]{:S(2)}) collective-permute-start(f32[256,32]{0,1:T(8,128)S(1)} %add.471), channel_id=1, source_target_pairs={{0,256},{128,384},{256,0},{384,128},{1,257},{129,385},{257,1},{385... | collective-permute-start | bytes 98312 | tf_op jit(solution)/shard_map/ppermute | solution.py:25
  438.5 8.3 %collective-permute-start.67 = (f32[512,64]{0,1:T(8,128)S(1)}, f32[512,64]{0,1:T(8,128)S(1)}, u32[]{:S(2)}, u32[]{:S(2)}) collective-permute-start(f32[512,64]{0,1:T(8,128)S(1)} %add.474), channel_id=1, source_target_pairs={{0,16},{8,24},{16,0},{24,8},{32,48},{40,56},{48,32},{56,40},{1,17}... | collective-permute-start | bytes 393224 | tf_op jit(solution)/shard_map/ppermute | solution.py:25
  446.8 10.2 %collective-permute-start.68 = (f32[512,64]{0,1:T(8,128)S(1)}, f32[512,64]{0,1:T(8,128)S(1)}, u32[]{:S(2)}, u32[]{:S(2)}) collective-permute-start(f32[512,64]{0,1:T(8,128)S(1)} %add.475), channel_id=1, source_target_pairs={{0,32},{8,40},{16,48},{24,56},{32,0},{40,8},{48,16},{56,24},{1,33}... | collective-permute-start | bytes 393224 | tf_op jit(solution)/shard_map/ppermute | solution.py:25
  460.3 10.8 %collective-permute-start.69 = (f32[256,32]{0,1:T(8,128)S(1)}, f32[256,32]{0,1:T(8,128)S(1)}, u32[]{:S(2)}, u32[]{:S(2)}) collective-permute-start(f32[256,32]{0,1:T(8,128)S(1)} %convolution_add_fusion), channel_id=1, source_target_pairs={{0,1},{1,0},{2,3},{3,2},{4,5},{5,4},{6,7},{7,6},{8,9},{9,8},{10,11... | collective-permute-start | bytes 98312 | tf_op jit(solution)/shard_map/ppermute | solution.py:25
  468.1 25.4 %collective-permute-start.78 = (f32[512,64]{0,1:T(8,128)S(1)}, f32[512,64]{0,1:T(8,128)S(1)}, u32[]{:S(2)}, u32[]{:S(2)}) collective-permute-start(f32[512,64]{0,1:T(8,128)S(1)} %pad_maximum_fusion.6), channel_id=1, source_target_pairs={{0,64},{64,0},{1,65},{65,1},{2,66},{66,2},{3,67},{67,3},{4,68},{68... | collective-permute-start | bytes 393224 | tf_op jit(solution)/shard_map/ppermute | solution.py:25
  475.8 6.2 %collective-permute-start.71 = (f32[256,32]{0,1:T(8,128)S(1)}, f32[256,32]{0,1:T(8,128)S(1)}, u32[]{:S(2)}, u32[]{:S(2)}) collective-permute-start(f32[256,32]{0,1:T(8,128)S(1)} %add.480), channel_id=1, source_target_pairs={{0,4},{2,6},{4,0},{6,2},{1,5},{3,7},{5,1},{7,3},{8,12},{10,14},{12... | collective-permute-start | bytes 98312 | tf_op jit(solution)/shard_map/ppermute | solution.py:25
  487.5 8.8 %collective-permute-start.73 = (f32[256,32]{0,1:T(8,128)S(1)}, f32[256,32]{0,1:T(8,128)S(1)}, u32[]{:S(2)}, u32[]{:S(2)}) collective-permute-start(f32[256,32]{0,1:T(8,128)S(1)} %add.482), channel_id=1, source_target_pairs={{0,256},{128,384},{256,0},{384,128},{1,257},{129,385},{257,1},{385... | collective-permute-start | bytes 98312 | tf_op jit(solution)/shard_map/ppermute | solution.py:25
  493.5 8.4 %collective-permute-start.79 = (f32[512,64]{0,1:T(8,128)S(1)}, f32[512,64]{0,1:T(8,128)S(1)}, u32[]{:S(2)}, u32[]{:S(2)}) collective-permute-start(f32[512,64]{0,1:T(8,128)S(1)} %fusion.36), channel_id=1, source_target_pairs={{0,8},{8,0},{16,24},{24,16},{32,40},{40,32},{48,56},{56,48},{1,9},... | collective-permute-start | bytes 393224 | tf_op jit(solution)/shard_map/ppermute | solution.py:25
  498.9 7.1 %collective-permute-start.74 = (f32[2]{0:T(128)S(1)}, f32[2]{0:T(128)S(1)}, u32[]{:S(2)}, u32[]{:S(2)}) collective-permute-start(f32[2]{0:T(128)S(1)} %pad_maximum_fusion.11), channel_id=1, source_target_pairs={{0,64},{64,0},{1,65},{65,1},{2,66},{66,2},{3,67},{67,3},{4,68},{68... | collective-permute-start | bytes 32 | tf_op jit(solution)/shard_map/ppermute | solution.py:25
  501.9 8.5 %collective-permute-start.80 = (f32[512,64]{0,1:T(8,128)S(1)}, f32[512,64]{0,1:T(8,128)S(1)}, u32[]{:S(2)}, u32[]{:S(2)}) collective-permute-start(f32[512,64]{0,1:T(8,128)S(1)} %add.490), channel_id=1, source_target_pairs={{0,16},{8,24},{16,0},{24,8},{32,48},{40,56},{48,32},{56,40},{1,17}... | collective-permute-start | bytes 393224 | tf_op jit(solution)/shard_map/ppermute | solution.py:25
  507.3 10.5 %collective-permute-start.75 = (f32[2]{0:T(128)S(1)}, f32[2]{0:T(128)S(1)}, u32[]{:S(2)}, u32[]{:S(2)}) collective-permute-start(f32[2]{0:T(128)S(1)} %fusion.121), channel_id=1, source_target_pairs={{0,8},{8,0},{16,24},{24,16},{32,40},{40,32},{48,56},{56,48},{1,9},... | collective-permute-start | bytes 32 | tf_op jit(solution)/shard_map/ppermute | solution.py:25
  510.4 22.7 %collective-permute-start.81 = (f32[512,64]{0,1:T(8,128)S(1)}, f32[512,64]{0,1:T(8,128)S(1)}, u32[]{:S(2)}, u32[]{:S(2)}) collective-permute-start(f32[512,64]{0,1:T(8,128)S(1)} %add.491), channel_id=1, source_target_pairs={{0,32},{8,40},{16,48},{24,56},{32,0},{40,8},{48,16},{56,24},{1,33}... | collective-permute-start | bytes 393224 | tf_op jit(solution)/shard_map/ppermute | solution.py:25
  524.4 8.2 %collective-permute-start.77 = (f32[2]{0:T(128)S(1)}, f32[2]{0:T(128)S(1)}, u32[]{:S(2)}, u32[]{:S(2)}) collective-permute-start(f32[2]{0:T(128)S(1)} %add.487), channel_id=1, source_target_pairs={{0,32},{8,40},{16,48},{24,56},{32,0},{40,8},{48,16},{56,24},{1,33}... | collective-permute-start | bytes 32 | tf_op jit(solution)/shard_map/ppermute | solution.py:25
  535.2 11.1 %collective-permute-start.82 = (f32[2]{0:T(128)S(1)}, f32[2]{0:T(128)S(1)}, u32[]{:S(2)}, u32[]{:S(2)}) collective-permute-start(f32[2]{0:T(128)S(1)} %pad_maximum_fusion.12), channel_id=1, source_target_pairs={{0,1},{1,0},{2,3},{3,2},{4,5},{5,4},{6,7},{7,6},{8,9},{9,8},{10,11... | collective-permute-start | bytes 32 | tf_op jit(solution)/shard_map/ppermute | solution.py:25
  564.2 8.6 %collective-permute-start.86 = (f32[2]{0:T(128)S(1)}, f32[2]{0:T(128)S(1)}, u32[]{:S(2)}, u32[]{:S(2)}) collective-permute-start(f32[2]{0:T(128)S(1)} %add.498), channel_id=1, source_target_pairs={{0,256},{128,384},{256,0},{384,128},{1,257},{129,385},{257,1},{385... | collective-permute-start | bytes 32 | tf_op jit(solution)/shard_map/ppermute | solution.py:25
  (26 other events, 147.0 us)

commit v3 on v2

--- a/solution.py
+++ b/solution.py
@@ -25,6 +25,15 @@
             value = value + lax.ppermute(value, name, pairs)
             step *= 2
     return value
+
+
+def group_total(value, axes):
+    count = 1
+    for name in axes:
+        count *= lax.axis_size(name)
+    spread = jnp.broadcast_to(value[None], (count,) + value.shape)
+    gathered = lax.all_to_all(spread, axes, 0, 0, tiled=True)
+    return jnp.sum(gathered, axis=0)
 
 
 def doubling_gather(value, axes):
@@ -82,8 +91,8 @@
         rf = f_one - f_zero
         vq = q_two - 2.0 * q_one + q_zero
         vf = f_two - 2.0 * f_one + f_zero
-        q_parts = doubling_sum(jnp.stack([jnp.sum(rq * rq), jnp.sum(vq * vq)]), ROW_GROUP)
-        f_parts = doubling_sum(jnp.stack([jnp.sum(rf * rf), jnp.sum(vf * vf)]), COL_GROUP)
+        q_parts = group_total(jnp.stack([jnp.sum(rq * rq), jnp.sum(vq * vq)]), ROW_GROUP)
+        f_parts = group_total(jnp.stack([jnp.sum(rf * rf), jnp.sum(vf * vf)]), COL_GROUP)
         first = q_parts[0] + f_parts[0]
         second = q_parts[1] + f_parts[1]
         alpha = -jnp.sqrt(first / (second + 1e-20))

time: 586 us -> 500 us (0.85); the launches traced: 578 us -> 498 us
  starting transfers between devices: 386 us -> 281 us
  blocking collectives: 0 us -> 25.3 us
  other arithmetic: 40.3 us -> 24.3 us
  waiting for transfers between devices: 112 us -> 125 us
    ppermute x81 -> x54, starting transfers between devices: 349 us -> 201 us  [doubling_sum(): value = value + lax.ppermute(value, name, pairs)]
    all_to_all x0 -> x4, starting transfers between devices: none -> 43.9 us  [group_total(): gathered = lax.all_to_all(spread, axes, 0, 0, tiled=True)]
    all_to_all x0 -> x4, waiting for transfers between devices: none -> 33 us  [group_total(): gathered = lax.all_to_all(spread, axes, 0, 0, tiled=True)]
    all_to_all x0 -> x2, blocking collectives: none -> 25.3 us  [group_total(): gathered = lax.all_to_all(spread, axes, 0, 0, tiled=True)]
    ppermute x81 -> x54, waiting for transfers between devices: 108 us -> 88.1 us  [doubling_sum(): value = value + lax.ppermute(value, name, pairs)]
    add x75 -> x48, other arithmetic: 16.9 us -> 0.61 us  [doubling_sum(): value = value + lax.ppermute(value, name, pairs)]
  transfers between devices with their start and end apart: 88 -> 65, of which waited for: 51 -> 37; matrix products, arithmetic and copies ran while one was open for 5% -> 4% of each run, Pallas kernels for 0% -> 0%
where the time goes in v3:
time: 500 us; the launch traced here: 498 us
  starting transfers between devices  281 us (56%)
  waiting for transfers between devices  125 us (25%)
  blocking collectives  25.3 us (5%)
  other arithmetic  24.3 us (5%)
  matrix products  16.2 us (3%)
  local copies, waits for them, and re-layouts  15.8 us (3%)
  between operations  10 us (2%)
    ppermute x54, starting transfers between devices, doubling_sum(): value = value + lax.ppermute(value, name, pairs)  201 us
    ppermute x54, waiting for transfers between devices, doubling_sum(): value = value + lax.ppermute(value, name, pairs)  88.1 us
    all_to_all x4, starting transfers between devices, group_total(): gathered = lax.all_to_all(spread, axes, 0, 0, tiled=True)  43.9 us
    all_to_all x4, waiting for transfers between devices, group_total(): gathered = lax.all_to_all(spread, axes, 0, 0, tiled=True)  33 us
    ppermute x6, starting transfers between devices, doubling_gather(): other = lax.ppermute(value, name, pairs)  29 us
    all_to_all x2, blocking collectives, group_total(): gathered = lax.all_to_all(spread, axes, 0, 0, tiled=True)  25.3 us
  transfers between devices with their start and end apart: 65, of which 37 were waited for; matrix products, arithmetic and copies ran while one was open for 4% of the time, Pallas kernels for 0%

profile of v3, /device:TPU:1, one launch (start us, length us, event | category | flops | bytes accessed | tf_op | source)
XLA Modules:
  0.0 497.5 jit_solution(8258687508116548786)
XLA Ops:
  6.0 3.1 reshape.84
  9.1 7.6 %all-to-all-start = ((f32[4,1,65536]{2,1,0:T(1,128)}), f32[4,1,65536]{2,1,0:T(1,128)S(1)}, u32[]{:S(2)}, u32[]{:S(2)}) async-start(f32[4,1,65536]{2,1,0:T(1,128)} %reshape.84), calls=%async_computation | async-start | bytes 2097152 | tf_op jit(solution)/shard_map/all_to_all | solution.py:58
  16.8 4.0 collective-permute-start.2
  22.0 5.8 %collective-permute-start.3 = (f32[64,32]{0,1:T(8,128)S(1)}, f32[64,32]{0,1:T(8,128)S(1)}, u32[]{:S(2)}, u32[]{:S(2)}) collective-permute-start(f32[64,32]{0,1:T(8,128)S(1)} %maximum_select_fusion.4), channel_id=1, source_target_pairs={{0,16},{8,24},{16,0},{24,8},{32,48},{40,56},{48,32},{56,40},{1,17}... | collective-permute-start | bytes 24584 | tf_op jit(solution)/shard_map/ppermute | solution.py:46
  27.9 4.6 collective-permute-start
  32.6 8.2 %collective-permute-start.4 = (f32[128,32]{0,1:T(8,128)S(1)}, f32[128,32]{0,1:T(8,128)S(1)}, u32[]{:S(2)}, u32[]{:S(2)}) collective-permute-start(f32[128,32]{0,1:T(8,128)S(1)} %maximum_select_fusion.5), channel_id=1, source_target_pairs={{0,32},{8,40},{16,48},{24,56},{32,0},{40,8},{48,16},{56,24},{1,33}... | collective-permute-start | bytes 49160 | tf_op jit(solution)/shard_map/ppermute | solution.py:46
  43.6 4.5 collective-permute-start.1
  50.6 3.7 reduce.6
  58.6 3.4 collective-permute-start.11
  63.1 4.0 collective-permute-start.6
  67.2 4.0 collective-permute-start.12
  71.2 3.1 collective-permute-start.7
  75.9 4.6 collective-permute-start.8
  84.7 3.0 collective-permute-done.9
  87.8 3.8 collective-permute-start.10
  91.6 5.8 %collective-permute-start.13 = (f32[512,64]{0,1:T(8,128)S(1)}, f32[512,64]{0,1:T(8,128)S(1)}, u32[]{:S(2)}, u32[]{:S(2)}) collective-permute-start(f32[512,64]{0,1:T(8,128)S(1)} %add.317), channel_id=1, source_target_pairs={{0,16},{8,24},{16,0},{24,8},{32,48},{40,56},{48,32},{56,40},{1,17}... | collective-permute-start | bytes 393224 | tf_op jit(solution)/shard_map/ppermute | solution.py:25
  97.5 3.7 collective-permute-done.13
  101.2 8.8 %collective-permute-start.14 = (f32[512,64]{0,1:T(8,128)S(1)}, f32[512,64]{0,1:T(8,128)S(1)}, u32[]{:S(2)}, u32[]{:S(2)}) collective-permute-start(f32[512,64]{0,1:T(8,128)S(1)} %add.318), channel_id=1, source_target_pairs={{0,32},{8,40},{16,48},{24,56},{32,0},{40,8},{48,16},{56,24},{1,33}... | collective-permute-start | bytes 393224 | tf_op jit(solution)/shard_map/ppermute | solution.py:25
  115.1 2.9 collective-permute-start.20
  118.5 9.8 %collective-permute-start.15 = (f32[256,32]{0,1:T(8,128)S(1)}, f32[256,32]{0,1:T(8,128)S(1)}, u32[]{:S(2)}, u32[]{:S(2)}) collective-permute-start(f32[256,32]{0,1:T(8,128)S(1)} %convolution_add_fusion.4), channel_id=1, source_target_pairs={{0,1},{1,0},{2,3},{3,2},{4,5},{5,4},{6,7},{7,6},{8,9},{9,8},{10,11... | collective-permute-start | bytes 98312 | tf_op jit(solution)/shard_map/ppermute | solution.py:25
  130.3 3.1 collective-permute-start.16
  135.3 4.6 collective-permute-start.17
  143.4 3.6 collective-permute-done.18
  147.0 5.4 %collective-permute-start.19 = (f32[256,32]{0,1:T(8,128)S(1)}, f32[256,32]{0,1:T(8,128)S(1)}, u32[]{:S(2)}, u32[]{:S(2)}) collective-permute-start(f32[256,32]{0,1:T(8,128)S(1)} %add.325), channel_id=1, source_target_pairs={{0,256},{128,384},{256,0},{384,128},{1,257},{129,385},{257,1},{385... | collective-permute-start | bytes 98312 | tf_op jit(solution)/shard_map/ppermute | solution.py:25
  152.4 4.2 collective-permute-start.22
  157.3 3.1 collective-permute-done.22
  160.5 7.5 %collective-permute-start.23 = (f32[512,64]{0,1:T(8,128)S(1)}, f32[512,64]{0,1:T(8,128)S(1)}, u32[]{:S(2)}, u32[]{:S(2)}) collective-permute-start(f32[512,64]{0,1:T(8,128)S(1)} %add.330), channel_id=1, source_target_pairs={{0,32},{8,40},{16,48},{24,56},{32,0},{40,8},{48,16},{56,24},{1,33}... | collective-permute-start | bytes 393224 | tf_op jit(solution)/shard_map/ppermute | solution.py:25
  170.0 10.5 %all_to_all.51 = f32[16,1,2]{2,1,0:T(1,128)S(1)} all-to-all(f32[16,1,2]{2,1,0:T(1,128)S(1)} %broadcast_in_dim.12), channel_id=1, replica_groups=mesh['yh'=4,'yl'=2,'z'=8,'x'=4,'c'=2] {'yl','z'}, dimensions={0} | all-to-all | bytes 256 | tf_op jit(solution)/shard_map/all_to_all | solution.py:35
  183.3 15.0 %all-to-all-start.2 = ((f32[32,1,2]{2,1,0:T(1,128)}), f32[32,1,2]{2,1,0:T(1,128)S(1)}, u32[]{:S(2)}, u32[]{:S(2)}) async-start(f32[32,1,2]{2,1,0:T(1,128)} %broadcast_in_dim.13), calls=%async_computation.2 | async-start | bytes 32768 | tf_op jit(solution)/shard_map/all_to_all | solution.py:35
  198.8 8.6 %all-to-all-done.2 = f32[32,1,2]{2,1,0:T(1,128)S(1)} async-done(((f32[32,1,2]{2,1,0:T(1,128)}), f32[32,1,2]{2,1,0:T(1,128)S(1)}, u32[]{:S(2)}, u32[]{:S(2)}) %all-to-all-start.2) | async-done | bytes 288 | tf_op jit(solution)/shard_map/all_to_all | solution.py:35
  215.8 2.9 collective-permute-start.24
  229.3 3.3 collective-permute-done.26
  234.7 3.4 collective-permute-done.27
  242.7 4.1 collective-permute-done.28
  248.5 3.1 collective-permute-start.32
  251.6 6.6 %collective-permute-done.32 = f32[512,64]{0,1:T(8,128)S(1)} collective-permute-done((f32[512,64]{0,1:T(8,128)S(1)}, f32[512,64]{0,1:T(8,128)S(1)}, u32[]{:S(2)}, u32[]{:S(2)}) %collective-permute-start.32) | collective-permute-done | bytes 131104 | tf_op jit(solution)/shard_map/ppermute | solution.py:25
  264.4 10.2 %collective-permute-start.33 = (f32[256,32]{0,1:T(8,128)S(1)}, f32[256,32]{0,1:T(8,128)S(1)}, u32[]{:S(2)}, u32[]{:S(2)}) collective-permute-start(f32[256,32]{0,1:T(8,128)S(1)} %convolution_add_fusion.2), channel_id=1, source_target_pairs={{0,1},{1,0},{2,3},{3,2},{4,5},{5,4},{6,7},{7,6},{8,9},{9,8},{10,11... | collective-permute-start | bytes 98312 | tf_op jit(solution)/shard_map/ppermute | solution.py:25
  284.0 3.5 collective-permute-done.35
  287.5 3.8 collective-permute-start.36
  293.0 6.9 %collective-permute-start.37 = (f32[256,32]{0,1:T(8,128)S(1)}, f32[256,32]{0,1:T(8,128)S(1)}, u32[]{:S(2)}, u32[]{:S(2)}) collective-permute-start(f32[256,32]{0,1:T(8,128)S(1)} %add.354), channel_id=1, source_target_pairs={{0,256},{128,384},{256,0},{384,128},{1,257},{129,385},{257,1},{385... | collective-permute-start | bytes 98312 | tf_op jit(solution)/shard_map/ppermute | solution.py:25
  300.0 3.0 collective-permute-start.40
  303.6 3.3 collective-permute-done.40
  306.9 3.5 collective-permute-start.41
  312.5 14.8 %all_to_all.52 = f32[16,1,2]{2,1,0:T(1,128)S(1)} all-to-all(f32[16,1,2]{2,1,0:T(1,128)S(1)} %broadcast_in_dim.14), channel_id=1, replica_groups=mesh['yh'=4,'yl'=2,'z'=8,'x'=4,'c'=2] {'yl','z'}, dimensions={0} | all-to-all | bytes 256 | tf_op jit(solution)/shard_map/all_to_all | solution.py:35
  329.9 10.7 %all-to-all-start.4 = ((f32[32,1,2]{2,1,0:T(1,128)}), f32[32,1,2]{2,1,0:T(1,128)S(1)}, u32[]{:S(2)}, u32[]{:S(2)}) async-start(f32[32,1,2]{2,1,0:T(1,128)} %broadcast_in_dim.15), calls=%async_computation.4 | async-start | bytes 32768 | tf_op jit(solution)/shard_map/all_to_all | solution.py:35
  341.1 8.6 %all-to-all-done.4 = f32[32,1,2]{2,1,0:T(1,128)S(1)} async-done(((f32[32,1,2]{2,1,0:T(1,128)}), f32[32,1,2]{2,1,0:T(1,128)S(1)}, u32[]{:S(2)}, u32[]{:S(2)}) %all-to-all-start.4) | async-done | bytes 288 | tf_op jit(solution)/shard_map/all_to_all | solution.py:35
  358.2 2.9 collective-permute-start.42
  371.5 3.3 collective-permute-done.44
  377.0 3.3 collective-permute-done.45
  384.9 4.0 collective-permute-done.46
  390.8 3.1 collective-permute-start.50
  393.9 6.6 %collective-permute-done.50 = f32[512,64]{0,1:T(8,128)S(1)} collective-permute-done((f32[512,64]{0,1:T(8,128)S(1)}, f32[512,64]{0,1:T(8,128)S(1)}, u32[]{:S(2)}, u32[]{:S(2)}) %collective-permute-start.50) | collective-permute-done | bytes 131104 | tf_op jit(solution)/shard_map/ppermute | solution.py:25
  403.3 3.3 collective-permute-start.56
  407.1 9.8 %collective-permute-start.51 = (f32[256,32]{0,1:T(8,128)S(1)}, f32[256,32]{0,1:T(8,128)S(1)}, u32[]{:S(2)}, u32[]{:S(2)}) collective-permute-start(f32[256,32]{0,1:T(8,128)S(1)} %convolution_add_fusion), channel_id=1, source_target_pairs={{0,1},{1,0},{2,3},{3,2},{4,5},{5,4},{6,7},{7,6},{8,9},{9,8},{10,11... | collective-permute-start | bytes 98312 | tf_op jit(solution)/shard_map/ppermute | solution.py:25
  426.3 3.5 collective-permute-done.53
  429.7 3.8 collective-permute-start.54
  435.3 6.9 %collective-permute-start.55 = (f32[256,32]{0,1:T(8,128)S(1)}, f32[256,32]{0,1:T(8,128)S(1)}, u32[]{:S(2)}, u32[]{:S(2)}) collective-permute-start(f32[256,32]{0,1:T(8,128)S(1)} %add.383), channel_id=1, source_target_pairs={{0,256},{128,384},{256,0},{384,128},{1,257},{129,385},{257,1},{385... | collective-permute-start | bytes 98312 | tf_op jit(solution)/shard_map/ppermute | solution.py:25
  442.2 3.0 collective-permute-start.58
  445.9 3.2 collective-permute-done.58
  449.1 3.5 collective-permute-start.59
  455.3 7.7 %all-to-all-start.5 = ((f32[16,1,2]{2,1,0:T(1,128)}), f32[16,1,2]{2,1,0:T(1,128)S(1)}, u32[]{:S(2)}, u32[]{:S(2)}) async-start(f32[16,1,2]{2,1,0:T(1,128)} %broadcast_in_dim.16), calls=%async_computation.5 | async-start | bytes 16384 | tf_op jit(solution)/shard_map/all_to_all | solution.py:35
  463.0 7.2 %all-to-all-done.5 = f32[16,1,2]{2,1,0:T(1,128)S(1)} async-done(((f32[16,1,2]{2,1,0:T(1,128)}), f32[16,1,2]{2,1,0:T(1,128)S(1)}, u32[]{:S(2)}, u32[]{:S(2)}) %all-to-all-start.5) | async-done | bytes 160 | tf_op jit(solution)/shard_map/all_to_all | solution.py:35
  472.9 10.6 %all-to-all-start.6 = ((f32[32,1,2]{2,1,0:T(1,128)}), f32[32,1,2]{2,1,0:T(1,128)S(1)}, u32[]{:S(2)}, u32[]{:S(2)}) async-start(f32[32,1,2]{2,1,0:T(1,128)} %broadcast_in_dim.17), calls=%async_computation.6 | async-start | bytes 32768 | tf_op jit(solution)/shard_map/all_to_all | solution.py:35
  484.1 8.6 %all-to-all-done.6 = f32[32,1,2]{2,1,0:T(1,128)S(1)} async-done(((f32[32,1,2]{2,1,0:T(1,128)}), f32[32,1,2]{2,1,0:T(1,128)S(1)}, u32[]{:S(2)}, u32[]{:S(2)}) %all-to-all-start.6) | async-done | bytes 288 | tf_op jit(solution)/shard_map/all_to_all | solution.py:35
  (224 shorter events, 137.3 us)
Async XLA Ops:
  9.1 41.0 %all-to-all-start = ((f32[4,1,65536]{2,1,0:T(1,128)}), f32[4,1,65536]{2,1,0:T(1,128)S(1)}, u32[]{:S(2)}, u32[]{:S(2)}) async-start(f32[4,1,65536]{2,1,0:T(1,128)} %reshape.84), calls=%async_computation | async-start | bytes 2097152 | tf_op jit(solution)/shard_map/all_to_all | solution.py:58
  16.8 5.1 %collective-permute-start.2 = (f32[32,32]{0,1:T(8,128)S(1)}, f32[32,32]{0,1:T(8,128)S(1)}, u32[]{:S(2)}, u32[]{:S(2)}) collective-permute-start(f32[32,32]{0,1:T(8,128)S(1)} %copy.31), channel_id=1, source_target_pairs={{0,8},{8,0},{16,24},{24,16},{32,40},{40,32},{48,56},{56,48},{1,9},... | collective-permute-start | bytes 12296 | tf_op jit(solution)/shard_map/ppermute | solution.py:46
  22.0 10.5 %collective-permute-start.3 = (f32[64,32]{0,1:T(8,128)S(1)}, f32[64,32]{0,1:T(8,128)S(1)}, u32[]{:S(2)}, u32[]{:S(2)}) collective-permute-start(f32[64,32]{0,1:T(8,128)S(1)} %maximum_select_fusion.4), channel_id=1, source_target_pairs={{0,16},{8,24},{16,0},{24,8},{32,48},{40,56},{48,32},{56,40},{1,17}... | collective-permute-start | bytes 24584 | tf_op jit(solution)/shard_map/ppermute | solution.py:46
  27.9 15.7 %collective-permute-start = (f32[64,32]{0,1:T(8,128)S(1)}, f32[64,32]{0,1:T(8,128)S(1)}, u32[]{:S(2)}, u32[]{:S(2)}) collective-permute-start(f32[64,32]{0,1:T(8,128)S(1)} %broadcast_divide_fusion.5), channel_id=1, source_target_pairs={{0,128},{128,0},{256,384},{384,256},{1,129},{129,1},{257,385},{385... | collective-permute-start | bytes 24584 | tf_op jit(solution)/shard_map/ppermute | solution.py:46
  32.6 15.5 %collective-permute-start.4 = (f32[128,32]{0,1:T(8,128)S(1)}, f32[128,32]{0,1:T(8,128)S(1)}, u32[]{:S(2)}, u32[]{:S(2)}) collective-permute-start(f32[128,32]{0,1:T(8,128)S(1)} %maximum_select_fusion.5), channel_id=1, source_target_pairs={{0,32},{8,40},{16,48},{24,56},{32,0},{40,8},{48,16},{56,24},{1,33}... | collective-permute-start | bytes 49160 | tf_op jit(solution)/shard_map/ppermute | solution.py:46
  43.6 13.4 %collective-permute-start.1 = (f32[128,32]{0,1:T(8,128)S(1)}, f32[128,32]{0,1:T(8,128)S(1)}, u32[]{:S(2)}, u32[]{:S(2)}) collective-permute-start(f32[128,32]{0,1:T(8,128)S(1)} %maximum_select_fusion.3), channel_id=1, source_target_pairs={{0,256},{128,384},{256,0},{384,128},{1,257},{129,385},{257,1},{385... | collective-permute-start | bytes 49160 | tf_op jit(solution)/shard_map/ppermute | solution.py:46
  48.2 8.8 %collective-permute-start.5 = (f32[256,32]{0,1:T(8,128)S(1)}, f32[256,32]{0,1:T(8,128)S(1)}, u32[]{:S(2)}, u32[]{:S(2)}) collective-permute-start(f32[256,32]{0,1:T(8,128)S(1)} %maximum_select_fusion.2), channel_id=1, source_target_pairs={{0,64},{64,0},{1,65},{65,1},{2,66},{66,2},{3,67},{67,3},{4,68},{68... | collective-permute-start | bytes 98312 | tf_op jit(solution)/shard_map/ppermute | solution.py:46
  58.6 8.5 %collective-permute-start.11 = (f32[512,64]{0,1:T(8,128)S(1)}, f32[512,64]{0,1:T(8,128)S(1)}, u32[]{:S(2)}, u32[]{:S(2)}) collective-permute-start(f32[512,64]{0,1:T(8,128)S(1)} %pad_maximum_fusion.1), channel_id=1, source_target_pairs={{0,64},{64,0},{1,65},{65,1},{2,66},{66,2},{3,67},{67,3},{4,68},{68... | collective-permute-start | bytes 393224 | tf_op jit(solution)/shard_map/ppermute | solution.py:25
  63.1 8.1 %collective-permute-start.6 = (f32[256,32]{0,1:T(8,128)S(1)}, f32[256,32]{0,1:T(8,128)S(1)}, u32[]{:S(2)}, u32[]{:S(2)}) collective-permute-start(f32[256,32]{0,1:T(8,128)S(1)} %convolution_add_fusion.5), channel_id=1, source_target_pairs={{0,1},{1,0},{2,3},{3,2},{4,5},{5,4},{6,7},{7,6},{8,9},{9,8},{10,11... | collective-permute-start | bytes 98312 | tf_op jit(solution)/shard_map/ppermute | solution.py:25
  67.2 24.4 %collective-permute-start.12 = (f32[512,64]{0,1:T(8,128)S(1)}, f32[512,64]{0,1:T(8,128)S(1)}, u32[]{:S(2)}, u32[]{:S(2)}) collective-permute-start(f32[512,64]{0,1:T(8,128)S(1)} %fusion.41), channel_id=1, source_target_pairs={{0,8},{8,0},{16,24},{24,16},{32,40},{40,32},{48,56},{56,48},{1,9},... | collective-permute-start | bytes 393224 | tf_op jit(solution)/shard_map/ppermute | solution.py:25
  71.2 4.7 collective-permute-start.7
  75.9 6.2 %collective-permute-start.8 = (f32[256,32]{0,1:T(8,128)S(1)}, f32[256,32]{0,1:T(8,128)S(1)}, u32[]{:S(2)}, u32[]{:S(2)}) collective-permute-start(f32[256,32]{0,1:T(8,128)S(1)} %add.312), channel_id=1, source_target_pairs={{0,4},{2,6},{4,0},{6,2},{1,5},{3,7},{5,1},{7,3},{8,12},{10,14},{12... | collective-permute-start | bytes 98312 | tf_op jit(solution)/shard_map/ppermute | solution.py:25
  82.1 5.7 %collective-permute-start.9 = (f32[256,32]{0,1:T(8,128)S(1)}, f32[256,32]{0,1:T(8,128)S(1)}, u32[]{:S(2)}, u32[]{:S(2)}) collective-permute-start(f32[256,32]{0,1:T(8,128)S(1)} %add.313), channel_id=1, source_target_pairs={{0,128},{128,0},{256,384},{384,256},{1,129},{129,1},{257,385},{385... | collective-permute-start | bytes 98312 | tf_op jit(solution)/shard_map/ppermute | solution.py:25
  87.8 9.7 %collective-permute-start.10 = (f32[256,32]{0,1:T(8,128)S(1)}, f32[256,32]{0,1:T(8,128)S(1)}, u32[]{:S(2)}, u32[]{:S(2)}) collective-permute-start(f32[256,32]{0,1:T(8,128)S(1)} %add.314), channel_id=1, source_target_pairs={{0,256},{128,384},{256,0},{384,128},{1,257},{129,385},{257,1},{385... | collective-permute-start | bytes 98312 | tf_op jit(solution)/shard_map/ppermute | solution.py:25
  91.6 9.6 %collective-permute-start.13 = (f32[512,64]{0,1:T(8,128)S(1)}, f32[512,64]{0,1:T(8,128)S(1)}, u32[]{:S(2)}, u32[]{:S(2)}) collective-permute-start(f32[512,64]{0,1:T(8,128)S(1)} %add.317), channel_id=1, source_target_pairs={{0,16},{8,24},{16,0},{24,8},{32,48},{40,56},{48,32},{56,40},{1,17}... | collective-permute-start | bytes 393224 | tf_op jit(solution)/shard_map/ppermute | solution.py:25
  101.2 11.0 %collective-permute-start.14 = (f32[512,64]{0,1:T(8,128)S(1)}, f32[512,64]{0,1:T(8,128)S(1)}, u32[]{:S(2)}, u32[]{:S(2)}) collective-permute-start(f32[512,64]{0,1:T(8,128)S(1)} %add.318), channel_id=1, source_target_pairs={{0,32},{8,40},{16,48},{24,56},{32,0},{40,8},{48,16},{56,24},{1,33}... | collective-permute-start | bytes 393224 | tf_op jit(solution)/shard_map/ppermute | solution.py:25
  115.1 13.3 %collective-permute-start.20 = (f32[512,64]{0,1:T(8,128)S(1)}, f32[512,64]{0,1:T(8,128)S(1)}, u32[]{:S(2)}, u32[]{:S(2)}) collective-permute-start(f32[512,64]{0,1:T(8,128)S(1)} %pad_maximum_fusion.2), channel_id=1, source_target_pairs={{0,64},{64,0},{1,65},{65,1},{2,66},{66,2},{3,67},{67,3},{4,68},{68... | collective-permute-start | bytes 393224 | tf_op jit(solution)/shard_map/ppermute | solution.py:25
  118.5 11.8 %collective-permute-start.15 = (f32[256,32]{0,1:T(8,128)S(1)}, f32[256,32]{0,1:T(8,128)S(1)}, u32[]{:S(2)}, u32[]{:S(2)}) collective-permute-start(f32[256,32]{0,1:T(8,128)S(1)} %convolution_add_fusion.4), channel_id=1, source_target_pairs={{0,1},{1,0},{2,3},{3,2},{4,5},{5,4},{6,7},{7,6},{8,9},{9,8},{10,11... | collective-permute-start | bytes 98312 | tf_op jit(solution)/shard_map/ppermute | solution.py:25
  128.4 24.0 %collective-permute-start.21 = (f32[512,64]{0,1:T(8,128)S(1)}, f32[512,64]{0,1:T(8,128)S(1)}, u32[]{:S(2)}, u32[]{:S(2)}) collective-permute-start(f32[512,64]{0,1:T(8,128)S(1)} %fusion.40), channel_id=1, source_target_pairs={{0,8},{8,0},{16,24},{24,16},{32,40},{40,32},{48,56},{56,48},{1,9},... | collective-permute-start | bytes 393224 | tf_op jit(solution)/shard_map/ppermute | solution.py:25
  130.3 5.0 collective-permute-start.16
  135.3 6.2 %collective-permute-start.17 = (f32[256,32]{0,1:T(8,128)S(1)}, f32[256,32]{0,1:T(8,128)S(1)}, u32[]{:S(2)}, u32[]{:S(2)}) collective-permute-start(f32[256,32]{0,1:T(8,128)S(1)} %add.323), channel_id=1, source_target_pairs={{0,4},{2,6},{4,0},{6,2},{1,5},{3,7},{5,1},{7,3},{8,12},{10,14},{12... | collective-permute-start | bytes 98312 | tf_op jit(solution)/shard_map/ppermute | solution.py:25
  141.5 5.5 %collective-permute-start.18 = (f32[256,32]{0,1:T(8,128)S(1)}, f32[256,32]{0,1:T(8,128)S(1)}, u32[]{:S(2)}, u32[]{:S(2)}) collective-permute-start(f32[256,32]{0,1:T(8,128)S(1)} %add.324), channel_id=1, source_target_pairs={{0,128},{128,0},{256,384},{384,256},{1,129},{129,1},{257,385},{385... | collective-permute-start | bytes 98312 | tf_op jit(solution)/shard_map/ppermute | solution.py:25
  147.0 9.7 %collective-permute-start.19 = (f32[256,32]{0,1:T(8,128)S(1)}, f32[256,32]{0,1:T(8,128)S(1)}, u32[]{:S(2)}, u32[]{:S(2)}) collective-permute-start(f32[256,32]{0,1:T(8,128)S(1)} %add.325), channel_id=1, source_target_pairs={{0,256},{128,384},{256,0},{384,128},{1,257},{129,385},{257,1},{385... | collective-permute-start | bytes 98312 | tf_op jit(solution)/shard_map/ppermute | solution.py:25
  152.4 8.0 %collective-permute-start.22 = (f32[512,64]{0,1:T(8,128)S(1)}, f32[512,64]{0,1:T(8,128)S(1)}, u32[]{:S(2)}, u32[]{:S(2)}) collective-permute-start(f32[512,64]{0,1:T(8,128)S(1)} %add.329), channel_id=1, source_target_pairs={{0,16},{8,24},{16,0},{24,8},{32,48},{40,56},{48,32},{56,40},{1,17}... | collective-permute-start | bytes 393224 | tf_op jit(solution)/shard_map/ppermute | solution.py:25
  160.5 20.2 %collective-permute-start.23 = (f32[512,64]{0,1:T(8,128)S(1)}, f32[512,64]{0,1:T(8,128)S(1)}, u32[]{:S(2)}, u32[]{:S(2)}) collective-permute-start(f32[512,64]{0,1:T(8,128)S(1)} %add.330), channel_id=1, source_target_pairs={{0,32},{8,40},{16,48},{24,56},{32,0},{40,8},{48,16},{56,24},{1,33}... | collective-permute-start | bytes 393224 | tf_op jit(solution)/shard_map/ppermute | solution.py:25
  183.3 24.2 %all-to-all-start.2 = ((f32[32,1,2]{2,1,0:T(1,128)}), f32[32,1,2]{2,1,0:T(1,128)S(1)}, u32[]{:S(2)}, u32[]{:S(2)}) async-start(f32[32,1,2]{2,1,0:T(1,128)} %broadcast_in_dim.13), calls=%async_computation.2 | async-start | bytes 32768 | tf_op jit(solution)/shard_map/all_to_all | solution.py:35
  213.0 6.2 %collective-permute-start.29 = (f32[512,64]{0,1:T(8,128)S(1)}, f32[512,64]{0,1:T(8,128)S(1)}, u32[]{:S(2)}, u32[]{:S(2)}) collective-permute-start(f32[512,64]{0,1:T(8,128)S(1)} %pad_maximum_fusion.3), channel_id=1, source_target_pairs={{0,64},{64,0},{1,65},{65,1},{2,66},{66,2},{3,67},{67,3},{4,68},{68... | collective-permute-start | bytes 393224 | tf_op jit(solution)/shard_map/ppermute | solution.py:25
  215.8 5.7 %collective-permute-start.24 = (f32[256,32]{0,1:T(8,128)S(1)}, f32[256,32]{0,1:T(8,128)S(1)}, u32[]{:S(2)}, u32[]{:S(2)}) collective-permute-start(f32[256,32]{0,1:T(8,128)S(1)} %convolution_add_fusion.3), channel_id=1, source_target_pairs={{0,1},{1,0},{2,3},{3,2},{4,5},{5,4},{6,7},{7,6},{8,9},{9,8},{10,11... | collective-permute-start | bytes 98312 | tf_op jit(solution)/shard_map/ppermute | solution.py:25
  219.2 21.2 %collective-permute-start.30 = (f32[512,64]{0,1:T(8,128)S(1)}, f32[512,64]{0,1:T(8,128)S(1)}, u32[]{:S(2)}, u32[]{:S(2)}) collective-permute-start(f32[512,64]{0,1:T(8,128)S(1)} %fusion.39), channel_id=1, source_target_pairs={{0,8},{8,0},{16,24},{24,16},{32,40},{40,32},{48,56},{56,48},{1,9},... | collective-permute-start | bytes 393224 | tf_op jit(solution)/shard_map/ppermute | solution.py:25
  221.5 5.0 collective-permute-start.25
  226.4 6.2 %collective-permute-start.26 = (f32[256,32]{0,1:T(8,128)S(1)}, f32[256,32]{0,1:T(8,128)S(1)}, u32[]{:S(2)}, u32[]{:S(2)}) collective-permute-start(f32[256,32]{0,1:T(8,128)S(1)} %add.341), channel_id=1, source_target_pairs={{0,4},{2,6},{4,0},{6,2},{1,5},{3,7},{5,1},{7,3},{8,12},{10,14},{12... | collective-permute-start | bytes 98312 | tf_op jit(solution)/shard_map/ppermute | solution.py:25
  232.6 5.5 %collective-permute-start.27 = (f32[256,32]{0,1:T(8,128)S(1)}, f32[256,32]{0,1:T(8,128)S(1)}, u32[]{:S(2)}, u32[]{:S(2)}) collective-permute-start(f32[256,32]{0,1:T(8,128)S(1)} %add.342), channel_id=1, source_target_pairs={{0,128},{128,0},{256,384},{384,256},{1,129},{129,1},{257,385},{385... | collective-permute-start | bytes 98312 | tf_op jit(solution)/shard_map/ppermute | solution.py:25
  238.1 8.7 %collective-permute-start.28 = (f32[256,32]{0,1:T(8,128)S(1)}, f32[256,32]{0,1:T(8,128)S(1)}, u32[]{:S(2)}, u32[]{:S(2)}) collective-permute-start(f32[256,32]{0,1:T(8,128)S(1)} %add.343), channel_id=1, source_target_pairs={{0,256},{128,384},{256,0},{384,128},{1,257},{129,385},{257,1},{385... | collective-permute-start | bytes 98312 | tf_op jit(solution)/shard_map/ppermute | solution.py:25
  240.4 8.0 %collective-permute-start.31 = (f32[512,64]{0,1:T(8,128)S(1)}, f32[512,64]{0,1:T(8,128)S(1)}, u32[]{:S(2)}, u32[]{:S(2)}) collective-permute-start(f32[512,64]{0,1:T(8,128)S(1)} %add.346), channel_id=1, source_target_pairs={{0,16},{8,24},{16,0},{24,8},{32,48},{40,56},{48,32},{56,40},{1,17}... | collective-permute-start | bytes 393224 | tf_op jit(solution)/shard_map/ppermute | solution.py:25
  248.5 9.7 %collective-permute-start.32 = (f32[512,64]{0,1:T(8,128)S(1)}, f32[512,64]{0,1:T(8,128)S(1)}, u32[]{:S(2)}, u32[]{:S(2)}) collective-permute-start(f32[512,64]{0,1:T(8,128)S(1)} %add.347), channel_id=1, source_target_pairs={{0,32},{8,40},{16,48},{24,56},{32,0},{40,8},{48,16},{56,24},{1,33}... | collective-permute-start | bytes 393224 | tf_op jit(solution)/shard_map/ppermute | solution.py:25
  261.0 13.6 %collective-permute-start.38 = (f32[512,64]{0,1:T(8,128)S(1)}, f32[512,64]{0,1:T(8,128)S(1)}, u32[]{:S(2)}, u32[]{:S(2)}) collective-permute-start(f32[512,64]{0,1:T(8,128)S(1)} %pad_maximum_fusion.4), channel_id=1, source_target_pairs={{0,64},{64,0},{1,65},{65,1},{2,66},{66,2},{3,67},{67,3},{4,68},{68... | collective-permute-start | bytes 393224 | tf_op jit(solution)/shard_map/ppermute | solution.py:25
  264.4 12.2 %collective-permute-start.33 = (f32[256,32]{0,1:T(8,128)S(1)}, f32[256,32]{0,1:T(8,128)S(1)}, u32[]{:S(2)}, u32[]{:S(2)}) collective-permute-start(f32[256,32]{0,1:T(8,128)S(1)} %convolution_add_fusion.2), channel_id=1, source_target_pairs={{0,1},{1,0},{2,3},{3,2},{4,5},{5,4},{6,7},{7,6},{8,9},{9,8},{10,11... | collective-permute-start | bytes 98312 | tf_op jit(solution)/shard_map/ppermute | solution.py:25
  274.7 25.2 %collective-permute-start.39 = (f32[512,64]{0,1:T(8,128)S(1)}, f32[512,64]{0,1:T(8,128)S(1)}, u32[]{:S(2)}, u32[]{:S(2)}) collective-permute-start(f32[512,64]{0,1:T(8,128)S(1)} %fusion.38), channel_id=1, source_target_pairs={{0,8},{8,0},{16,24},{24,16},{32,40},{40,32},{48,56},{56,48},{1,9},... | collective-permute-start | bytes 393224 | tf_op jit(solution)/shard_map/ppermute | solution.py:25
  276.6 4.7 collective-permute-start.34
  281.3 6.2 %collective-permute-start.35 = (f32[256,32]{0,1:T(8,128)S(1)}, f32[256,32]{0,1:T(8,128)S(1)}, u32[]{:S(2)}, u32[]{:S(2)}) collective-permute-start(f32[256,32]{0,1:T(8,128)S(1)} %add.352), channel_id=1, source_target_pairs={{0,4},{2,6},{4,0},{6,2},{1,5},{3,7},{5,1},{7,3},{8,12},{10,14},{12... | collective-permute-start | bytes 98312 | tf_op jit(solution)/shard_map/ppermute | solution.py:25
  287.5 5.5 %collective-permute-start.36 = (f32[256,32]{0,1:T(8,128)S(1)}, f32[256,32]{0,1:T(8,128)S(1)}, u32[]{:S(2)}, u32[]{:S(2)}) collective-permute-start(f32[256,32]{0,1:T(8,128)S(1)} %add.353), channel_id=1, source_target_pairs={{0,128},{128,0},{256,384},{384,256},{1,129},{129,1},{257,385},{385... | collective-permute-start | bytes 98312 | tf_op jit(solution)/shard_map/ppermute | solution.py:25
  293.0 10.0 %collective-permute-start.37 = (f32[256,32]{0,1:T(8,128)S(1)}, f32[256,32]{0,1:T(8,128)S(1)}, u32[]{:S(2)}, u32[]{:S(2)}) collective-permute-start(f32[256,32]{0,1:T(8,128)S(1)} %add.354), channel_id=1, source_target_pairs={{0,256},{128,384},{256,0},{384,128},{1,257},{129,385},{257,1},{385... | collective-permute-start | bytes 98312 | tf_op jit(solution)/shard_map/ppermute | solution.py:25
  300.0 6.9 %collective-permute-start.40 = (f32[512,64]{0,1:T(8,128)S(1)}, f32[512,64]{0,1:T(8,128)S(1)}, u32[]{:S(2)}, u32[]{:S(2)}) collective-permute-start(f32[512,64]{0,1:T(8,128)S(1)} %add.358), channel_id=1, source_target_pairs={{0,16},{8,24},{16,0},{24,8},{32,48},{40,56},{48,32},{56,40},{1,17}... | collective-permute-start | bytes 393224 | tf_op jit(solution)/shard_map/ppermute | solution.py:25
  306.9 20.3 %collective-permute-start.41 = (f32[512,64]{0,1:T(8,128)S(1)}, f32[512,64]{0,1:T(8,128)S(1)}, u32[]{:S(2)}, u32[]{:S(2)}) collective-permute-start(f32[512,64]{0,1:T(8,128)S(1)} %add.359), channel_id=1, source_target_pairs={{0,32},{8,40},{16,48},{24,56},{32,0},{40,8},{48,16},{56,24},{1,33}... | collective-permute-start | bytes 393224 | tf_op jit(solution)/shard_map/ppermute | solution.py:25
  329.9 19.8 %all-to-all-start.4 = ((f32[32,1,2]{2,1,0:T(1,128)}), f32[32,1,2]{2,1,0:T(1,128)S(1)}, u32[]{:S(2)}, u32[]{:S(2)}) async-start(f32[32,1,2]{2,1,0:T(1,128)} %broadcast_in_dim.15), calls=%async_computation.4 | async-start | bytes 32768 | tf_op jit(solution)/shard_map/all_to_all | solution.py:35
  355.2 6.2 %collective-permute-start.47 = (f32[512,64]{0,1:T(8,128)S(1)}, f32[512,64]{0,1:T(8,128)S(1)}, u32[]{:S(2)}, u32[]{:S(2)}) collective-permute-start(f32[512,64]{0,1:T(8,128)S(1)} %pad_maximum_fusion.5), channel_id=1, source_target_pairs={{0,64},{64,0},{1,65},{65,1},{2,66},{66,2},{3,67},{67,3},{4,68},{68... | collective-permute-start | bytes 393224 | tf_op jit(solution)/shard_map/ppermute | solution.py:25
  358.2 5.4 %collective-permute-start.42 = (f32[256,32]{0,1:T(8,128)S(1)}, f32[256,32]{0,1:T(8,128)S(1)}, u32[]{:S(2)}, u32[]{:S(2)}) collective-permute-start(f32[256,32]{0,1:T(8,128)S(1)} %convolution_add_fusion.1), channel_id=1, source_target_pairs={{0,1},{1,0},{2,3},{3,2},{4,5},{5,4},{6,7},{7,6},{8,9},{9,8},{10,11... | collective-permute-start | bytes 98312 | tf_op jit(solution)/shard_map/ppermute | solution.py:25
  361.5 21.2 %collective-permute-start.48 = (f32[512,64]{0,1:T(8,128)S(1)}, f32[512,64]{0,1:T(8,128)S(1)}, u32[]{:S(2)}, u32[]{:S(2)}) collective-permute-start(f32[512,64]{0,1:T(8,128)S(1)} %fusion.37), channel_id=1, source_target_pairs={{0,8},{8,0},{16,24},{24,16},{32,40},{40,32},{48,56},{56,48},{1,9},... | collective-permute-start | bytes 393224 | tf_op jit(solution)/shard_map/ppermute | solution.py:25
  363.7 5.0 collective-permute-start.43
  368.7 6.2 %collective-permute-start.44 = (f32[256,32]{0,1:T(8,128)S(1)}, f32[256,32]{0,1:T(8,128)S(1)}, u32[]{:S(2)}, u32[]{:S(2)}) collective-permute-start(f32[256,32]{0,1:T(8,128)S(1)} %add.370), channel_id=1, source_target_pairs={{0,4},{2,6},{4,0},{6,2},{1,5},{3,7},{5,1},{7,3},{8,12},{10,14},{12... | collective-permute-start | bytes 98312 | tf_op jit(solution)/shard_map/ppermute | solution.py:25
  374.8 5.5 %collective-permute-start.45 = (f32[256,32]{0,1:T(8,128)S(1)}, f32[256,32]{0,1:T(8,128)S(1)}, u32[]{:S(2)}, u32[]{:S(2)}) collective-permute-start(f32[256,32]{0,1:T(8,128)S(1)} %add.371), channel_id=1, source_target_pairs={{0,128},{128,0},{256,384},{384,256},{1,129},{129,1},{257,385},{385... | collective-permute-start | bytes 98312 | tf_op jit(solution)/shard_map/ppermute | solution.py:25
  380.4 8.6 %collective-permute-start.46 = (f32[256,32]{0,1:T(8,128)S(1)}, f32[256,32]{0,1:T(8,128)S(1)}, u32[]{:S(2)}, u32[]{:S(2)}) collective-permute-start(f32[256,32]{0,1:T(8,128)S(1)} %add.372), channel_id=1, source_target_pairs={{0,256},{128,384},{256,0},{384,128},{1,257},{129,385},{257,1},{385... | collective-permute-start | bytes 98312 | tf_op jit(solution)/shard_map/ppermute | solution.py:25
  382.7 8.0 %collective-permute-start.49 = (f32[512,64]{0,1:T(8,128)S(1)}, f32[512,64]{0,1:T(8,128)S(1)}, u32[]{:S(2)}, u32[]{:S(2)}) collective-permute-start(f32[512,64]{0,1:T(8,128)S(1)} %add.375), channel_id=1, source_target_pairs={{0,16},{8,24},{16,0},{24,8},{32,48},{40,56},{48,32},{56,40},{1,17}... | collective-permute-start | bytes 393224 | tf_op jit(solution)/shard_map/ppermute | solution.py:25
  390.8 9.7 %collective-permute-start.50 = (f32[512,64]{0,1:T(8,128)S(1)}, f32[512,64]{0,1:T(8,128)S(1)}, u32[]{:S(2)}, u32[]{:S(2)}) collective-permute-start(f32[512,64]{0,1:T(8,128)S(1)} %add.376), channel_id=1, source_target_pairs={{0,32},{8,40},{16,48},{24,56},{32,0},{40,8},{48,16},{56,24},{1,33}... | collective-permute-start | bytes 393224 | tf_op jit(solution)/shard_map/ppermute | solution.py:25
  403.3 13.6 %collective-permute-start.56 = (f32[512,64]{0,1:T(8,128)S(1)}, f32[512,64]{0,1:T(8,128)S(1)}, u32[]{:S(2)}, u32[]{:S(2)}) collective-permute-start(f32[512,64]{0,1:T(8,128)S(1)} %pad_maximum_fusion.6), channel_id=1, source_target_pairs={{0,64},{64,0},{1,65},{65,1},{2,66},{66,2},{3,67},{67,3},{4,68},{68... | collective-permute-start | bytes 393224 | tf_op jit(solution)/shard_map/ppermute | solution.py:25
  407.1 11.8 %collective-permute-start.51 = (f32[256,32]{0,1:T(8,128)S(1)}, f32[256,32]{0,1:T(8,128)S(1)}, u32[]{:S(2)}, u32[]{:S(2)}) collective-permute-start(f32[256,32]{0,1:T(8,128)S(1)} %convolution_add_fusion), channel_id=1, source_target_pairs={{0,1},{1,0},{2,3},{3,2},{4,5},{5,4},{6,7},{7,6},{8,9},{9,8},{10,11... | collective-permute-start | bytes 98312 | tf_op jit(solution)/shard_map/ppermute | solution.py:25
  417.0 25.2 %collective-permute-start.57 = (f32[512,64]{0,1:T(8,128)S(1)}, f32[512,64]{0,1:T(8,128)S(1)}, u32[]{:S(2)}, u32[]{:S(2)}) collective-permute-start(f32[512,64]{0,1:T(8,128)S(1)} %fusion.36), channel_id=1, source_target_pairs={{0,8},{8,0},{16,24},{24,16},{32,40},{40,32},{48,56},{56,48},{1,9},... | collective-permute-start | bytes 393224 | tf_op jit(solution)/shard_map/ppermute | solution.py:25
  423.6 6.2 %collective-permute-start.53 = (f32[256,32]{0,1:T(8,128)S(1)}, f32[256,32]{0,1:T(8,128)S(1)}, u32[]{:S(2)}, u32[]{:S(2)}) collective-permute-start(f32[256,32]{0,1:T(8,128)S(1)} %add.381), channel_id=1, source_target_pairs={{0,4},{2,6},{4,0},{6,2},{1,5},{3,7},{5,1},{7,3},{8,12},{10,14},{12... | collective-permute-start | bytes 98312 | tf_op jit(solution)/shard_map/ppermute | solution.py:25
  429.7 5.5 %collective-permute-start.54 = (f32[256,32]{0,1:T(8,128)S(1)}, f32[256,32]{0,1:T(8,128)S(1)}, u32[]{:S(2)}, u32[]{:S(2)}) collective-permute-start(f32[256,32]{0,1:T(8,128)S(1)} %add.382), channel_id=1, source_target_pairs={{0,128},{128,0},{256,384},{384,256},{1,129},{129,1},{257,385},{385... | collective-permute-start | bytes 98312 | tf_op jit(solution)/shard_map/ppermute | solution.py:25
  435.3 10.0 %collective-permute-start.55 = (f32[256,32]{0,1:T(8,128)S(1)}, f32[256,32]{0,1:T(8,128)S(1)}, u32[]{:S(2)}, u32[]{:S(2)}) collective-permute-start(f32[256,32]{0,1:T(8,128)S(1)} %add.383), channel_id=1, source_target_pairs={{0,256},{128,384},{256,0},{384,128},{1,257},{129,385},{257,1},{385... | collective-permute-start | bytes 98312 | tf_op jit(solution)/shard_map/ppermute | solution.py:25
  442.2 6.9 %collective-permute-start.58 = (f32[512,64]{0,1:T(8,128)S(1)}, f32[512,64]{0,1:T(8,128)S(1)}, u32[]{:S(2)}, u32[]{:S(2)}) collective-permute-start(f32[512,64]{0,1:T(8,128)S(1)} %add.387), channel_id=1, source_target_pairs={{0,16},{8,24},{16,0},{24,8},{32,48},{40,56},{48,32},{56,40},{1,17}... | collective-permute-start | bytes 393224 | tf_op jit(solution)/shard_map/ppermute | solution.py:25
  449.1 21.1 %collective-permute-start.59 = (f32[512,64]{0,1:T(8,128)S(1)}, f32[512,64]{0,1:T(8,128)S(1)}, u32[]{:S(2)}, u32[]{:S(2)}) collective-permute-start(f32[512,64]{0,1:T(8,128)S(1)} %add.388), channel_id=1, source_target_pairs={{0,32},{8,40},{16,48},{24,56},{32,0},{40,8},{48,16},{56,24},{1,33}... | collective-permute-start | bytes 393224 | tf_op jit(solution)/shard_map/ppermute | solution.py:25
  455.3 14.9 %all-to-all-start.5 = ((f32[16,1,2]{2,1,0:T(1,128)}), f32[16,1,2]{2,1,0:T(1,128)S(1)}, u32[]{:S(2)}, u32[]{:S(2)}) async-start(f32[16,1,2]{2,1,0:T(1,128)} %broadcast_in_dim.16), calls=%async_computation.5 | async-start | bytes 16384 | tf_op jit(solution)/shard_map/all_to_all | solution.py:35
  472.9 19.8 %all-to-all-start.6 = ((f32[32,1,2]{2,1,0:T(1,128)}), f32[32,1,2]{2,1,0:T(1,128)S(1)}, u32[]{:S(2)}, u32[]{:S(2)}) async-start(f32[32,1,2]{2,1,0:T(1,128)} %broadcast_in_dim.17), calls=%async_computation.6 | async-start | bytes 32768 | tf_op jit(solution)/shard_map/all_to_all | solution.py:35
  (3 other events, 30.3 us)

commit v4 on v3

--- a/solution.py
+++ b/solution.py
@@ -84,7 +84,8 @@
         f_next = f_state * c_total / (f_state * c_total + (1.0 - f_state) * d_total)
         return (q_next, f_next)
 
-    for step in range(STEPS):
+    def one_step(step, state):
+        q_zero, f_zero = state
         q_one, f_one = em_map(q_zero, f_zero)
         q_two, f_two = em_map(q_one, f_one)
         rq = q_one - q_zero
@@ -99,6 +100,9 @@
         q_ext = jnp.clip(q_zero - 2.0 * alpha * rq + alpha * alpha * vq, clip_low, 1.0 - clip_low)
         q_zero = q_ext / jnp.sum(q_ext, axis=1, keepdims=True)
         f_zero = jnp.clip(f_zero - 2.0 * alpha * rf + alpha * alpha * vf, clip_low, 1.0 - clip_low)
+        return (q_zero, f_zero)
+
+    q_zero, f_zero = lax.fori_loop(0, STEPS, one_step, (q_zero, f_zero))
     q_final = lax.dynamic_slice_in_dim(q_zero, lax.axis_index("yh") * own_rows, own_rows, 0)
     f_index = lax.axis_index("yl") * lax.axis_size("z") + lax.axis_index("z")
     f_final = lax.dynamic_slice_in_dim(f_zero, f_index * own_snps, own_snps, 0)

time: 500 us -> 513 us (1.026)
  blocking collectives: 25.3 us -> 0 us
  starting transfers between devices: 281 us -> 298 us
  waiting for transfers between devices: 125 us -> 139 us
  loops' own time: 0 us -> 9.08 us
  between operations: 10 us -> 0.95 us
  local copies, waits for them, and re-layouts: 15.8 us -> 22.3 us
    all_to_all x2 -> x0, blocking collectives: 25.3 us -> none  [group_total(): gathered = lax.all_to_all(spread, axes, 0, 0, tiled=True)]
    all_to_all x4 -> x6, starting transfers between devices: 43.9 us -> 60 us  [group_total(): gathered = lax.all_to_all(spread, axes, 0, 0, tiled=True)]
    all_to_all x4 -> x6, waiting for transfers between devices: 33 us -> 47.3 us  [group_total(): gathered = lax.all_to_all(spread, axes, 0, 0, tiled=True)]
    another operation x0 -> x1, loops' own time: none -> 9.08 us  [per_device(): q_zero, f_zero = lax.fori_loop(0, STEPS, one_step, (q_zero, f_zero))]
    slice x1 -> x3, local copies, waits for them, and re-layouts: 0.07 us -> 5.46 us  [per_device(): hits, misses = (counts[0], counts[1])]
  transfers between devices with their start and end apart: 65 -> 67, of which waited for: 37 -> 39; matrix products, arithmetic and copies ran while one was open for 4% -> 4% of each run, Pallas kernels for 0% -> 0%
where the time goes in v4:
time: 513 us; the launch traced here: 510 us
  starting transfers between devices  298 us (58%)
  waiting for transfers between devices  139 us (27%)
  other arithmetic  23.7 us (5%)
  local copies, waits for them, and re-layouts  22.3 us (4%)
  matrix products  16.9 us (3%)
  loops' own time  9.08 us (2%)
    ppermute x54, starting transfers between devices, doubling_sum(): value = value + lax.ppermute(value, name, pairs)  201 us
    ppermute x54, waiting for transfers between devices, doubling_sum(): value = value + lax.ppermute(value, name, pairs)  85.1 us
    all_to_all x6, starting transfers between devices, group_total(): gathered = lax.all_to_all(spread, axes, 0, 0, tiled=True)  60 us
    all_to_all x6, waiting for transfers between devices, group_total(): gathered = lax.all_to_all(spread, axes, 0, 0, tiled=True)  47.3 us
    ppermute x6, starting transfers between devices, doubling_gather(): other = lax.ppermute(value, name, pairs)  29 us
  transfers between devices with their start and end apart: 67, of which 39 were waited for; matrix products, arithmetic and copies ran while one was open for 4% of the time, Pallas kernels for 0%

profile of v4, /device:TPU:1, one launch (start us, length us, event | category | flops | bytes accessed | tf_op | source)
XLA Modules:
  0.0 510.2 jit_solution(10332920983541094406)
XLA Ops:
  6.0 3.1 reshape.34
  9.1 7.6 %all-to-all-start.2 = ((f32[4,1,65536]{2,1,0:T(1,128)}), f32[4,1,65536]{2,1,0:T(1,128)S(1)}, u32[]{:S(2)}, u32[]{:S(2)}) async-start(f32[4,1,65536]{2,1,0:T(1,128)} %reshape.34), calls=%async_computation.2 | async-start | bytes 2097152 | tf_op jit(solution)/shard_map/all_to_all | solution.py:58
  16.8 4.0 collective-permute-start.20
  22.0 5.8 %collective-permute-start.21 = (f32[64,32]{0,1:T(8,128)S(1)}, f32[64,32]{0,1:T(8,128)S(1)}, u32[]{:S(2)}, u32[]{:S(2)}) collective-permute-start(f32[64,32]{0,1:T(8,128)S(1)} %maximum_select_fusion.4), channel_id=1, source_target_pairs={{0,16},{8,24},{16,0},{24,8},{32,48},{40,56},{48,32},{56,40},{1,17}... | collective-permute-start | bytes 24584 | tf_op jit(solution)/shard_map/ppermute | solution.py:46
  27.8 4.6 collective-permute-start.18
  32.6 8.2 %collective-permute-start.22 = (f32[128,32]{0,1:T(8,128)S(1)}, f32[128,32]{0,1:T(8,128)S(1)}, u32[]{:S(2)}, u32[]{:S(2)}) collective-permute-start(f32[128,32]{0,1:T(8,128)S(1)} %maximum_select_fusion.5), channel_id=1, source_target_pairs={{0,32},{8,40},{16,48},{24,56},{32,0},{40,8},{48,16},{56,24},{1,33}... | collective-permute-start | bytes 49160 | tf_op jit(solution)/shard_map/ppermute | solution.py:46
  43.6 4.5 collective-permute-start.19
  53.6 3.7 reduce.2
  64.4 444.4 %while.12 = (s32[]{:T(128)}, f32[256,32]{0,1:T(8,128)S(1)}, f32[512,32]{0,1:T(8,128)S(1)}, f32[256,512]{1,0:T(8,128)S(1)}, f32[256,512]{1,0:T(8,128)S(1)}, /*index=5*/s32[]{:T(128)}, f32[]{:T(128)}, f32[1]{0:T(128)}, f32[1]{0:T(128)}) while((s32[]{:T(128)}, f32[256,32]{0,1:T(8,128)S(1)}, f32[512,32]{0,1:T(8,128)S(1)}, ...), condition=%wide.region_11.12_spmd, body=%wide.region_1.11_spmd.sunk | while | flops 505994592 | bytes 22143180 | solution.py:105
  69.3 4.6 collective-permute-start
  73.9 4.0 collective-permute-start.6
  77.9 3.1 collective-permute-start.1
  82.6 4.6 collective-permute-start.2
  88.7 4.4 collective-permute-start.3
  94.4 3.6 collective-permute-start.4
  98.1 5.8 %collective-permute-start.7 = (f32[512,64]{0,1:T(8,128)S(1)}, f32[512,64]{0,1:T(8,128)S(1)}, u32[]{:S(2)}, u32[]{:S(2)}) collective-permute-start(f32[512,64]{0,1:T(8,128)S(1)} %add.205), channel_id=1, source_target_pairs={{0,16},{8,24},{16,0},{24,8},{32,48},{40,56},{48,32},{56,40},{1,17}... | collective-permute-start | bytes 393224 | tf_op jit(solution)/shard_map/while/body/eval_jaxpr/ppermute | solution.py:25
  103.9 4.0 collective-permute-done.7
  107.9 8.2 %collective-permute-start.8 = (f32[512,64]{0,1:T(8,128)S(1)}, f32[512,64]{0,1:T(8,128)S(1)}, u32[]{:S(2)}, u32[]{:S(2)}) collective-permute-start(f32[512,64]{0,1:T(8,128)S(1)} %add.206), channel_id=1, source_target_pairs={{0,32},{8,40},{16,48},{24,56},{32,0},{40,8},{48,16},{56,24},{1,33}... | collective-permute-start | bytes 393224 | tf_op jit(solution)/shard_map/while/body/eval_jaxpr/ppermute | solution.py:25
  116.7 3.2 collective-permute-done.8
  125.8 9.1 %collective-permute-start.9 = (f32[256,32]{0,1:T(8,128)S(1)}, f32[256,32]{0,1:T(8,128)S(1)}, u32[]{:S(2)}, u32[]{:S(2)}) collective-permute-start(f32[256,32]{0,1:T(8,128)S(1)} %convolution_add_fusion.5), channel_id=1, source_target_pairs={{0,1},{1,0},{2,3},{3,2},{4,5},{5,4},{6,7},{7,6},{8,9},{9,8},{10,11... | collective-permute-start | bytes 98312 | tf_op jit(solution)/shard_map/while/body/eval_jaxpr/ppermute | solution.py:25
  136.9 3.1 collective-permute-start.10
  141.6 4.6 collective-permute-start.11
  147.8 4.4 collective-permute-start.12
  153.4 5.6 %collective-permute-start.13 = (f32[256,32]{0,1:T(8,128)S(1)}, f32[256,32]{0,1:T(8,128)S(1)}, u32[]{:S(2)}, u32[]{:S(2)}) collective-permute-start(f32[256,32]{0,1:T(8,128)S(1)} %add.211), channel_id=1, source_target_pairs={{0,256},{128,384},{256,0},{384,128},{1,257},{129,385},{257,1},{385... | collective-permute-start | bytes 98312 | tf_op jit(solution)/shard_map/while/body/eval_jaxpr/ppermute | solution.py:25
  159.1 4.3 collective-permute-start.16
  163.5 4.0 collective-permute-done.16
  167.5 7.5 %collective-permute-start.17 = (f32[512,64]{0,1:T(8,128)S(1)}, f32[512,64]{0,1:T(8,128)S(1)}, u32[]{:S(2)}, u32[]{:S(2)}) collective-permute-start(f32[512,64]{0,1:T(8,128)S(1)} %add.213), channel_id=1, source_target_pairs={{0,32},{8,40},{16,48},{24,56},{32,0},{40,8},{48,16},{56,24},{1,33}... | collective-permute-start | bytes 393224 | tf_op jit(solution)/shard_map/while/body/eval_jaxpr/ppermute | solution.py:25
  177.7 4.7 all-to-all-start
  182.4 7.2 %all-to-all-done = f32[16,1,2]{2,1,0:T(1,128)S(1)} async-done(((f32[16,1,2]{2,1,0:T(1,128)}), f32[16,1,2]{2,1,0:T(1,128)S(1)}, u32[]{:S(2)}, u32[]{:S(2)}) %all-to-all-start) | async-done | bytes 160 | tf_op jit(solution)/shard_map/while/body/eval_jaxpr/all_to_all | solution.py:35
  192.3 18.8 %all-to-all-start.1 = ((f32[32,1,2]{2,1,0:T(1,128)}), f32[32,1,2]{2,1,0:T(1,128)S(1)}, u32[]{:S(2)}, u32[]{:S(2)}) async-start(f32[32,1,2]{2,1,0:T(1,128)} %broadcast_in_dim.7), calls=%async_computation.1 | async-start | bytes 32768 | tf_op jit(solution)/shard_map/while/body/eval_jaxpr/all_to_all | solution.py:35
  211.7 8.5 %all-to-all-done.1 = f32[32,1,2]{2,1,0:T(1,128)S(1)} async-done(((f32[32,1,2]{2,1,0:T(1,128)}), f32[32,1,2]{2,1,0:T(1,128)S(1)}, u32[]{:S(2)}, u32[]{:S(2)}) %all-to-all-start.1) | async-done | bytes 288 | tf_op jit(solution)/shard_map/while/body/eval_jaxpr/all_to_all | solution.py:35
  241.8 3.3 collective-permute-done.2
  247.3 3.3 collective-permute-done.3
  255.1 4.1 collective-permute-done.4
  264.5 6.1 %collective-permute-done.8 = f32[512,64]{0,1:T(8,128)S(1)} collective-permute-done((f32[512,64]{0,1:T(8,128)S(1)}, f32[512,64]{0,1:T(8,128)S(1)}, u32[]{:S(2)}, u32[]{:S(2)}) %collective-permute-start.8) | collective-permute-done | bytes 131104 | tf_op jit(solution)/shard_map/while/body/eval_jaxpr/ppermute | solution.py:25
  273.6 3.7 collective-permute-start.14
  277.9 9.2 %collective-permute-start.9 = (f32[256,32]{0,1:T(8,128)S(1)}, f32[256,32]{0,1:T(8,128)S(1)}, u32[]{:S(2)}, u32[]{:S(2)}) collective-permute-start(f32[256,32]{0,1:T(8,128)S(1)} %convolution_add_fusion.5), channel_id=1, source_target_pairs={{0,1},{1,0},{2,3},{3,2},{4,5},{5,4},{6,7},{7,6},{8,9},{9,8},{10,11... | collective-permute-start | bytes 98312 | tf_op jit(solution)/shard_map/while/body/eval_jaxpr/ppermute | solution.py:25
  296.5 3.4 collective-permute-done.11
  299.9 3.8 collective-permute-start.12
  305.5 6.9 %collective-permute-start.13 = (f32[256,32]{0,1:T(8,128)S(1)}, f32[256,32]{0,1:T(8,128)S(1)}, u32[]{:S(2)}, u32[]{:S(2)}) collective-permute-start(f32[256,32]{0,1:T(8,128)S(1)} %add.211), channel_id=1, source_target_pairs={{0,256},{128,384},{256,0},{384,128},{1,257},{129,385},{257,1},{385... | collective-permute-start | bytes 98312 | tf_op jit(solution)/shard_map/while/body/eval_jaxpr/ppermute | solution.py:25
  312.4 3.0 collective-permute-start.16
  315.5 3.9 collective-permute-done.16
  319.4 3.5 collective-permute-start.17
  325.5 7.8 %all-to-all-start = ((f32[16,1,2]{2,1,0:T(1,128)}), f32[16,1,2]{2,1,0:T(1,128)S(1)}, u32[]{:S(2)}, u32[]{:S(2)}) async-start(f32[16,1,2]{2,1,0:T(1,128)} %broadcast_in_dim.6), calls=%async_computation | async-start | bytes 16384 | tf_op jit(solution)/shard_map/while/body/eval_jaxpr/all_to_all | solution.py:35
  333.3 7.2 %all-to-all-done = f32[16,1,2]{2,1,0:T(1,128)S(1)} async-done(((f32[16,1,2]{2,1,0:T(1,128)}), f32[16,1,2]{2,1,0:T(1,128)S(1)}, u32[]{:S(2)}, u32[]{:S(2)}) %all-to-all-start) | async-done | bytes 160 | tf_op jit(solution)/shard_map/while/body/eval_jaxpr/all_to_all | solution.py:35
  343.2 10.5 %all-to-all-start.1 = ((f32[32,1,2]{2,1,0:T(1,128)}), f32[32,1,2]{2,1,0:T(1,128)S(1)}, u32[]{:S(2)}, u32[]{:S(2)}) async-start(f32[32,1,2]{2,1,0:T(1,128)} %broadcast_in_dim.7), calls=%async_computation.1 | async-start | bytes 32768 | tf_op jit(solution)/shard_map/while/body/eval_jaxpr/all_to_all | solution.py:35
  354.4 8.5 %all-to-all-done.1 = f32[32,1,2]{2,1,0:T(1,128)S(1)} async-done(((f32[32,1,2]{2,1,0:T(1,128)}), f32[32,1,2]{2,1,0:T(1,128)S(1)}, u32[]{:S(2)}, u32[]{:S(2)}) %all-to-all-start.1) | async-done | bytes 288 | tf_op jit(solution)/shard_map/while/body/eval_jaxpr/all_to_all | solution.py:35
  384.4 3.2 collective-permute-done.2
  389.9 3.3 collective-permute-done.3
  397.7 4.2 collective-permute-done.4
  403.6 2.9 collective-permute-start.8
  407.1 6.1 %collective-permute-done.8 = f32[512,64]{0,1:T(8,128)S(1)} collective-permute-done((f32[512,64]{0,1:T(8,128)S(1)}, f32[512,64]{0,1:T(8,128)S(1)}, u32[]{:S(2)}, u32[]{:S(2)}) %collective-permute-start.8) | collective-permute-done | bytes 131104 | tf_op jit(solution)/shard_map/while/body/eval_jaxpr/ppermute | solution.py:25
  416.2 3.7 collective-permute-start.14
  420.5 9.2 %collective-permute-start.9 = (f32[256,32]{0,1:T(8,128)S(1)}, f32[256,32]{0,1:T(8,128)S(1)}, u32[]{:S(2)}, u32[]{:S(2)}) collective-permute-start(f32[256,32]{0,1:T(8,128)S(1)} %convolution_add_fusion.5), channel_id=1, source_target_pairs={{0,1},{1,0},{2,3},{3,2},{4,5},{5,4},{6,7},{7,6},{8,9},{9,8},{10,11... | collective-permute-start | bytes 98312 | tf_op jit(solution)/shard_map/while/body/eval_jaxpr/ppermute | solution.py:25
  439.1 3.5 collective-permute-done.11
  442.6 3.8 collective-permute-start.12
  448.1 6.9 %collective-permute-start.13 = (f32[256,32]{0,1:T(8,128)S(1)}, f32[256,32]{0,1:T(8,128)S(1)}, u32[]{:S(2)}, u32[]{:S(2)}) collective-permute-start(f32[256,32]{0,1:T(8,128)S(1)} %add.211), channel_id=1, source_target_pairs={{0,256},{128,384},{256,0},{384,128},{1,257},{129,385},{257,1},{385... | collective-permute-start | bytes 98312 | tf_op jit(solution)/shard_map/while/body/eval_jaxpr/ppermute | solution.py:25
  455.0 3.1 collective-permute-start.16
  458.2 3.8 collective-permute-done.16
  462.0 3.6 collective-permute-start.17
  468.1 7.7 %all-to-all-start = ((f32[16,1,2]{2,1,0:T(1,128)}), f32[16,1,2]{2,1,0:T(1,128)S(1)}, u32[]{:S(2)}, u32[]{:S(2)}) async-start(f32[16,1,2]{2,1,0:T(1,128)} %broadcast_in_dim.6), calls=%async_computation | async-start | bytes 16384 | tf_op jit(solution)/shard_map/while/body/eval_jaxpr/all_to_all | solution.py:35
  475.9 7.2 %all-to-all-done = f32[16,1,2]{2,1,0:T(1,128)S(1)} async-done(((f32[16,1,2]{2,1,0:T(1,128)}), f32[16,1,2]{2,1,0:T(1,128)S(1)}, u32[]{:S(2)}, u32[]{:S(2)}) %all-to-all-start) | async-done | bytes 160 | tf_op jit(solution)/shard_map/while/body/eval_jaxpr/all_to_all | solution.py:35
  485.8 10.5 %all-to-all-start.1 = ((f32[32,1,2]{2,1,0:T(1,128)}), f32[32,1,2]{2,1,0:T(1,128)S(1)}, u32[]{:S(2)}, u32[]{:S(2)}) async-start(f32[32,1,2]{2,1,0:T(1,128)} %broadcast_in_dim.7), calls=%async_computation.1 | async-start | bytes 32768 | tf_op jit(solution)/shard_map/while/body/eval_jaxpr/all_to_all | solution.py:35
  497.0 8.5 %all-to-all-done.1 = f32[32,1,2]{2,1,0:T(1,128)S(1)} async-done(((f32[32,1,2]{2,1,0:T(1,128)}), f32[32,1,2]{2,1,0:T(1,128)S(1)}, u32[]{:S(2)}, u32[]{:S(2)}) %all-to-all-start.1) | async-done | bytes 288 | tf_op jit(solution)/shard_map/while/body/eval_jaxpr/all_to_all | solution.py:35
  (233 shorter events, 151.5 us)
Async XLA Ops:
  9.1 44.0 %all-to-all-start.2 = ((f32[4,1,65536]{2,1,0:T(1,128)}), f32[4,1,65536]{2,1,0:T(1,128)S(1)}, u32[]{:S(2)}, u32[]{:S(2)}) async-start(f32[4,1,65536]{2,1,0:T(1,128)} %reshape.34), calls=%async_computation.2 | async-start | bytes 2097152 | tf_op jit(solution)/shard_map/all_to_all | solution.py:58
  16.8 5.1 %collective-permute-start.20 = (f32[32,32]{0,1:T(8,128)S(1)}, f32[32,32]{0,1:T(8,128)S(1)}, u32[]{:S(2)}, u32[]{:S(2)}) collective-permute-start(f32[32,32]{0,1:T(8,128)S(1)} %copy.31), channel_id=1, source_target_pairs={{0,8},{8,0},{16,24},{24,16},{32,40},{40,32},{48,56},{56,48},{1,9},... | collective-permute-start | bytes 12296 | tf_op jit(solution)/shard_map/ppermute | solution.py:46
  22.0 10.5 %collective-permute-start.21 = (f32[64,32]{0,1:T(8,128)S(1)}, f32[64,32]{0,1:T(8,128)S(1)}, u32[]{:S(2)}, u32[]{:S(2)}) collective-permute-start(f32[64,32]{0,1:T(8,128)S(1)} %maximum_select_fusion.4), channel_id=1, source_target_pairs={{0,16},{8,24},{16,0},{24,8},{32,48},{40,56},{48,32},{56,40},{1,17}... | collective-permute-start | bytes 24584 | tf_op jit(solution)/shard_map/ppermute | solution.py:46
  27.8 15.7 %collective-permute-start.18 = (f32[64,32]{0,1:T(8,128)S(1)}, f32[64,32]{0,1:T(8,128)S(1)}, u32[]{:S(2)}, u32[]{:S(2)}) collective-permute-start(f32[64,32]{0,1:T(8,128)S(1)} %broadcast_divide_fusion.2), channel_id=1, source_target_pairs={{0,128},{128,0},{256,384},{384,256},{1,129},{129,1},{257,385},{385... | collective-permute-start | bytes 24584 | tf_op jit(solution)/shard_map/ppermute | solution.py:46
  32.6 15.5 %collective-permute-start.22 = (f32[128,32]{0,1:T(8,128)S(1)}, f32[128,32]{0,1:T(8,128)S(1)}, u32[]{:S(2)}, u32[]{:S(2)}) collective-permute-start(f32[128,32]{0,1:T(8,128)S(1)} %maximum_select_fusion.5), channel_id=1, source_target_pairs={{0,32},{8,40},{16,48},{24,56},{32,0},{40,8},{48,16},{56,24},{1,33}... | collective-permute-start | bytes 49160 | tf_op jit(solution)/shard_map/ppermute | solution.py:46
  43.6 8.4 %collective-permute-start.19 = (f32[128,32]{0,1:T(8,128)S(1)}, f32[128,32]{0,1:T(8,128)S(1)}, u32[]{:S(2)}, u32[]{:S(2)}) collective-permute-start(f32[128,32]{0,1:T(8,128)S(1)} %maximum_select_fusion.3), channel_id=1, source_target_pairs={{0,256},{128,384},{256,0},{384,128},{1,257},{129,385},{257,1},{385... | collective-permute-start | bytes 49160 | tf_op jit(solution)/shard_map/ppermute | solution.py:46
  48.1 5.0 collective-permute-start.23
  66.1 7.8 %collective-permute-start.5 = (f32[512,64]{0,1:T(8,128)S(1)}, f32[512,64]{0,1:T(8,128)S(1)}, u32[]{:S(2)}, u32[]{:S(2)}) collective-permute-start(f32[512,64]{0,1:T(8,128)S(1)} %pad_maximum_fusion.9), channel_id=1, source_target_pairs={{0,64},{64,0},{1,65},{65,1},{2,66},{66,2},{3,67},{67,3},{4,68},{68... | collective-permute-start | bytes 393224 | tf_op jit(solution)/shard_map/while/body/eval_jaxpr/ppermute | solution.py:25
  69.3 8.6 %collective-permute-start = (f32[256,32]{0,1:T(8,128)S(1)}, f32[256,32]{0,1:T(8,128)S(1)}, u32[]{:S(2)}, u32[]{:S(2)}) collective-permute-start(f32[256,32]{0,1:T(8,128)S(1)} %convolution_add_fusion.4), channel_id=1, source_target_pairs={{0,1},{1,0},{2,3},{3,2},{4,5},{5,4},{6,7},{7,6},{8,9},{9,8},{10,11... | collective-permute-start | bytes 98312 | tf_op jit(solution)/shard_map/while/body/eval_jaxpr/ppermute | solution.py:25
  73.9 24.1 %collective-permute-start.6 = (f32[512,64]{0,1:T(8,128)S(1)}, f32[512,64]{0,1:T(8,128)S(1)}, u32[]{:S(2)}, u32[]{:S(2)}) collective-permute-start(f32[512,64]{0,1:T(8,128)S(1)} %fusion.92), channel_id=1, source_target_pairs={{0,8},{8,0},{16,24},{24,16},{32,40},{40,32},{48,56},{56,48},{1,9},... | collective-permute-start | bytes 393224 | tf_op jit(solution)/shard_map/while/body/eval_jaxpr/ppermute | solution.py:25
  77.9 4.7 collective-permute-start.1
  82.6 6.2 %collective-permute-start.2 = (f32[256,32]{0,1:T(8,128)S(1)}, f32[256,32]{0,1:T(8,128)S(1)}, u32[]{:S(2)}, u32[]{:S(2)}) collective-permute-start(f32[256,32]{0,1:T(8,128)S(1)} %add.202), channel_id=1, source_target_pairs={{0,4},{2,6},{4,0},{6,2},{1,5},{3,7},{5,1},{7,3},{8,12},{10,14},{12... | collective-permute-start | bytes 98312 | tf_op jit(solution)/shard_map/while/body/eval_jaxpr/ppermute | solution.py:25
  88.7 5.7 %collective-permute-start.3 = (f32[256,32]{0,1:T(8,128)S(1)}, f32[256,32]{0,1:T(8,128)S(1)}, u32[]{:S(2)}, u32[]{:S(2)}) collective-permute-start(f32[256,32]{0,1:T(8,128)S(1)} %add.203), channel_id=1, source_target_pairs={{0,128},{128,0},{256,384},{384,256},{1,129},{129,1},{257,385},{385... | collective-permute-start | bytes 98312 | tf_op jit(solution)/shard_map/while/body/eval_jaxpr/ppermute | solution.py:25
  94.4 9.5 %collective-permute-start.4 = (f32[256,32]{0,1:T(8,128)S(1)}, f32[256,32]{0,1:T(8,128)S(1)}, u32[]{:S(2)}, u32[]{:S(2)}) collective-permute-start(f32[256,32]{0,1:T(8,128)S(1)} %add.204), channel_id=1, source_target_pairs={{0,256},{128,384},{256,0},{384,128},{1,257},{129,385},{257,1},{385... | collective-permute-start | bytes 98312 | tf_op jit(solution)/shard_map/while/body/eval_jaxpr/ppermute | solution.py:25
  98.1 9.9 %collective-permute-start.7 = (f32[512,64]{0,1:T(8,128)S(1)}, f32[512,64]{0,1:T(8,128)S(1)}, u32[]{:S(2)}, u32[]{:S(2)}) collective-permute-start(f32[512,64]{0,1:T(8,128)S(1)} %add.205), channel_id=1, source_target_pairs={{0,16},{8,24},{16,0},{24,8},{32,48},{40,56},{48,32},{56,40},{1,17}... | collective-permute-start | bytes 393224 | tf_op jit(solution)/shard_map/while/body/eval_jaxpr/ppermute | solution.py:25
  107.9 12.0 %collective-permute-start.8 = (f32[512,64]{0,1:T(8,128)S(1)}, f32[512,64]{0,1:T(8,128)S(1)}, u32[]{:S(2)}, u32[]{:S(2)}) collective-permute-start(f32[512,64]{0,1:T(8,128)S(1)} %add.206), channel_id=1, source_target_pairs={{0,32},{8,40},{16,48},{24,56},{32,0},{40,8},{48,16},{56,24},{1,33}... | collective-permute-start | bytes 393224 | tf_op jit(solution)/shard_map/while/body/eval_jaxpr/ppermute | solution.py:25
  122.9 12.0 %collective-permute-start.14 = (f32[512,64]{0,1:T(8,128)S(1)}, f32[512,64]{0,1:T(8,128)S(1)}, u32[]{:S(2)}, u32[]{:S(2)}) collective-permute-start(f32[512,64]{0,1:T(8,128)S(1)} %pad_maximum_fusion.11), channel_id=1, source_target_pairs={{0,64},{64,0},{1,65},{65,1},{2,66},{66,2},{3,67},{67,3},{4,68},{68... | collective-permute-start | bytes 393224 | tf_op jit(solution)/shard_map/while/body/eval_jaxpr/ppermute | solution.py:25
  125.8 11.1 %collective-permute-start.9 = (f32[256,32]{0,1:T(8,128)S(1)}, f32[256,32]{0,1:T(8,128)S(1)}, u32[]{:S(2)}, u32[]{:S(2)}) collective-permute-start(f32[256,32]{0,1:T(8,128)S(1)} %convolution_add_fusion.5), channel_id=1, source_target_pairs={{0,1},{1,0},{2,3},{3,2},{4,5},{5,4},{6,7},{7,6},{8,9},{9,8},{10,11... | collective-permute-start | bytes 98312 | tf_op jit(solution)/shard_map/while/body/eval_jaxpr/ppermute | solution.py:25
  135.0 24.1 %collective-permute-start.15 = (f32[512,64]{0,1:T(8,128)S(1)}, f32[512,64]{0,1:T(8,128)S(1)}, u32[]{:S(2)}, u32[]{:S(2)}) collective-permute-start(f32[512,64]{0,1:T(8,128)S(1)} %fusion.99), channel_id=1, source_target_pairs={{0,8},{8,0},{16,24},{24,16},{32,40},{40,32},{48,56},{56,48},{1,9},... | collective-permute-start | bytes 393224 | tf_op jit(solution)/shard_map/while/body/eval_jaxpr/ppermute | solution.py:25
  141.6 6.2 %collective-permute-start.11 = (f32[256,32]{0,1:T(8,128)S(1)}, f32[256,32]{0,1:T(8,128)S(1)}, u32[]{:S(2)}, u32[]{:S(2)}) collective-permute-start(f32[256,32]{0,1:T(8,128)S(1)} %add.209), channel_id=1, source_target_pairs={{0,4},{2,6},{4,0},{6,2},{1,5},{3,7},{5,1},{7,3},{8,12},{10,14},{12... | collective-permute-start | bytes 98312 | tf_op jit(solution)/shard_map/while/body/eval_jaxpr/ppermute | solution.py:25
  147.8 5.7 %collective-permute-start.12 = (f32[256,32]{0,1:T(8,128)S(1)}, f32[256,32]{0,1:T(8,128)S(1)}, u32[]{:S(2)}, u32[]{:S(2)}) collective-permute-start(f32[256,32]{0,1:T(8,128)S(1)} %add.210), channel_id=1, source_target_pairs={{0,128},{128,0},{256,384},{384,256},{1,129},{129,1},{257,385},{385... | collective-permute-start | bytes 98312 | tf_op jit(solution)/shard_map/while/body/eval_jaxpr/ppermute | solution.py:25
  153.4 10.0 %collective-permute-start.13 = (f32[256,32]{0,1:T(8,128)S(1)}, f32[256,32]{0,1:T(8,128)S(1)}, u32[]{:S(2)}, u32[]{:S(2)}) collective-permute-start(f32[256,32]{0,1:T(8,128)S(1)} %add.211), channel_id=1, source_target_pairs={{0,256},{128,384},{256,0},{384,128},{1,257},{129,385},{257,1},{385... | collective-permute-start | bytes 98312 | tf_op jit(solution)/shard_map/while/body/eval_jaxpr/ppermute | solution.py:25
  159.1 8.4 %collective-permute-start.16 = (f32[512,64]{0,1:T(8,128)S(1)}, f32[512,64]{0,1:T(8,128)S(1)}, u32[]{:S(2)}, u32[]{:S(2)}) collective-permute-start(f32[512,64]{0,1:T(8,128)S(1)} %add.212), channel_id=1, source_target_pairs={{0,16},{8,24},{16,0},{24,8},{32,48},{40,56},{48,32},{56,40},{1,17}... | collective-permute-start | bytes 393224 | tf_op jit(solution)/shard_map/while/body/eval_jaxpr/ppermute | solution.py:25
  167.5 22.1 %collective-permute-start.17 = (f32[512,64]{0,1:T(8,128)S(1)}, f32[512,64]{0,1:T(8,128)S(1)}, u32[]{:S(2)}, u32[]{:S(2)}) collective-permute-start(f32[512,64]{0,1:T(8,128)S(1)} %add.213), channel_id=1, source_target_pairs={{0,32},{8,40},{16,48},{24,56},{32,0},{40,8},{48,16},{56,24},{1,33}... | collective-permute-start | bytes 393224 | tf_op jit(solution)/shard_map/while/body/eval_jaxpr/ppermute | solution.py:25
  177.7 11.9 %all-to-all-start = ((f32[16,1,2]{2,1,0:T(1,128)}), f32[16,1,2]{2,1,0:T(1,128)S(1)}, u32[]{:S(2)}, u32[]{:S(2)}) async-start(f32[16,1,2]{2,1,0:T(1,128)} %broadcast_in_dim.6), calls=%async_computation | async-start | bytes 16384 | tf_op jit(solution)/shard_map/while/body/eval_jaxpr/all_to_all | solution.py:35
  192.3 28.0 %all-to-all-start.1 = ((f32[32,1,2]{2,1,0:T(1,128)}), f32[32,1,2]{2,1,0:T(1,128)S(1)}, u32[]{:S(2)}, u32[]{:S(2)}) async-start(f32[32,1,2]{2,1,0:T(1,128)} %broadcast_in_dim.7), calls=%async_computation.1 | async-start | bytes 32768 | tf_op jit(solution)/shard_map/while/body/eval_jaxpr/all_to_all | solution.py:35
  225.3 6.3 %collective-permute-start.5 = (f32[512,64]{0,1:T(8,128)S(1)}, f32[512,64]{0,1:T(8,128)S(1)}, u32[]{:S(2)}, u32[]{:S(2)}) collective-permute-start(f32[512,64]{0,1:T(8,128)S(1)} %pad_maximum_fusion.9), channel_id=1, source_target_pairs={{0,64},{64,0},{1,65},{65,1},{2,66},{66,2},{3,67},{67,3},{4,68},{68... | collective-permute-start | bytes 393224 | tf_op jit(solution)/shard_map/while/body/eval_jaxpr/ppermute | solution.py:25
  228.7 5.2 %collective-permute-start = (f32[256,32]{0,1:T(8,128)S(1)}, f32[256,32]{0,1:T(8,128)S(1)}, u32[]{:S(2)}, u32[]{:S(2)}) collective-permute-start(f32[256,32]{0,1:T(8,128)S(1)} %convolution_add_fusion.4), channel_id=1, source_target_pairs={{0,1},{1,0},{2,3},{3,2},{4,5},{5,4},{6,7},{7,6},{8,9},{9,8},{10,11... | collective-permute-start | bytes 98312 | tf_op jit(solution)/shard_map/while/body/eval_jaxpr/ppermute | solution.py:25
  231.7 21.2 %collective-permute-start.6 = (f32[512,64]{0,1:T(8,128)S(1)}, f32[512,64]{0,1:T(8,128)S(1)}, u32[]{:S(2)}, u32[]{:S(2)}) collective-permute-start(f32[512,64]{0,1:T(8,128)S(1)} %fusion.92), channel_id=1, source_target_pairs={{0,8},{8,0},{16,24},{24,16},{32,40},{40,32},{48,56},{56,48},{1,9},... | collective-permute-start | bytes 393224 | tf_op jit(solution)/shard_map/while/body/eval_jaxpr/ppermute | solution.py:25
  233.9 5.0 collective-permute-start.1
  238.9 6.2 %collective-permute-start.2 = (f32[256,32]{0,1:T(8,128)S(1)}, f32[256,32]{0,1:T(8,128)S(1)}, u32[]{:S(2)}, u32[]{:S(2)}) collective-permute-start(f32[256,32]{0,1:T(8,128)S(1)} %add.202), channel_id=1, source_target_pairs={{0,4},{2,6},{4,0},{6,2},{1,5},{3,7},{5,1},{7,3},{8,12},{10,14},{12... | collective-permute-start | bytes 98312 | tf_op jit(solution)/shard_map/while/body/eval_jaxpr/ppermute | solution.py:25
  245.0 5.5 %collective-permute-start.3 = (f32[256,32]{0,1:T(8,128)S(1)}, f32[256,32]{0,1:T(8,128)S(1)}, u32[]{:S(2)}, u32[]{:S(2)}) collective-permute-start(f32[256,32]{0,1:T(8,128)S(1)} %add.203), channel_id=1, source_target_pairs={{0,128},{128,0},{256,384},{384,256},{1,129},{129,1},{257,385},{385... | collective-permute-start | bytes 98312 | tf_op jit(solution)/shard_map/while/body/eval_jaxpr/ppermute | solution.py:25
  250.6 8.7 %collective-permute-start.4 = (f32[256,32]{0,1:T(8,128)S(1)}, f32[256,32]{0,1:T(8,128)S(1)}, u32[]{:S(2)}, u32[]{:S(2)}) collective-permute-start(f32[256,32]{0,1:T(8,128)S(1)} %add.204), channel_id=1, source_target_pairs={{0,256},{128,384},{256,0},{384,128},{1,257},{129,385},{257,1},{385... | collective-permute-start | bytes 98312 | tf_op jit(solution)/shard_map/while/body/eval_jaxpr/ppermute | solution.py:25
  252.9 8.0 %collective-permute-start.7 = (f32[512,64]{0,1:T(8,128)S(1)}, f32[512,64]{0,1:T(8,128)S(1)}, u32[]{:S(2)}, u32[]{:S(2)}) collective-permute-start(f32[512,64]{0,1:T(8,128)S(1)} %add.205), channel_id=1, source_target_pairs={{0,16},{8,24},{16,0},{24,8},{32,48},{40,56},{48,32},{56,40},{1,17}... | collective-permute-start | bytes 393224 | tf_op jit(solution)/shard_map/while/body/eval_jaxpr/ppermute | solution.py:25
  261.0 9.7 %collective-permute-start.8 = (f32[512,64]{0,1:T(8,128)S(1)}, f32[512,64]{0,1:T(8,128)S(1)}, u32[]{:S(2)}, u32[]{:S(2)}) collective-permute-start(f32[512,64]{0,1:T(8,128)S(1)} %add.206), channel_id=1, source_target_pairs={{0,32},{8,40},{16,48},{24,56},{32,0},{40,8},{48,16},{56,24},{1,33}... | collective-permute-start | bytes 393224 | tf_op jit(solution)/shard_map/while/body/eval_jaxpr/ppermute | solution.py:25
  273.6 13.5 %collective-permute-start.14 = (f32[512,64]{0,1:T(8,128)S(1)}, f32[512,64]{0,1:T(8,128)S(1)}, u32[]{:S(2)}, u32[]{:S(2)}) collective-permute-start(f32[512,64]{0,1:T(8,128)S(1)} %pad_maximum_fusion.11), channel_id=1, source_target_pairs={{0,64},{64,0},{1,65},{65,1},{2,66},{66,2},{3,67},{67,3},{4,68},{68... | collective-permute-start | bytes 393224 | tf_op jit(solution)/shard_map/while/body/eval_jaxpr/ppermute | solution.py:25
  277.9 11.2 %collective-permute-start.9 = (f32[256,32]{0,1:T(8,128)S(1)}, f32[256,32]{0,1:T(8,128)S(1)}, u32[]{:S(2)}, u32[]{:S(2)}) collective-permute-start(f32[256,32]{0,1:T(8,128)S(1)} %convolution_add_fusion.5), channel_id=1, source_target_pairs={{0,1},{1,0},{2,3},{3,2},{4,5},{5,4},{6,7},{7,6},{8,9},{9,8},{10,11... | collective-permute-start | bytes 98312 | tf_op jit(solution)/shard_map/while/body/eval_jaxpr/ppermute | solution.py:25
  287.2 25.2 %collective-permute-start.15 = (f32[512,64]{0,1:T(8,128)S(1)}, f32[512,64]{0,1:T(8,128)S(1)}, u32[]{:S(2)}, u32[]{:S(2)}) collective-permute-start(f32[512,64]{0,1:T(8,128)S(1)} %fusion.99), channel_id=1, source_target_pairs={{0,8},{8,0},{16,24},{24,16},{32,40},{40,32},{48,56},{56,48},{1,9},... | collective-permute-start | bytes 393224 | tf_op jit(solution)/shard_map/while/body/eval_jaxpr/ppermute | solution.py:25
  293.8 6.2 %collective-permute-start.11 = (f32[256,32]{0,1:T(8,128)S(1)}, f32[256,32]{0,1:T(8,128)S(1)}, u32[]{:S(2)}, u32[]{:S(2)}) collective-permute-start(f32[256,32]{0,1:T(8,128)S(1)} %add.209), channel_id=1, source_target_pairs={{0,4},{2,6},{4,0},{6,2},{1,5},{3,7},{5,1},{7,3},{8,12},{10,14},{12... | collective-permute-start | bytes 98312 | tf_op jit(solution)/shard_map/while/body/eval_jaxpr/ppermute | solution.py:25
  299.9 5.5 %collective-permute-start.12 = (f32[256,32]{0,1:T(8,128)S(1)}, f32[256,32]{0,1:T(8,128)S(1)}, u32[]{:S(2)}, u32[]{:S(2)}) collective-permute-start(f32[256,32]{0,1:T(8,128)S(1)} %add.210), channel_id=1, source_target_pairs={{0,128},{128,0},{256,384},{384,256},{1,129},{129,1},{257,385},{385... | collective-permute-start | bytes 98312 | tf_op jit(solution)/shard_map/while/body/eval_jaxpr/ppermute | solution.py:25
  305.5 10.0 %collective-permute-start.13 = (f32[256,32]{0,1:T(8,128)S(1)}, f32[256,32]{0,1:T(8,128)S(1)}, u32[]{:S(2)}, u32[]{:S(2)}) collective-permute-start(f32[256,32]{0,1:T(8,128)S(1)} %add.211), channel_id=1, source_target_pairs={{0,256},{128,384},{256,0},{384,128},{1,257},{129,385},{257,1},{385... | collective-permute-start | bytes 98312 | tf_op jit(solution)/shard_map/while/body/eval_jaxpr/ppermute | solution.py:25
  312.4 6.9 %collective-permute-start.16 = (f32[512,64]{0,1:T(8,128)S(1)}, f32[512,64]{0,1:T(8,128)S(1)}, u32[]{:S(2)}, u32[]{:S(2)}) collective-permute-start(f32[512,64]{0,1:T(8,128)S(1)} %add.212), channel_id=1, source_target_pairs={{0,16},{8,24},{16,0},{24,8},{32,48},{40,56},{48,32},{56,40},{1,17}... | collective-permute-start | bytes 393224 | tf_op jit(solution)/shard_map/while/body/eval_jaxpr/ppermute | solution.py:25
  319.4 21.2 %collective-permute-start.17 = (f32[512,64]{0,1:T(8,128)S(1)}, f32[512,64]{0,1:T(8,128)S(1)}, u32[]{:S(2)}, u32[]{:S(2)}) collective-permute-start(f32[512,64]{0,1:T(8,128)S(1)} %add.213), channel_id=1, source_target_pairs={{0,32},{8,40},{16,48},{24,56},{32,0},{40,8},{48,16},{56,24},{1,33}... | collective-permute-start | bytes 393224 | tf_op jit(solution)/shard_map/while/body/eval_jaxpr/ppermute | solution.py:25
  325.5 15.0 %all-to-all-start = ((f32[16,1,2]{2,1,0:T(1,128)}), f32[16,1,2]{2,1,0:T(1,128)S(1)}, u32[]{:S(2)}, u32[]{:S(2)}) async-start(f32[16,1,2]{2,1,0:T(1,128)} %broadcast_in_dim.6), calls=%async_computation | async-start | bytes 16384 | tf_op jit(solution)/shard_map/while/body/eval_jaxpr/all_to_all | solution.py:35
  343.2 19.7 %all-to-all-start.1 = ((f32[32,1,2]{2,1,0:T(1,128)}), f32[32,1,2]{2,1,0:T(1,128)S(1)}, u32[]{:S(2)}, u32[]{:S(2)}) async-start(f32[32,1,2]{2,1,0:T(1,128)} %broadcast_in_dim.7), calls=%async_computation.1 | async-start | bytes 32768 | tf_op jit(solution)/shard_map/while/body/eval_jaxpr/all_to_all | solution.py:35
  367.9 6.3 %collective-permute-start.5 = (f32[512,64]{0,1:T(8,128)S(1)}, f32[512,64]{0,1:T(8,128)S(1)}, u32[]{:S(2)}, u32[]{:S(2)}) collective-permute-start(f32[512,64]{0,1:T(8,128)S(1)} %pad_maximum_fusion.9), channel_id=1, source_target_pairs={{0,64},{64,0},{1,65},{65,1},{2,66},{66,2},{3,67},{67,3},{4,68},{68... | collective-permute-start | bytes 393224 | tf_op jit(solution)/shard_map/while/body/eval_jaxpr/ppermute | solution.py:25
  371.3 5.2 %collective-permute-start = (f32[256,32]{0,1:T(8,128)S(1)}, f32[256,32]{0,1:T(8,128)S(1)}, u32[]{:S(2)}, u32[]{:S(2)}) collective-permute-start(f32[256,32]{0,1:T(8,128)S(1)} %convolution_add_fusion.4), channel_id=1, source_target_pairs={{0,1},{1,0},{2,3},{3,2},{4,5},{5,4},{6,7},{7,6},{8,9},{9,8},{10,11... | collective-permute-start | bytes 98312 | tf_op jit(solution)/shard_map/while/body/eval_jaxpr/ppermute | solution.py:25
  374.3 21.2 %collective-permute-start.6 = (f32[512,64]{0,1:T(8,128)S(1)}, f32[512,64]{0,1:T(8,128)S(1)}, u32[]{:S(2)}, u32[]{:S(2)}) collective-permute-start(f32[512,64]{0,1:T(8,128)S(1)} %fusion.92), channel_id=1, source_target_pairs={{0,8},{8,0},{16,24},{24,16},{32,40},{40,32},{48,56},{56,48},{1,9},... | collective-permute-start | bytes 393224 | tf_op jit(solution)/shard_map/while/body/eval_jaxpr/ppermute | solution.py:25
  376.5 5.0 collective-permute-start.1
  381.5 6.2 %collective-permute-start.2 = (f32[256,32]{0,1:T(8,128)S(1)}, f32[256,32]{0,1:T(8,128)S(1)}, u32[]{:S(2)}, u32[]{:S(2)}) collective-permute-start(f32[256,32]{0,1:T(8,128)S(1)} %add.202), channel_id=1, source_target_pairs={{0,4},{2,6},{4,0},{6,2},{1,5},{3,7},{5,1},{7,3},{8,12},{10,14},{12... | collective-permute-start | bytes 98312 | tf_op jit(solution)/shard_map/while/body/eval_jaxpr/ppermute | solution.py:25
  387.7 5.5 %collective-permute-start.3 = (f32[256,32]{0,1:T(8,128)S(1)}, f32[256,32]{0,1:T(8,128)S(1)}, u32[]{:S(2)}, u32[]{:S(2)}) collective-permute-start(f32[256,32]{0,1:T(8,128)S(1)} %add.203), channel_id=1, source_target_pairs={{0,128},{128,0},{256,384},{384,256},{1,129},{129,1},{257,385},{385... | collective-permute-start | bytes 98312 | tf_op jit(solution)/shard_map/while/body/eval_jaxpr/ppermute | solution.py:25
  393.2 8.7 %collective-permute-start.4 = (f32[256,32]{0,1:T(8,128)S(1)}, f32[256,32]{0,1:T(8,128)S(1)}, u32[]{:S(2)}, u32[]{:S(2)}) collective-permute-start(f32[256,32]{0,1:T(8,128)S(1)} %add.204), channel_id=1, source_target_pairs={{0,256},{128,384},{256,0},{384,128},{1,257},{129,385},{257,1},{385... | collective-permute-start | bytes 98312 | tf_op jit(solution)/shard_map/while/body/eval_jaxpr/ppermute | solution.py:25
  395.5 8.0 %collective-permute-start.7 = (f32[512,64]{0,1:T(8,128)S(1)}, f32[512,64]{0,1:T(8,128)S(1)}, u32[]{:S(2)}, u32[]{:S(2)}) collective-permute-start(f32[512,64]{0,1:T(8,128)S(1)} %add.205), channel_id=1, source_target_pairs={{0,16},{8,24},{16,0},{24,8},{32,48},{40,56},{48,32},{56,40},{1,17}... | collective-permute-start | bytes 393224 | tf_op jit(solution)/shard_map/while/body/eval_jaxpr/ppermute | solution.py:25
  403.6 9.6 %collective-permute-start.8 = (f32[512,64]{0,1:T(8,128)S(1)}, f32[512,64]{0,1:T(8,128)S(1)}, u32[]{:S(2)}, u32[]{:S(2)}) collective-permute-start(f32[512,64]{0,1:T(8,128)S(1)} %add.206), channel_id=1, source_target_pairs={{0,32},{8,40},{16,48},{24,56},{32,0},{40,8},{48,16},{56,24},{1,33}... | collective-permute-start | bytes 393224 | tf_op jit(solution)/shard_map/while/body/eval_jaxpr/ppermute | solution.py:25
  416.2 13.6 %collective-permute-start.14 = (f32[512,64]{0,1:T(8,128)S(1)}, f32[512,64]{0,1:T(8,128)S(1)}, u32[]{:S(2)}, u32[]{:S(2)}) collective-permute-start(f32[512,64]{0,1:T(8,128)S(1)} %pad_maximum_fusion.11), channel_id=1, source_target_pairs={{0,64},{64,0},{1,65},{65,1},{2,66},{66,2},{3,67},{67,3},{4,68},{68... | collective-permute-start | bytes 393224 | tf_op jit(solution)/shard_map/while/body/eval_jaxpr/ppermute | solution.py:25
  420.5 11.2 %collective-permute-start.9 = (f32[256,32]{0,1:T(8,128)S(1)}, f32[256,32]{0,1:T(8,128)S(1)}, u32[]{:S(2)}, u32[]{:S(2)}) collective-permute-start(f32[256,32]{0,1:T(8,128)S(1)} %convolution_add_fusion.5), channel_id=1, source_target_pairs={{0,1},{1,0},{2,3},{3,2},{4,5},{5,4},{6,7},{7,6},{8,9},{9,8},{10,11... | collective-permute-start | bytes 98312 | tf_op jit(solution)/shard_map/while/body/eval_jaxpr/ppermute | solution.py:25
  429.8 25.2 %collective-permute-start.15 = (f32[512,64]{0,1:T(8,128)S(1)}, f32[512,64]{0,1:T(8,128)S(1)}, u32[]{:S(2)}, u32[]{:S(2)}) collective-permute-start(f32[512,64]{0,1:T(8,128)S(1)} %fusion.99), channel_id=1, source_target_pairs={{0,8},{8,0},{16,24},{24,16},{32,40},{40,32},{48,56},{56,48},{1,9},... | collective-permute-start | bytes 393224 | tf_op jit(solution)/shard_map/while/body/eval_jaxpr/ppermute | solution.py:25
  436.4 6.2 %collective-permute-start.11 = (f32[256,32]{0,1:T(8,128)S(1)}, f32[256,32]{0,1:T(8,128)S(1)}, u32[]{:S(2)}, u32[]{:S(2)}) collective-permute-start(f32[256,32]{0,1:T(8,128)S(1)} %add.209), channel_id=1, source_target_pairs={{0,4},{2,6},{4,0},{6,2},{1,5},{3,7},{5,1},{7,3},{8,12},{10,14},{12... | collective-permute-start | bytes 98312 | tf_op jit(solution)/shard_map/while/body/eval_jaxpr/ppermute | solution.py:25
  442.6 5.5 %collective-permute-start.12 = (f32[256,32]{0,1:T(8,128)S(1)}, f32[256,32]{0,1:T(8,128)S(1)}, u32[]{:S(2)}, u32[]{:S(2)}) collective-permute-start(f32[256,32]{0,1:T(8,128)S(1)} %add.210), channel_id=1, source_target_pairs={{0,128},{128,0},{256,384},{384,256},{1,129},{129,1},{257,385},{385... | collective-permute-start | bytes 98312 | tf_op jit(solution)/shard_map/while/body/eval_jaxpr/ppermute | solution.py:25
  448.1 10.0 %collective-permute-start.13 = (f32[256,32]{0,1:T(8,128)S(1)}, f32[256,32]{0,1:T(8,128)S(1)}, u32[]{:S(2)}, u32[]{:S(2)}) collective-permute-start(f32[256,32]{0,1:T(8,128)S(1)} %add.211), channel_id=1, source_target_pairs={{0,256},{128,384},{256,0},{384,128},{1,257},{129,385},{257,1},{385... | collective-permute-start | bytes 98312 | tf_op jit(solution)/shard_map/while/body/eval_jaxpr/ppermute | solution.py:25
  455.0 6.9 %collective-permute-start.16 = (f32[512,64]{0,1:T(8,128)S(1)}, f32[512,64]{0,1:T(8,128)S(1)}, u32[]{:S(2)}, u32[]{:S(2)}) collective-permute-start(f32[512,64]{0,1:T(8,128)S(1)} %add.212), channel_id=1, source_target_pairs={{0,16},{8,24},{16,0},{24,8},{32,48},{40,56},{48,32},{56,40},{1,17}... | collective-permute-start | bytes 393224 | tf_op jit(solution)/shard_map/while/body/eval_jaxpr/ppermute | solution.py:25
  462.0 21.2 %collective-permute-start.17 = (f32[512,64]{0,1:T(8,128)S(1)}, f32[512,64]{0,1:T(8,128)S(1)}, u32[]{:S(2)}, u32[]{:S(2)}) collective-permute-start(f32[512,64]{0,1:T(8,128)S(1)} %add.213), channel_id=1, source_target_pairs={{0,32},{8,40},{16,48},{24,56},{32,0},{40,8},{48,16},{56,24},{1,33}... | collective-permute-start | bytes 393224 | tf_op jit(solution)/shard_map/while/body/eval_jaxpr/ppermute | solution.py:25
  468.1 15.0 %all-to-all-start = ((f32[16,1,2]{2,1,0:T(1,128)}), f32[16,1,2]{2,1,0:T(1,128)S(1)}, u32[]{:S(2)}, u32[]{:S(2)}) async-start(f32[16,1,2]{2,1,0:T(1,128)} %broadcast_in_dim.6), calls=%async_computation | async-start | bytes 16384 | tf_op jit(solution)/shard_map/while/body/eval_jaxpr/all_to_all | solution.py:35
  485.8 19.7 %all-to-all-start.1 = ((f32[32,1,2]{2,1,0:T(1,128)}), f32[32,1,2]{2,1,0:T(1,128)S(1)}, u32[]{:S(2)}, u32[]{:S(2)}) async-start(f32[32,1,2]{2,1,0:T(1,128)} %broadcast_in_dim.7), calls=%async_computation.1 | async-start | bytes 32768 | tf_op jit(solution)/shard_map/while/body/eval_jaxpr/all_to_all | solution.py:35
  (5 other events, 39.6 us)

commit v5 on v3

--- a/solution.py
+++ b/solution.py
@@ -52,11 +52,13 @@
 
 def per_device(genotypes, observed, ancestry, freqs):
     quarter = lax.axis_size("yh")
-    geno = genotypes.astype(jnp.float32)
-    seen = observed.astype(jnp.float32)
-    counts = jnp.stack([seen * geno, seen * (2.0 - geno)])
-    counts = lax.all_to_all(counts, "yh", 2, 1, tiled=True)
-    hits, misses = counts[0], counts[1]
+    rows, width = genotypes.shape
+    geno = genotypes.astype(jnp.float32).reshape(rows, quarter, width // quarter).transpose(1, 0, 2)
+    seen = observed.astype(jnp.float32).reshape(rows, quarter, width // quarter).transpose(1, 0, 2)
+    counts = jnp.stack([seen * geno, seen * (2.0 - geno)], axis=1)
+    counts = lax.all_to_all(counts, "yh", 0, 0, tiled=True)
+    hits = counts[:, 0].reshape(quarter * rows, width // quarter)
+    misses = counts[:, 1].reshape(quarter * rows, width // quarter)
     own_rows = ancestry.shape[0]
     own_snps = freqs.shape[0]
     q_own = ancestry / jnp.sum(ancestry, axis=1, keepdims=True)
@@ -102,7 +104,6 @@
     q_final = lax.dynamic_slice_in_dim(q_zero, lax.axis_index("yh") * own_rows, own_rows, 0)
     f_index = lax.axis_index("yl") * lax.axis_size("z") + lax.axis_index("z")
     f_final = lax.dynamic_slice_in_dim(f_zero, f_index * own_snps, own_snps, 0)
-    del quarter
     return (q_final, f_final)
 
 

time: 500 us -> 493 us (0.986)
  local copies, waits for them, and re-layouts: 15.8 us -> 9.62 us
    unnamed x10 -> x8, local copies, waits for them, and re-layouts: 8.27 us -> 1.44 us
  transfers between devices with their start and end apart: 65 -> 65, of which waited for: 37 -> 39; matrix products, arithmetic and copies ran while one was open for 4% -> 3% of each run, Pallas kernels for 0% -> 0%
where the time goes in v5:
time: 493 us; the launch traced here: 491 us
  starting transfers between devices  283 us (57%)
  waiting for transfers between devices  125 us (25%)
  blocking collectives  26.2 us (5%)
  other arithmetic  19.9 us (4%)
  matrix products  16.1 us (3%)
  between operations  10.4 us (2%)
  local copies, waits for them, and re-layouts  9.62 us (2%)
    ppermute x54, starting transfers between devices, doubling_sum(): value = value + lax.ppermute(value, name, pairs)  202 us
    ppermute x54, waiting for transfers between devices, doubling_sum(): value = value + lax.ppermute(value, name, pairs)  85.6 us
    all_to_all x4, starting transfers between devices, group_total(): gathered = lax.all_to_all(spread, axes, 0, 0, tiled=True)  43.9 us
    all_to_all x4, waiting for transfers between devices, group_total(): gathered = lax.all_to_all(spread, axes, 0, 0, tiled=True)  32.9 us
    ppermute x6, starting transfers between devices, doubling_gather(): other = lax.ppermute(value, name, pairs)  29.1 us
    all_to_all x2, blocking collectives, group_total(): gathered = lax.all_to_all(spread, axes, 0, 0, tiled=True)  26.2 us
  transfers between devices with their start and end apart: 65, of which 39 were waited for; matrix products, arithmetic and copies ran while one was open for 3% of the time, Pallas kernels for 0%

profile of v5, /device:TPU:1, one launch (start us, length us, event | category | flops | bytes accessed | tf_op | source)
XLA Modules:
  0.0 490.5 jit_solution(6733319371853369563)
XLA Ops:
  4.9 7.8 %all-to-all-start = ((f32[4,2,64,512]{3,2,1,0:T(8,128)}), f32[4,2,64,512]{3,2,1,0:T(8,128)S(1)}, u32[]{:S(2)}, u32[]{:S(2)}) async-start(f32[4,2,64,512]{3,2,1,0:T(8,128)} %copy.27), calls=%async_computation | async-start | bytes 2097152 | tf_op jit(solution)/shard_map/all_to_all | solution.py:59
  12.8 4.1 collective-permute-start.2
  18.1 5.8 %collective-permute-start.3 = (f32[64,32]{0,1:T(8,128)S(1)}, f32[64,32]{0,1:T(8,128)S(1)}, u32[]{:S(2)}, u32[]{:S(2)}) collective-permute-start(f32[64,32]{0,1:T(8,128)S(1)} %maximum_select_fusion.4), channel_id=1, source_target_pairs={{0,16},{8,24},{16,0},{24,8},{32,48},{40,56},{48,32},{56,40},{1,17}... | collective-permute-start | bytes 24584 | tf_op jit(solution)/shard_map/ppermute | solution.py:46
  23.9 4.6 collective-permute-start
  28.7 8.2 %collective-permute-start.4 = (f32[128,32]{0,1:T(8,128)S(1)}, f32[128,32]{0,1:T(8,128)S(1)}, u32[]{:S(2)}, u32[]{:S(2)}) collective-permute-start(f32[128,32]{0,1:T(8,128)S(1)} %maximum_select_fusion.5), channel_id=1, source_target_pairs={{0,32},{8,40},{16,48},{24,56},{32,0},{40,8},{48,16},{56,24},{1,33}... | collective-permute-start | bytes 49160 | tf_op jit(solution)/shard_map/ppermute | solution.py:46
  39.6 4.5 collective-permute-start.1
  53.7 4.7 collective-permute-start.6
  58.5 3.8 collective-permute-start.12
  62.4 3.1 collective-permute-start.7
  67.1 4.6 collective-permute-start.8
  73.2 4.4 collective-permute-start.9
  78.9 3.7 collective-permute-start.10
  82.6 5.7 %collective-permute-start.13 = (f32[512,64]{0,1:T(8,128)S(1)}, f32[512,64]{0,1:T(8,128)S(1)}, u32[]{:S(2)}, u32[]{:S(2)}) collective-permute-start(f32[512,64]{0,1:T(8,128)S(1)} %add.317), channel_id=1, source_target_pairs={{0,16},{8,24},{16,0},{24,8},{32,48},{40,56},{48,32},{56,40},{1,17}... | collective-permute-start | bytes 393224 | tf_op jit(solution)/shard_map/ppermute | solution.py:25
  88.4 3.6 collective-permute-done.13
  92.0 8.6 %collective-permute-start.14 = (f32[512,64]{0,1:T(8,128)S(1)}, f32[512,64]{0,1:T(8,128)S(1)}, u32[]{:S(2)}, u32[]{:S(2)}) collective-permute-start(f32[512,64]{0,1:T(8,128)S(1)} %add.318), channel_id=1, source_target_pairs={{0,32},{8,40},{16,48},{24,56},{32,0},{40,8},{48,16},{56,24},{1,33}... | collective-permute-start | bytes 393224 | tf_op jit(solution)/shard_map/ppermute | solution.py:25
  100.6 3.8 collective-permute-done.14
  110.1 9.2 %collective-permute-start.15 = (f32[256,32]{0,1:T(8,128)S(1)}, f32[256,32]{0,1:T(8,128)S(1)}, u32[]{:S(2)}, u32[]{:S(2)}) collective-permute-start(f32[256,32]{0,1:T(8,128)S(1)} %convolution_add_fusion.4), channel_id=1, source_target_pairs={{0,1},{1,0},{2,3},{3,2},{4,5},{5,4},{6,7},{7,6},{8,9},{9,8},{10,11... | collective-permute-start | bytes 98312 | tf_op jit(solution)/shard_map/ppermute | solution.py:25
  121.3 3.1 collective-permute-start.16
  125.9 4.6 collective-permute-start.17
  132.1 4.4 collective-permute-start.18
  137.8 5.7 %collective-permute-start.19 = (f32[256,32]{0,1:T(8,128)S(1)}, f32[256,32]{0,1:T(8,128)S(1)}, u32[]{:S(2)}, u32[]{:S(2)}) collective-permute-start(f32[256,32]{0,1:T(8,128)S(1)} %add.325), channel_id=1, source_target_pairs={{0,256},{128,384},{256,0},{384,128},{1,257},{129,385},{257,1},{385... | collective-permute-start | bytes 98312 | tf_op jit(solution)/shard_map/ppermute | solution.py:25
  143.5 4.4 collective-permute-start.22
  148.5 3.4 collective-permute-done.22
  152.0 7.5 %collective-permute-start.23 = (f32[512,64]{0,1:T(8,128)S(1)}, f32[512,64]{0,1:T(8,128)S(1)}, u32[]{:S(2)}, u32[]{:S(2)}) collective-permute-start(f32[512,64]{0,1:T(8,128)S(1)} %add.330), channel_id=1, source_target_pairs={{0,32},{8,40},{16,48},{24,56},{32,0},{40,8},{48,16},{56,24},{1,33}... | collective-permute-start | bytes 393224 | tf_op jit(solution)/shard_map/ppermute | solution.py:25
  161.6 11.4 %all_to_all.41 = f32[16,1,2]{2,1,0:T(1,128)S(1)} all-to-all(f32[16,1,2]{2,1,0:T(1,128)S(1)} %broadcast_in_dim.12), channel_id=1, replica_groups=mesh['yh'=4,'yl'=2,'z'=8,'x'=4,'c'=2] {'yl','z'}, dimensions={0} | all-to-all | bytes 256 | tf_op jit(solution)/shard_map/all_to_all | solution.py:35
  175.8 14.9 %all-to-all-start.2 = ((f32[32,1,2]{2,1,0:T(1,128)}), f32[32,1,2]{2,1,0:T(1,128)S(1)}, u32[]{:S(2)}, u32[]{:S(2)}) async-start(f32[32,1,2]{2,1,0:T(1,128)} %broadcast_in_dim.13), calls=%async_computation.2 | async-start | bytes 32768 | tf_op jit(solution)/shard_map/all_to_all | solution.py:35
  191.3 8.6 %all-to-all-done.2 = f32[32,1,2]{2,1,0:T(1,128)S(1)} async-done(((f32[32,1,2]{2,1,0:T(1,128)}), f32[32,1,2]{2,1,0:T(1,128)S(1)}, u32[]{:S(2)}, u32[]{:S(2)}) %all-to-all-start.2) | async-done | bytes 288 | tf_op jit(solution)/shard_map/all_to_all | solution.py:35
  208.3 2.9 collective-permute-start.24
  219.0 2.8 collective-permute-start.26
  221.8 3.3 collective-permute-done.26
  227.3 3.4 collective-permute-done.27
  235.2 4.0 collective-permute-done.28
  241.0 3.3 collective-permute-start.32
  244.4 6.4 %collective-permute-done.32 = f32[512,64]{0,1:T(8,128)S(1)} collective-permute-done((f32[512,64]{0,1:T(8,128)S(1)}, f32[512,64]{0,1:T(8,128)S(1)}, u32[]{:S(2)}, u32[]{:S(2)}) %collective-permute-start.32) | collective-permute-done | bytes 131104 | tf_op jit(solution)/shard_map/ppermute | solution.py:25
  253.6 2.8 collective-permute-start.38
  257.0 10.2 %collective-permute-start.33 = (f32[256,32]{0,1:T(8,128)S(1)}, f32[256,32]{0,1:T(8,128)S(1)}, u32[]{:S(2)}, u32[]{:S(2)}) collective-permute-start(f32[256,32]{0,1:T(8,128)S(1)} %convolution_add_fusion.2), channel_id=1, source_target_pairs={{0,1},{1,0},{2,3},{3,2},{4,5},{5,4},{6,7},{7,6},{8,9},{9,8},{10,11... | collective-permute-start | bytes 98312 | tf_op jit(solution)/shard_map/ppermute | solution.py:25
  276.6 3.5 collective-permute-done.35
  280.0 3.8 collective-permute-start.36
  285.6 6.9 %collective-permute-start.37 = (f32[256,32]{0,1:T(8,128)S(1)}, f32[256,32]{0,1:T(8,128)S(1)}, u32[]{:S(2)}, u32[]{:S(2)}) collective-permute-start(f32[256,32]{0,1:T(8,128)S(1)} %add.354), channel_id=1, source_target_pairs={{0,256},{128,384},{256,0},{384,128},{1,257},{129,385},{257,1},{385... | collective-permute-start | bytes 98312 | tf_op jit(solution)/shard_map/ppermute | solution.py:25
  292.5 3.0 collective-permute-start.40
  296.2 3.3 collective-permute-done.40
  299.5 3.5 collective-permute-start.41
  305.1 14.7 %all_to_all.42 = f32[16,1,2]{2,1,0:T(1,128)S(1)} all-to-all(f32[16,1,2]{2,1,0:T(1,128)S(1)} %broadcast_in_dim.14), channel_id=1, replica_groups=mesh['yh'=4,'yl'=2,'z'=8,'x'=4,'c'=2] {'yl','z'}, dimensions={0} | all-to-all | bytes 256 | tf_op jit(solution)/shard_map/all_to_all | solution.py:35
  322.5 10.6 %all-to-all-start.4 = ((f32[32,1,2]{2,1,0:T(1,128)}), f32[32,1,2]{2,1,0:T(1,128)S(1)}, u32[]{:S(2)}, u32[]{:S(2)}) async-start(f32[32,1,2]{2,1,0:T(1,128)} %broadcast_in_dim.15), calls=%async_computation.4 | async-start | bytes 32768 | tf_op jit(solution)/shard_map/all_to_all | solution.py:35
  333.8 8.6 %all-to-all-done.4 = f32[32,1,2]{2,1,0:T(1,128)S(1)} async-done(((f32[32,1,2]{2,1,0:T(1,128)}), f32[32,1,2]{2,1,0:T(1,128)S(1)}, u32[]{:S(2)}, u32[]{:S(2)}) %all-to-all-start.4) | async-done | bytes 288 | tf_op jit(solution)/shard_map/all_to_all | solution.py:35
  350.8 2.9 collective-permute-start.42
  361.4 2.8 collective-permute-start.44
  364.3 3.3 collective-permute-done.44
  369.8 3.3 collective-permute-done.45
  377.7 4.1 collective-permute-done.46
  383.6 3.1 collective-permute-start.50
  386.7 6.6 %collective-permute-done.50 = f32[512,64]{0,1:T(8,128)S(1)} collective-permute-done((f32[512,64]{0,1:T(8,128)S(1)}, f32[512,64]{0,1:T(8,128)S(1)}, u32[]{:S(2)}, u32[]{:S(2)}) %collective-permute-start.50) | collective-permute-done | bytes 131104 | tf_op jit(solution)/shard_map/ppermute | solution.py:25
  396.1 2.8 collective-permute-start.56
  399.4 10.3 %collective-permute-start.51 = (f32[256,32]{0,1:T(8,128)S(1)}, f32[256,32]{0,1:T(8,128)S(1)}, u32[]{:S(2)}, u32[]{:S(2)}) collective-permute-start(f32[256,32]{0,1:T(8,128)S(1)} %convolution_add_fusion), channel_id=1, source_target_pairs={{0,1},{1,0},{2,3},{3,2},{4,5},{5,4},{6,7},{7,6},{8,9},{9,8},{10,11... | collective-permute-start | bytes 98312 | tf_op jit(solution)/shard_map/ppermute | solution.py:25
  419.1 3.5 collective-permute-done.53
  422.5 3.8 collective-permute-start.54
  428.1 6.9 %collective-permute-start.55 = (f32[256,32]{0,1:T(8,128)S(1)}, f32[256,32]{0,1:T(8,128)S(1)}, u32[]{:S(2)}, u32[]{:S(2)}) collective-permute-start(f32[256,32]{0,1:T(8,128)S(1)} %add.383), channel_id=1, source_target_pairs={{0,256},{128,384},{256,0},{384,128},{1,257},{129,385},{257,1},{385... | collective-permute-start | bytes 98312 | tf_op jit(solution)/shard_map/ppermute | solution.py:25
  435.0 3.0 collective-permute-start.58
  438.7 3.2 collective-permute-done.58
  441.9 3.5 collective-permute-start.59
  448.2 7.7 %all-to-all-start.5 = ((f32[16,1,2]{2,1,0:T(1,128)}), f32[16,1,2]{2,1,0:T(1,128)S(1)}, u32[]{:S(2)}, u32[]{:S(2)}) async-start(f32[16,1,2]{2,1,0:T(1,128)} %broadcast_in_dim.16), calls=%async_computation.5 | async-start | bytes 16384 | tf_op jit(solution)/shard_map/all_to_all | solution.py:35
  455.9 7.2 %all-to-all-done.5 = f32[16,1,2]{2,1,0:T(1,128)S(1)} async-done(((f32[16,1,2]{2,1,0:T(1,128)}), f32[16,1,2]{2,1,0:T(1,128)S(1)}, u32[]{:S(2)}, u32[]{:S(2)}) %all-to-all-start.5) | async-done | bytes 160 | tf_op jit(solution)/shard_map/all_to_all | solution.py:35
  465.8 10.6 %all-to-all-start.6 = ((f32[32,1,2]{2,1,0:T(1,128)}), f32[32,1,2]{2,1,0:T(1,128)S(1)}, u32[]{:S(2)}, u32[]{:S(2)}) async-start(f32[32,1,2]{2,1,0:T(1,128)} %broadcast_in_dim.17), calls=%async_computation.6 | async-start | bytes 32768 | tf_op jit(solution)/shard_map/all_to_all | solution.py:35
  477.0 8.6 %all-to-all-done.6 = f32[32,1,2]{2,1,0:T(1,128)S(1)} async-done(((f32[32,1,2]{2,1,0:T(1,128)}), f32[32,1,2]{2,1,0:T(1,128)S(1)}, u32[]{:S(2)}, u32[]{:S(2)}) %all-to-all-start.6) | async-done | bytes 288 | tf_op jit(solution)/shard_map/all_to_all | solution.py:35
  (224 shorter events, 127.4 us)
Async XLA Ops:
  4.9 41.1 %all-to-all-start = ((f32[4,2,64,512]{3,2,1,0:T(8,128)}), f32[4,2,64,512]{3,2,1,0:T(8,128)S(1)}, u32[]{:S(2)}, u32[]{:S(2)}) async-start(f32[4,2,64,512]{3,2,1,0:T(8,128)} %copy.27), calls=%async_computation | async-start | bytes 2097152 | tf_op jit(solution)/shard_map/all_to_all | solution.py:59
  12.8 5.2 %collective-permute-start.2 = (f32[32,32]{0,1:T(8,128)S(1)}, f32[32,32]{0,1:T(8,128)S(1)}, u32[]{:S(2)}, u32[]{:S(2)}) collective-permute-start(f32[32,32]{0,1:T(8,128)S(1)} %copy.28), channel_id=1, source_target_pairs={{0,8},{8,0},{16,24},{24,16},{32,40},{40,32},{48,56},{56,48},{1,9},... | collective-permute-start | bytes 12296 | tf_op jit(solution)/shard_map/ppermute | solution.py:46
  18.1 10.5 %collective-permute-start.3 = (f32[64,32]{0,1:T(8,128)S(1)}, f32[64,32]{0,1:T(8,128)S(1)}, u32[]{:S(2)}, u32[]{:S(2)}) collective-permute-start(f32[64,32]{0,1:T(8,128)S(1)} %maximum_select_fusion.4), channel_id=1, source_target_pairs={{0,16},{8,24},{16,0},{24,8},{32,48},{40,56},{48,32},{56,40},{1,17}... | collective-permute-start | bytes 24584 | tf_op jit(solution)/shard_map/ppermute | solution.py:46
  23.9 15.5 %collective-permute-start = (f32[64,32]{0,1:T(8,128)S(1)}, f32[64,32]{0,1:T(8,128)S(1)}, u32[]{:S(2)}, u32[]{:S(2)}) collective-permute-start(f32[64,32]{0,1:T(8,128)S(1)} %broadcast_divide_fusion.5), channel_id=1, source_target_pairs={{0,128},{128,0},{256,384},{384,256},{1,129},{129,1},{257,385},{385... | collective-permute-start | bytes 24584 | tf_op jit(solution)/shard_map/ppermute | solution.py:46
  28.7 15.4 %collective-permute-start.4 = (f32[128,32]{0,1:T(8,128)S(1)}, f32[128,32]{0,1:T(8,128)S(1)}, u32[]{:S(2)}, u32[]{:S(2)}) collective-permute-start(f32[128,32]{0,1:T(8,128)S(1)} %maximum_select_fusion.5), channel_id=1, source_target_pairs={{0,32},{8,40},{16,48},{24,56},{32,0},{40,8},{48,16},{56,24},{1,33}... | collective-permute-start | bytes 49160 | tf_op jit(solution)/shard_map/ppermute | solution.py:46
  39.6 8.4 %collective-permute-start.1 = (f32[128,32]{0,1:T(8,128)S(1)}, f32[128,32]{0,1:T(8,128)S(1)}, u32[]{:S(2)}, u32[]{:S(2)}) collective-permute-start(f32[128,32]{0,1:T(8,128)S(1)} %maximum_select_fusion.3), channel_id=1, source_target_pairs={{0,256},{128,384},{256,0},{384,128},{1,257},{129,385},{257,1},{385... | collective-permute-start | bytes 49160 | tf_op jit(solution)/shard_map/ppermute | solution.py:46
  44.1 5.0 %collective-permute-start.5 = (f32[256,32]{0,1:T(8,128)S(1)}, f32[256,32]{0,1:T(8,128)S(1)}, u32[]{:S(2)}, u32[]{:S(2)}) collective-permute-start(f32[256,32]{0,1:T(8,128)S(1)} %maximum_select_fusion.2), channel_id=1, source_target_pairs={{0,64},{64,0},{1,65},{65,1},{2,66},{66,2},{3,67},{67,3},{4,68},{68... | collective-permute-start | bytes 98312 | tf_op jit(solution)/shard_map/ppermute | solution.py:46
  50.7 7.8 %collective-permute-start.11 = (f32[512,64]{0,1:T(8,128)S(1)}, f32[512,64]{0,1:T(8,128)S(1)}, u32[]{:S(2)}, u32[]{:S(2)}) collective-permute-start(f32[512,64]{0,1:T(8,128)S(1)} %pad_maximum_fusion.1), channel_id=1, source_target_pairs={{0,64},{64,0},{1,65},{65,1},{2,66},{66,2},{3,67},{67,3},{4,68},{68... | collective-permute-start | bytes 393224 | tf_op jit(solution)/shard_map/ppermute | solution.py:25
  53.7 8.6 %collective-permute-start.6 = (f32[256,32]{0,1:T(8,128)S(1)}, f32[256,32]{0,1:T(8,128)S(1)}, u32[]{:S(2)}, u32[]{:S(2)}) collective-permute-start(f32[256,32]{0,1:T(8,128)S(1)} %convolution_add_fusion.5), channel_id=1, source_target_pairs={{0,1},{1,0},{2,3},{3,2},{4,5},{5,4},{6,7},{7,6},{8,9},{9,8},{10,11... | collective-permute-start | bytes 98312 | tf_op jit(solution)/shard_map/ppermute | solution.py:25
  58.5 24.1 %collective-permute-start.12 = (f32[512,64]{0,1:T(8,128)S(1)}, f32[512,64]{0,1:T(8,128)S(1)}, u32[]{:S(2)}, u32[]{:S(2)}) collective-permute-start(f32[512,64]{0,1:T(8,128)S(1)} %fusion.44), channel_id=1, source_target_pairs={{0,8},{8,0},{16,24},{24,16},{32,40},{40,32},{48,56},{56,48},{1,9},... | collective-permute-start | bytes 393224 | tf_op jit(solution)/shard_map/ppermute | solution.py:25
  62.4 4.7 collective-permute-start.7
  67.1 6.2 %collective-permute-start.8 = (f32[256,32]{0,1:T(8,128)S(1)}, f32[256,32]{0,1:T(8,128)S(1)}, u32[]{:S(2)}, u32[]{:S(2)}) collective-permute-start(f32[256,32]{0,1:T(8,128)S(1)} %add.312), channel_id=1, source_target_pairs={{0,4},{2,6},{4,0},{6,2},{1,5},{3,7},{5,1},{7,3},{8,12},{10,14},{12... | collective-permute-start | bytes 98312 | tf_op jit(solution)/shard_map/ppermute | solution.py:25
  73.2 5.7 %collective-permute-start.9 = (f32[256,32]{0,1:T(8,128)S(1)}, f32[256,32]{0,1:T(8,128)S(1)}, u32[]{:S(2)}, u32[]{:S(2)}) collective-permute-start(f32[256,32]{0,1:T(8,128)S(1)} %add.313), channel_id=1, source_target_pairs={{0,128},{128,0},{256,384},{384,256},{1,129},{129,1},{257,385},{385... | collective-permute-start | bytes 98312 | tf_op jit(solution)/shard_map/ppermute | solution.py:25
  78.9 9.5 %collective-permute-start.10 = (f32[256,32]{0,1:T(8,128)S(1)}, f32[256,32]{0,1:T(8,128)S(1)}, u32[]{:S(2)}, u32[]{:S(2)}) collective-permute-start(f32[256,32]{0,1:T(8,128)S(1)} %add.314), channel_id=1, source_target_pairs={{0,256},{128,384},{256,0},{384,128},{1,257},{129,385},{257,1},{385... | collective-permute-start | bytes 98312 | tf_op jit(solution)/shard_map/ppermute | solution.py:25
  82.6 9.3 %collective-permute-start.13 = (f32[512,64]{0,1:T(8,128)S(1)}, f32[512,64]{0,1:T(8,128)S(1)}, u32[]{:S(2)}, u32[]{:S(2)}) collective-permute-start(f32[512,64]{0,1:T(8,128)S(1)} %add.317), channel_id=1, source_target_pairs={{0,16},{8,24},{16,0},{24,8},{32,48},{40,56},{48,32},{56,40},{1,17}... | collective-permute-start | bytes 393224 | tf_op jit(solution)/shard_map/ppermute | solution.py:25
  92.0 12.4 %collective-permute-start.14 = (f32[512,64]{0,1:T(8,128)S(1)}, f32[512,64]{0,1:T(8,128)S(1)}, u32[]{:S(2)}, u32[]{:S(2)}) collective-permute-start(f32[512,64]{0,1:T(8,128)S(1)} %add.318), channel_id=1, source_target_pairs={{0,32},{8,40},{16,48},{24,56},{32,0},{40,8},{48,16},{56,24},{1,33}... | collective-permute-start | bytes 393224 | tf_op jit(solution)/shard_map/ppermute | solution.py:25
  107.2 12.1 %collective-permute-start.20 = (f32[512,64]{0,1:T(8,128)S(1)}, f32[512,64]{0,1:T(8,128)S(1)}, u32[]{:S(2)}, u32[]{:S(2)}) collective-permute-start(f32[512,64]{0,1:T(8,128)S(1)} %pad_maximum_fusion.2), channel_id=1, source_target_pairs={{0,64},{64,0},{1,65},{65,1},{2,66},{66,2},{3,67},{67,3},{4,68},{68... | collective-permute-start | bytes 393224 | tf_op jit(solution)/shard_map/ppermute | solution.py:25
  110.1 11.1 %collective-permute-start.15 = (f32[256,32]{0,1:T(8,128)S(1)}, f32[256,32]{0,1:T(8,128)S(1)}, u32[]{:S(2)}, u32[]{:S(2)}) collective-permute-start(f32[256,32]{0,1:T(8,128)S(1)} %convolution_add_fusion.4), channel_id=1, source_target_pairs={{0,1},{1,0},{2,3},{3,2},{4,5},{5,4},{6,7},{7,6},{8,9},{9,8},{10,11... | collective-permute-start | bytes 98312 | tf_op jit(solution)/shard_map/ppermute | solution.py:25
  119.3 24.1 %collective-permute-start.21 = (f32[512,64]{0,1:T(8,128)S(1)}, f32[512,64]{0,1:T(8,128)S(1)}, u32[]{:S(2)}, u32[]{:S(2)}) collective-permute-start(f32[512,64]{0,1:T(8,128)S(1)} %fusion.43), channel_id=1, source_target_pairs={{0,8},{8,0},{16,24},{24,16},{32,40},{40,32},{48,56},{56,48},{1,9},... | collective-permute-start | bytes 393224 | tf_op jit(solution)/shard_map/ppermute | solution.py:25
  121.3 4.7 collective-permute-start.16
  125.9 6.2 %collective-permute-start.17 = (f32[256,32]{0,1:T(8,128)S(1)}, f32[256,32]{0,1:T(8,128)S(1)}, u32[]{:S(2)}, u32[]{:S(2)}) collective-permute-start(f32[256,32]{0,1:T(8,128)S(1)} %add.323), channel_id=1, source_target_pairs={{0,4},{2,6},{4,0},{6,2},{1,5},{3,7},{5,1},{7,3},{8,12},{10,14},{12... | collective-permute-start | bytes 98312 | tf_op jit(solution)/shard_map/ppermute | solution.py:25
  132.1 5.7 %collective-permute-start.18 = (f32[256,32]{0,1:T(8,128)S(1)}, f32[256,32]{0,1:T(8,128)S(1)}, u32[]{:S(2)}, u32[]{:S(2)}) collective-permute-start(f32[256,32]{0,1:T(8,128)S(1)} %add.324), channel_id=1, source_target_pairs={{0,128},{128,0},{256,384},{384,256},{1,129},{129,1},{257,385},{385... | collective-permute-start | bytes 98312 | tf_op jit(solution)/shard_map/ppermute | solution.py:25
  137.8 10.1 %collective-permute-start.19 = (f32[256,32]{0,1:T(8,128)S(1)}, f32[256,32]{0,1:T(8,128)S(1)}, u32[]{:S(2)}, u32[]{:S(2)}) collective-permute-start(f32[256,32]{0,1:T(8,128)S(1)} %add.325), channel_id=1, source_target_pairs={{0,256},{128,384},{256,0},{384,128},{1,257},{129,385},{257,1},{385... | collective-permute-start | bytes 98312 | tf_op jit(solution)/shard_map/ppermute | solution.py:25
  143.5 8.4 %collective-permute-start.22 = (f32[512,64]{0,1:T(8,128)S(1)}, f32[512,64]{0,1:T(8,128)S(1)}, u32[]{:S(2)}, u32[]{:S(2)}) collective-permute-start(f32[512,64]{0,1:T(8,128)S(1)} %add.329), channel_id=1, source_target_pairs={{0,16},{8,24},{16,0},{24,8},{32,48},{40,56},{48,32},{56,40},{1,17}... | collective-permute-start | bytes 393224 | tf_op jit(solution)/shard_map/ppermute | solution.py:25
  152.0 21.1 %collective-permute-start.23 = (f32[512,64]{0,1:T(8,128)S(1)}, f32[512,64]{0,1:T(8,128)S(1)}, u32[]{:S(2)}, u32[]{:S(2)}) collective-permute-start(f32[512,64]{0,1:T(8,128)S(1)} %add.330), channel_id=1, source_target_pairs={{0,32},{8,40},{16,48},{24,56},{32,0},{40,8},{48,16},{56,24},{1,33}... | collective-permute-start | bytes 393224 | tf_op jit(solution)/shard_map/ppermute | solution.py:25
  175.8 24.1 %all-to-all-start.2 = ((f32[32,1,2]{2,1,0:T(1,128)}), f32[32,1,2]{2,1,0:T(1,128)S(1)}, u32[]{:S(2)}, u32[]{:S(2)}) async-start(f32[32,1,2]{2,1,0:T(1,128)} %broadcast_in_dim.13), calls=%async_computation.2 | async-start | bytes 32768 | tf_op jit(solution)/shard_map/all_to_all | solution.py:35
  205.5 6.2 %collective-permute-start.29 = (f32[512,64]{0,1:T(8,128)S(1)}, f32[512,64]{0,1:T(8,128)S(1)}, u32[]{:S(2)}, u32[]{:S(2)}) collective-permute-start(f32[512,64]{0,1:T(8,128)S(1)} %pad_maximum_fusion.3), channel_id=1, source_target_pairs={{0,64},{64,0},{1,65},{65,1},{2,66},{66,2},{3,67},{67,3},{4,68},{68... | collective-permute-start | bytes 393224 | tf_op jit(solution)/shard_map/ppermute | solution.py:25
  208.3 5.7 %collective-permute-start.24 = (f32[256,32]{0,1:T(8,128)S(1)}, f32[256,32]{0,1:T(8,128)S(1)}, u32[]{:S(2)}, u32[]{:S(2)}) collective-permute-start(f32[256,32]{0,1:T(8,128)S(1)} %convolution_add_fusion.3), channel_id=1, source_target_pairs={{0,1},{1,0},{2,3},{3,2},{4,5},{5,4},{6,7},{7,6},{8,9},{9,8},{10,11... | collective-permute-start | bytes 98312 | tf_op jit(solution)/shard_map/ppermute | solution.py:25
  211.8 21.2 %collective-permute-start.30 = (f32[512,64]{0,1:T(8,128)S(1)}, f32[512,64]{0,1:T(8,128)S(1)}, u32[]{:S(2)}, u32[]{:S(2)}) collective-permute-start(f32[512,64]{0,1:T(8,128)S(1)} %fusion.42), channel_id=1, source_target_pairs={{0,8},{8,0},{16,24},{24,16},{32,40},{40,32},{48,56},{56,48},{1,9},... | collective-permute-start | bytes 393224 | tf_op jit(solution)/shard_map/ppermute | solution.py:25
  214.0 5.0 %collective-permute-start.25 = (f32[256,32]{0,1:T(8,128)S(1)}, f32[256,32]{0,1:T(8,128)S(1)}, u32[]{:S(2)}, u32[]{:S(2)}) collective-permute-start(f32[256,32]{0,1:T(8,128)S(1)} %add.340), channel_id=1, source_target_pairs={{0,2},{2,0},{4,6},{6,4},{1,3},{3,1},{5,7},{7,5},{8,10},{10,8},{12,... | collective-permute-start | bytes 98312 | tf_op jit(solution)/shard_map/ppermute | solution.py:25
  219.0 6.2 %collective-permute-start.26 = (f32[256,32]{0,1:T(8,128)S(1)}, f32[256,32]{0,1:T(8,128)S(1)}, u32[]{:S(2)}, u32[]{:S(2)}) collective-permute-start(f32[256,32]{0,1:T(8,128)S(1)} %add.341), channel_id=1, source_target_pairs={{0,4},{2,6},{4,0},{6,2},{1,5},{3,7},{5,1},{7,3},{8,12},{10,14},{12... | collective-permute-start | bytes 98312 | tf_op jit(solution)/shard_map/ppermute | solution.py:25
  225.1 5.5 %collective-permute-start.27 = (f32[256,32]{0,1:T(8,128)S(1)}, f32[256,32]{0,1:T(8,128)S(1)}, u32[]{:S(2)}, u32[]{:S(2)}) collective-permute-start(f32[256,32]{0,1:T(8,128)S(1)} %add.342), channel_id=1, source_target_pairs={{0,128},{128,0},{256,384},{384,256},{1,129},{129,1},{257,385},{385... | collective-permute-start | bytes 98312 | tf_op jit(solution)/shard_map/ppermute | solution.py:25
  230.7 8.6 %collective-permute-start.28 = (f32[256,32]{0,1:T(8,128)S(1)}, f32[256,32]{0,1:T(8,128)S(1)}, u32[]{:S(2)}, u32[]{:S(2)}) collective-permute-start(f32[256,32]{0,1:T(8,128)S(1)} %add.343), channel_id=1, source_target_pairs={{0,256},{128,384},{256,0},{384,128},{1,257},{129,385},{257,1},{385... | collective-permute-start | bytes 98312 | tf_op jit(solution)/shard_map/ppermute | solution.py:25
  233.0 8.0 %collective-permute-start.31 = (f32[512,64]{0,1:T(8,128)S(1)}, f32[512,64]{0,1:T(8,128)S(1)}, u32[]{:S(2)}, u32[]{:S(2)}) collective-permute-start(f32[512,64]{0,1:T(8,128)S(1)} %add.346), channel_id=1, source_target_pairs={{0,16},{8,24},{16,0},{24,8},{32,48},{40,56},{48,32},{56,40},{1,17}... | collective-permute-start | bytes 393224 | tf_op jit(solution)/shard_map/ppermute | solution.py:25
  241.0 9.7 %collective-permute-start.32 = (f32[512,64]{0,1:T(8,128)S(1)}, f32[512,64]{0,1:T(8,128)S(1)}, u32[]{:S(2)}, u32[]{:S(2)}) collective-permute-start(f32[512,64]{0,1:T(8,128)S(1)} %add.347), channel_id=1, source_target_pairs={{0,32},{8,40},{16,48},{24,56},{32,0},{40,8},{48,16},{56,24},{1,33}... | collective-permute-start | bytes 393224 | tf_op jit(solution)/shard_map/ppermute | solution.py:25
  253.6 13.6 %collective-permute-start.38 = (f32[512,64]{0,1:T(8,128)S(1)}, f32[512,64]{0,1:T(8,128)S(1)}, u32[]{:S(2)}, u32[]{:S(2)}) collective-permute-start(f32[512,64]{0,1:T(8,128)S(1)} %pad_maximum_fusion.4), channel_id=1, source_target_pairs={{0,64},{64,0},{1,65},{65,1},{2,66},{66,2},{3,67},{67,3},{4,68},{68... | collective-permute-start | bytes 393224 | tf_op jit(solution)/shard_map/ppermute | solution.py:25
  257.0 12.2 %collective-permute-start.33 = (f32[256,32]{0,1:T(8,128)S(1)}, f32[256,32]{0,1:T(8,128)S(1)}, u32[]{:S(2)}, u32[]{:S(2)}) collective-permute-start(f32[256,32]{0,1:T(8,128)S(1)} %convolution_add_fusion.2), channel_id=1, source_target_pairs={{0,1},{1,0},{2,3},{3,2},{4,5},{5,4},{6,7},{7,6},{8,9},{9,8},{10,11... | collective-permute-start | bytes 98312 | tf_op jit(solution)/shard_map/ppermute | solution.py:25
  267.2 25.2 %collective-permute-start.39 = (f32[512,64]{0,1:T(8,128)S(1)}, f32[512,64]{0,1:T(8,128)S(1)}, u32[]{:S(2)}, u32[]{:S(2)}) collective-permute-start(f32[512,64]{0,1:T(8,128)S(1)} %fusion.41), channel_id=1, source_target_pairs={{0,8},{8,0},{16,24},{24,16},{32,40},{40,32},{48,56},{56,48},{1,9},... | collective-permute-start | bytes 393224 | tf_op jit(solution)/shard_map/ppermute | solution.py:25
  269.2 4.7 collective-permute-start.34
  273.9 6.2 %collective-permute-start.35 = (f32[256,32]{0,1:T(8,128)S(1)}, f32[256,32]{0,1:T(8,128)S(1)}, u32[]{:S(2)}, u32[]{:S(2)}) collective-permute-start(f32[256,32]{0,1:T(8,128)S(1)} %add.352), channel_id=1, source_target_pairs={{0,4},{2,6},{4,0},{6,2},{1,5},{3,7},{5,1},{7,3},{8,12},{10,14},{12... | collective-permute-start | bytes 98312 | tf_op jit(solution)/shard_map/ppermute | solution.py:25
  280.0 5.5 %collective-permute-start.36 = (f32[256,32]{0,1:T(8,128)S(1)}, f32[256,32]{0,1:T(8,128)S(1)}, u32[]{:S(2)}, u32[]{:S(2)}) collective-permute-start(f32[256,32]{0,1:T(8,128)S(1)} %add.353), channel_id=1, source_target_pairs={{0,128},{128,0},{256,384},{384,256},{1,129},{129,1},{257,385},{385... | collective-permute-start | bytes 98312 | tf_op jit(solution)/shard_map/ppermute | solution.py:25
  285.6 10.0 %collective-permute-start.37 = (f32[256,32]{0,1:T(8,128)S(1)}, f32[256,32]{0,1:T(8,128)S(1)}, u32[]{:S(2)}, u32[]{:S(2)}) collective-permute-start(f32[256,32]{0,1:T(8,128)S(1)} %add.354), channel_id=1, source_target_pairs={{0,256},{128,384},{256,0},{384,128},{1,257},{129,385},{257,1},{385... | collective-permute-start | bytes 98312 | tf_op jit(solution)/shard_map/ppermute | solution.py:25
  292.5 6.9 %collective-permute-start.40 = (f32[512,64]{0,1:T(8,128)S(1)}, f32[512,64]{0,1:T(8,128)S(1)}, u32[]{:S(2)}, u32[]{:S(2)}) collective-permute-start(f32[512,64]{0,1:T(8,128)S(1)} %add.358), channel_id=1, source_target_pairs={{0,16},{8,24},{16,0},{24,8},{32,48},{40,56},{48,32},{56,40},{1,17}... | collective-permute-start | bytes 393224 | tf_op jit(solution)/shard_map/ppermute | solution.py:25
  299.5 20.5 %collective-permute-start.41 = (f32[512,64]{0,1:T(8,128)S(1)}, f32[512,64]{0,1:T(8,128)S(1)}, u32[]{:S(2)}, u32[]{:S(2)}) collective-permute-start(f32[512,64]{0,1:T(8,128)S(1)} %add.359), channel_id=1, source_target_pairs={{0,32},{8,40},{16,48},{24,56},{32,0},{40,8},{48,16},{56,24},{1,33}... | collective-permute-start | bytes 393224 | tf_op jit(solution)/shard_map/ppermute | solution.py:25
  322.5 19.8 %all-to-all-start.4 = ((f32[32,1,2]{2,1,0:T(1,128)}), f32[32,1,2]{2,1,0:T(1,128)S(1)}, u32[]{:S(2)}, u32[]{:S(2)}) async-start(f32[32,1,2]{2,1,0:T(1,128)} %broadcast_in_dim.15), calls=%async_computation.4 | async-start | bytes 32768 | tf_op jit(solution)/shard_map/all_to_all | solution.py:35
  348.0 6.2 %collective-permute-start.47 = (f32[512,64]{0,1:T(8,128)S(1)}, f32[512,64]{0,1:T(8,128)S(1)}, u32[]{:S(2)}, u32[]{:S(2)}) collective-permute-start(f32[512,64]{0,1:T(8,128)S(1)} %pad_maximum_fusion.5), channel_id=1, source_target_pairs={{0,64},{64,0},{1,65},{65,1},{2,66},{66,2},{3,67},{67,3},{4,68},{68... | collective-permute-start | bytes 393224 | tf_op jit(solution)/shard_map/ppermute | solution.py:25
  350.8 5.7 %collective-permute-start.42 = (f32[256,32]{0,1:T(8,128)S(1)}, f32[256,32]{0,1:T(8,128)S(1)}, u32[]{:S(2)}, u32[]{:S(2)}) collective-permute-start(f32[256,32]{0,1:T(8,128)S(1)} %convolution_add_fusion.1), channel_id=1, source_target_pairs={{0,1},{1,0},{2,3},{3,2},{4,5},{5,4},{6,7},{7,6},{8,9},{9,8},{10,11... | collective-permute-start | bytes 98312 | tf_op jit(solution)/shard_map/ppermute | solution.py:25
  354.2 21.2 %collective-permute-start.48 = (f32[512,64]{0,1:T(8,128)S(1)}, f32[512,64]{0,1:T(8,128)S(1)}, u32[]{:S(2)}, u32[]{:S(2)}) collective-permute-start(f32[512,64]{0,1:T(8,128)S(1)} %fusion.40), channel_id=1, source_target_pairs={{0,8},{8,0},{16,24},{24,16},{32,40},{40,32},{48,56},{56,48},{1,9},... | collective-permute-start | bytes 393224 | tf_op jit(solution)/shard_map/ppermute | solution.py:25
  356.5 5.0 %collective-permute-start.43 = (f32[256,32]{0,1:T(8,128)S(1)}, f32[256,32]{0,1:T(8,128)S(1)}, u32[]{:S(2)}, u32[]{:S(2)}) collective-permute-start(f32[256,32]{0,1:T(8,128)S(1)} %add.369), channel_id=1, source_target_pairs={{0,2},{2,0},{4,6},{6,4},{1,3},{3,1},{5,7},{7,5},{8,10},{10,8},{12,... | collective-permute-start | bytes 98312 | tf_op jit(solution)/shard_map/ppermute | solution.py:25
  361.4 6.2 %collective-permute-start.44 = (f32[256,32]{0,1:T(8,128)S(1)}, f32[256,32]{0,1:T(8,128)S(1)}, u32[]{:S(2)}, u32[]{:S(2)}) collective-permute-start(f32[256,32]{0,1:T(8,128)S(1)} %add.370), channel_id=1, source_target_pairs={{0,4},{2,6},{4,0},{6,2},{1,5},{3,7},{5,1},{7,3},{8,12},{10,14},{12... | collective-permute-start | bytes 98312 | tf_op jit(solution)/shard_map/ppermute | solution.py:25
  367.6 5.5 %collective-permute-start.45 = (f32[256,32]{0,1:T(8,128)S(1)}, f32[256,32]{0,1:T(8,128)S(1)}, u32[]{:S(2)}, u32[]{:S(2)}) collective-permute-start(f32[256,32]{0,1:T(8,128)S(1)} %add.371), channel_id=1, source_target_pairs={{0,128},{128,0},{256,384},{384,256},{1,129},{129,1},{257,385},{385... | collective-permute-start | bytes 98312 | tf_op jit(solution)/shard_map/ppermute | solution.py:25
  373.2 8.7 %collective-permute-start.46 = (f32[256,32]{0,1:T(8,128)S(1)}, f32[256,32]{0,1:T(8,128)S(1)}, u32[]{:S(2)}, u32[]{:S(2)}) collective-permute-start(f32[256,32]{0,1:T(8,128)S(1)} %add.372), channel_id=1, source_target_pairs={{0,256},{128,384},{256,0},{384,128},{1,257},{129,385},{257,1},{385... | collective-permute-start | bytes 98312 | tf_op jit(solution)/shard_map/ppermute | solution.py:25
  375.5 8.0 %collective-permute-start.49 = (f32[512,64]{0,1:T(8,128)S(1)}, f32[512,64]{0,1:T(8,128)S(1)}, u32[]{:S(2)}, u32[]{:S(2)}) collective-permute-start(f32[512,64]{0,1:T(8,128)S(1)} %add.375), channel_id=1, source_target_pairs={{0,16},{8,24},{16,0},{24,8},{32,48},{40,56},{48,32},{56,40},{1,17}... | collective-permute-start | bytes 393224 | tf_op jit(solution)/shard_map/ppermute | solution.py:25
  383.6 9.7 %collective-permute-start.50 = (f32[512,64]{0,1:T(8,128)S(1)}, f32[512,64]{0,1:T(8,128)S(1)}, u32[]{:S(2)}, u32[]{:S(2)}) collective-permute-start(f32[512,64]{0,1:T(8,128)S(1)} %add.376), channel_id=1, source_target_pairs={{0,32},{8,40},{16,48},{24,56},{32,0},{40,8},{48,16},{56,24},{1,33}... | collective-permute-start | bytes 393224 | tf_op jit(solution)/shard_map/ppermute | solution.py:25
  396.1 13.6 %collective-permute-start.56 = (f32[512,64]{0,1:T(8,128)S(1)}, f32[512,64]{0,1:T(8,128)S(1)}, u32[]{:S(2)}, u32[]{:S(2)}) collective-permute-start(f32[512,64]{0,1:T(8,128)S(1)} %pad_maximum_fusion.6), channel_id=1, source_target_pairs={{0,64},{64,0},{1,65},{65,1},{2,66},{66,2},{3,67},{67,3},{4,68},{68... | collective-permute-start | bytes 393224 | tf_op jit(solution)/shard_map/ppermute | solution.py:25
  399.4 12.2 %collective-permute-start.51 = (f32[256,32]{0,1:T(8,128)S(1)}, f32[256,32]{0,1:T(8,128)S(1)}, u32[]{:S(2)}, u32[]{:S(2)}) collective-permute-start(f32[256,32]{0,1:T(8,128)S(1)} %convolution_add_fusion), channel_id=1, source_target_pairs={{0,1},{1,0},{2,3},{3,2},{4,5},{5,4},{6,7},{7,6},{8,9},{9,8},{10,11... | collective-permute-start | bytes 98312 | tf_op jit(solution)/shard_map/ppermute | solution.py:25
  409.7 25.2 %collective-permute-start.57 = (f32[512,64]{0,1:T(8,128)S(1)}, f32[512,64]{0,1:T(8,128)S(1)}, u32[]{:S(2)}, u32[]{:S(2)}) collective-permute-start(f32[512,64]{0,1:T(8,128)S(1)} %fusion.39), channel_id=1, source_target_pairs={{0,8},{8,0},{16,24},{24,16},{32,40},{40,32},{48,56},{56,48},{1,9},... | collective-permute-start | bytes 393224 | tf_op jit(solution)/shard_map/ppermute | solution.py:25
  416.4 6.2 %collective-permute-start.53 = (f32[256,32]{0,1:T(8,128)S(1)}, f32[256,32]{0,1:T(8,128)S(1)}, u32[]{:S(2)}, u32[]{:S(2)}) collective-permute-start(f32[256,32]{0,1:T(8,128)S(1)} %add.381), channel_id=1, source_target_pairs={{0,4},{2,6},{4,0},{6,2},{1,5},{3,7},{5,1},{7,3},{8,12},{10,14},{12... | collective-permute-start | bytes 98312 | tf_op jit(solution)/shard_map/ppermute | solution.py:25
  422.5 5.5 %collective-permute-start.54 = (f32[256,32]{0,1:T(8,128)S(1)}, f32[256,32]{0,1:T(8,128)S(1)}, u32[]{:S(2)}, u32[]{:S(2)}) collective-permute-start(f32[256,32]{0,1:T(8,128)S(1)} %add.382), channel_id=1, source_target_pairs={{0,128},{128,0},{256,384},{384,256},{1,129},{129,1},{257,385},{385... | collective-permute-start | bytes 98312 | tf_op jit(solution)/shard_map/ppermute | solution.py:25
  428.1 10.0 %collective-permute-start.55 = (f32[256,32]{0,1:T(8,128)S(1)}, f32[256,32]{0,1:T(8,128)S(1)}, u32[]{:S(2)}, u32[]{:S(2)}) collective-permute-start(f32[256,32]{0,1:T(8,128)S(1)} %add.383), channel_id=1, source_target_pairs={{0,256},{128,384},{256,0},{384,128},{1,257},{129,385},{257,1},{385... | collective-permute-start | bytes 98312 | tf_op jit(solution)/shard_map/ppermute | solution.py:25
  435.0 6.9 %collective-permute-start.58 = (f32[512,64]{0,1:T(8,128)S(1)}, f32[512,64]{0,1:T(8,128)S(1)}, u32[]{:S(2)}, u32[]{:S(2)}) collective-permute-start(f32[512,64]{0,1:T(8,128)S(1)} %add.387), channel_id=1, source_target_pairs={{0,16},{8,24},{16,0},{24,8},{32,48},{40,56},{48,32},{56,40},{1,17}... | collective-permute-start | bytes 393224 | tf_op jit(solution)/shard_map/ppermute | solution.py:25
  441.9 21.2 %collective-permute-start.59 = (f32[512,64]{0,1:T(8,128)S(1)}, f32[512,64]{0,1:T(8,128)S(1)}, u32[]{:S(2)}, u32[]{:S(2)}) collective-permute-start(f32[512,64]{0,1:T(8,128)S(1)} %add.388), channel_id=1, source_target_pairs={{0,32},{8,40},{16,48},{24,56},{32,0},{40,8},{48,16},{56,24},{1,33}... | collective-permute-start | bytes 393224 | tf_op jit(solution)/shard_map/ppermute | solution.py:25
  448.2 14.9 %all-to-all-start.5 = ((f32[16,1,2]{2,1,0:T(1,128)}), f32[16,1,2]{2,1,0:T(1,128)S(1)}, u32[]{:S(2)}, u32[]{:S(2)}) async-start(f32[16,1,2]{2,1,0:T(1,128)} %broadcast_in_dim.16), calls=%async_computation.5 | async-start | bytes 16384 | tf_op jit(solution)/shard_map/all_to_all | solution.py:35
  465.8 19.8 %all-to-all-start.6 = ((f32[32,1,2]{2,1,0:T(1,128)}), f32[32,1,2]{2,1,0:T(1,128)S(1)}, u32[]{:S(2)}, u32[]{:S(2)}) async-start(f32[32,1,2]{2,1,0:T(1,128)} %broadcast_in_dim.17), calls=%async_computation.6 | async-start | bytes 32768 | tf_op jit(solution)/shard_map/all_to_all | solution.py:35
  (4 other events, 17.6 us)

commit v6 on v5

--- a/solution.py
+++ b/solution.py
@@ -56,7 +56,16 @@
     geno = genotypes.astype(jnp.float32).reshape(rows, quarter, width // quarter).transpose(1, 0, 2)
     seen = observed.astype(jnp.float32).reshape(rows, quarter, width // quarter).transpose(1, 0, 2)
     counts = jnp.stack([seen * geno, seen * (2.0 - geno)], axis=1)
-    counts = lax.all_to_all(counts, "yh", 0, 0, tiled=True)
+    me = lax.axis_index("yh")
+    arrived = [lax.dynamic_index_in_dim(counts, me, 0, keepdims=False)]
+    for shift in range(1, quarter):
+        outgoing = lax.dynamic_index_in_dim(counts, (me + shift) % quarter, 0, keepdims=False)
+        pairs = [(j, (j + shift) % quarter) for j in range(quarter)]
+        arrived.append(lax.ppermute(outgoing, "yh", pairs))
+    arrived = jnp.stack(arrived)
+    counts = jnp.stack(
+        [lax.dynamic_index_in_dim(arrived, (me - src) % quarter, 0, keepdims=False) for src in range(quarter)]
+    )
     hits = counts[:, 0].reshape(quarter * rows, width // quarter)
     misses = counts[:, 1].reshape(quarter * rows, width // quarter)
     own_rows = ancestry.shape[0]

time: 493 us -> 492 us (level)
  waiting for transfers between devices: 125 us -> 131 us
  starting transfers between devices: 283 us -> 278 us
    ppermute x0 -> x3, starting transfers between devices: none -> 13 us  [per_device(): arrived.append(lax.ppermute(outgoing, 'yh', pairs))]
    ppermute x54, starting transfers between devices: 202 us -> 190 us  [doubling_sum(): value = value + lax.ppermute(value, name, pairs)]
    all_to_all x1 -> x0, starting transfers between devices: 7.77 us -> none  [per_device(): counts = lax.all_to_all(counts, 'yh', 0, 0, tiled=True)]
    ppermute x6, waiting for transfers between devices: 6.57 us -> 0.02 us  [doubling_gather(): other = lax.ppermute(value, name, pairs)]
    ppermute x0 -> x3, waiting for transfers between devices: none -> 6.18 us  [per_device(): arrived.append(lax.ppermute(outgoing, 'yh', pairs))]
    ppermute x54, waiting for transfers between devices: 85.6 us -> 91.5 us  [doubling_sum(): value = value + lax.ppermute(value, name, pairs)]
  transfers between devices with their start and end apart: 65 -> 67, of which waited for: 39 -> 38; matrix products, arithmetic and copies ran while one was open for 3% -> 3% of each run, Pallas kernels for 0% -> 0%
where the time goes in v6:
time: 492 us; the launch traced here: 490 us
  starting transfers between devices  278 us (57%)
  waiting for transfers between devices  131 us (27%)
  blocking collectives  27.4 us (6%)
  other arithmetic  19.2 us (4%)
  matrix products  16.2 us (3%)
  between operations  9.97 us (2%)
  local copies, waits for them, and re-layouts  7.74 us (2%)
    ppermute x54, starting transfers between devices, doubling_sum(): value = value + lax.ppermute(value, name, pairs)  190 us
    ppermute x54, waiting for transfers between devices, doubling_sum(): value = value + lax.ppermute(value, name, pairs)  91.5 us
    all_to_all x4, starting transfers between devices, group_total(): gathered = lax.all_to_all(spread, axes, 0, 0, tiled=True)  46.1 us
    all_to_all x4, waiting for transfers between devices, group_total(): gathered = lax.all_to_all(spread, axes, 0, 0, tiled=True)  33 us
    ppermute x6, starting transfers between devices, doubling_gather(): other = lax.ppermute(value, name, pairs)  29.6 us
    all_to_all x2, blocking collectives, group_total(): gathered = lax.all_to_all(spread, axes, 0, 0, tiled=True)  27.4 us
    ppermute x3, starting transfers between devices, per_device(): arrived.append(lax.ppermute(outgoing, 'yh', pairs))  13 us
  transfers between devices with their start and end apart: 67, of which 38 were waited for; matrix products, arithmetic and copies ran while one was open for 3% of the time, Pallas kernels for 0%

profile of v6, /device:TPU:1, one launch (start us, length us, event | category | flops | bytes accessed | tf_op | source)
XLA Modules:
  0.0 489.5 jit_solution(2018435164111699993)
XLA Ops:
  1.4 4.8 collective-permute-start.5
  6.3 4.3 collective-permute-start
  12.1 5.8 %collective-permute-start.6 = (f32[64,32]{0,1:T(8,128)S(1)}, f32[64,32]{0,1:T(8,128)S(1)}, u32[]{:S(2)}, u32[]{:S(2)}) collective-permute-start(f32[64,32]{0,1:T(8,128)S(1)} %maximum_select_fusion.4), channel_id=1, source_target_pairs={{0,16},{8,24},{16,0},{24,8},{32,48},{40,56},{48,32},{56,40},{1,17}... | collective-permute-start | bytes 24584 | tf_op jit(solution)/shard_map/ppermute | solution.py:46
  20.0 7.5 %collective-permute-start.3 = (f32[2,64,512]{2,1,0:T(8,128)S(1)}, f32[2,64,512]{2,1,0:T(8,128)S(1)}, u32[]{:S(2)}, u32[]{:S(2)}) collective-permute-start(f32[2,64,512]{2,1,0:T(8,128)S(1)} %get-tuple-element.48), channel_id=1, source_target_pairs={{0,256},{128,384},{256,0},{384,128},{1,257},{129,385},{257,1},{385... | collective-permute-start | bytes 786440 | tf_op jit(solution)/shard_map/ppermute | solution.py:64
  27.4 3.6 collective-permute-start.4
  31.4 7.9 %collective-permute-start.7 = (f32[128,32]{0,1:T(8,128)S(1)}, f32[128,32]{0,1:T(8,128)S(1)}, u32[]{:S(2)}, u32[]{:S(2)}) collective-permute-start(f32[128,32]{0,1:T(8,128)S(1)} %maximum_select_fusion.5), channel_id=1, source_target_pairs={{0,32},{8,40},{16,48},{24,56},{32,0},{40,8},{48,16},{56,24},{1,33}... | collective-permute-start | bytes 49160 | tf_op jit(solution)/shard_map/ppermute | solution.py:46
  39.4 3.5 collective-permute-start.1
  42.9 3.2 collective-permute-start.8
  46.2 6.2 %collective-permute-done.4 = f32[2,64,512]{2,1,0:T(8,128)S(1)} collective-permute-done((f32[2,64,512]{2,1,0:T(8,128)S(1)}, f32[2,64,512]{2,1,0:T(8,128)S(1)}, u32[]{:S(2)}, u32[]{:S(2)}) %collective-permute-start.4) | collective-permute-done | bytes 262176 | tf_op jit(solution)/shard_map/ppermute | solution.py:64
  57.4 5.7 %collective-permute-start.9 = (f32[256,32]{0,1:T(8,128)S(1)}, f32[256,32]{0,1:T(8,128)S(1)}, u32[]{:S(2)}, u32[]{:S(2)}) collective-permute-start(f32[256,32]{0,1:T(8,128)S(1)} %convolution_add_fusion.5), channel_id=1, source_target_pairs={{0,1},{1,0},{2,3},{3,2},{4,5},{5,4},{6,7},{7,6},{8,9},{9,8},{10,11... | collective-permute-start | bytes 98312 | tf_op jit(solution)/shard_map/ppermute | solution.py:25
  65.1 3.1 collective-permute-start.10
  70.1 4.6 collective-permute-start.11
  76.2 3.6 collective-permute-start.12
  81.8 4.3 collective-permute-start.13
  90.4 4.1 collective-permute-done.16
  94.5 6.9 %collective-permute-start.17 = (f32[512,64]{0,1:T(8,128)S(1)}, f32[512,64]{0,1:T(8,128)S(1)}, u32[]{:S(2)}, u32[]{:S(2)}) collective-permute-start(f32[512,64]{0,1:T(8,128)S(1)} %add.394), channel_id=1, source_target_pairs={{0,32},{8,40},{16,48},{24,56},{32,0},{40,8},{48,16},{56,24},{1,33}... | collective-permute-start | bytes 393224 | tf_op jit(solution)/shard_map/ppermute | solution.py:25
  109.8 9.6 %collective-permute-start.18 = (f32[256,32]{0,1:T(8,128)S(1)}, f32[256,32]{0,1:T(8,128)S(1)}, u32[]{:S(2)}, u32[]{:S(2)}) collective-permute-start(f32[256,32]{0,1:T(8,128)S(1)} %convolution_add_fusion.4), channel_id=1, source_target_pairs={{0,1},{1,0},{2,3},{3,2},{4,5},{5,4},{6,7},{7,6},{8,9},{9,8},{10,11... | collective-permute-start | bytes 98312 | tf_op jit(solution)/shard_map/ppermute | solution.py:25
  119.5 3.0 collective-permute-start.24
  122.5 3.1 collective-permute-start.19
  127.5 4.7 collective-permute-start.20
  133.6 3.2 collective-permute-start.21
  139.2 4.9 collective-permute-start.22
  148.3 3.6 collective-permute-done.25
  151.9 4.3 collective-permute-start.26
  158.1 12.7 %all_to_all.36 = f32[16,1,2]{2,1,0:T(1,128)S(1)} all-to-all(f32[16,1,2]{2,1,0:T(1,128)S(1)} %broadcast_in_dim.12), channel_id=1, replica_groups=mesh['yh'=4,'yl'=2,'z'=8,'x'=4,'c'=2] {'yl','z'}, dimensions={0} | all-to-all | bytes 256 | tf_op jit(solution)/shard_map/all_to_all | solution.py:35
  173.5 17.2 %all-to-all-start.1 = ((f32[32,1,2]{2,1,0:T(1,128)}), f32[32,1,2]{2,1,0:T(1,128)S(1)}, u32[]{:S(2)}, u32[]{:S(2)}) async-start(f32[32,1,2]{2,1,0:T(1,128)} %broadcast_in_dim.13), calls=%async_computation.1 | async-start | bytes 32768 | tf_op jit(solution)/shard_map/all_to_all | solution.py:35
  191.3 8.6 %all-to-all-done.1 = f32[32,1,2]{2,1,0:T(1,128)S(1)} async-done(((f32[32,1,2]{2,1,0:T(1,128)}), f32[32,1,2]{2,1,0:T(1,128)S(1)}, u32[]{:S(2)}, u32[]{:S(2)}) %all-to-all-start.1) | async-done | bytes 288 | tf_op jit(solution)/shard_map/all_to_all | solution.py:35
  208.1 2.9 collective-permute-start.27
  218.8 2.8 collective-permute-start.29
  221.6 3.3 collective-permute-done.29
  227.1 3.4 collective-permute-done.30
  235.0 4.0 collective-permute-done.31
  240.8 3.3 collective-permute-start.35
  244.2 6.4 %collective-permute-done.35 = f32[512,64]{0,1:T(8,128)S(1)} collective-permute-done((f32[512,64]{0,1:T(8,128)S(1)}, f32[512,64]{0,1:T(8,128)S(1)}, u32[]{:S(2)}, u32[]{:S(2)}) %collective-permute-start.35) | collective-permute-done | bytes 131104 | tf_op jit(solution)/shard_map/ppermute | solution.py:25
  253.4 2.8 collective-permute-start.41
  256.8 10.2 %collective-permute-start.36 = (f32[256,32]{0,1:T(8,128)S(1)}, f32[256,32]{0,1:T(8,128)S(1)}, u32[]{:S(2)}, u32[]{:S(2)}) collective-permute-start(f32[256,32]{0,1:T(8,128)S(1)} %convolution_add_fusion.2), channel_id=1, source_target_pairs={{0,1},{1,0},{2,3},{3,2},{4,5},{5,4},{6,7},{7,6},{8,9},{9,8},{10,11... | collective-permute-start | bytes 98312 | tf_op jit(solution)/shard_map/ppermute | solution.py:25
  276.4 3.5 collective-permute-done.38
  279.8 3.8 collective-permute-start.39
  285.4 6.9 %collective-permute-start.40 = (f32[256,32]{0,1:T(8,128)S(1)}, f32[256,32]{0,1:T(8,128)S(1)}, u32[]{:S(2)}, u32[]{:S(2)}) collective-permute-start(f32[256,32]{0,1:T(8,128)S(1)} %add.430), channel_id=1, source_target_pairs={{0,256},{128,384},{256,0},{384,128},{1,257},{129,385},{257,1},{385... | collective-permute-start | bytes 98312 | tf_op jit(solution)/shard_map/ppermute | solution.py:25
  292.3 3.0 collective-permute-start.43
  296.0 3.3 collective-permute-done.43
  299.3 3.5 collective-permute-start.44
  304.7 14.7 %all_to_all.37 = f32[16,1,2]{2,1,0:T(1,128)S(1)} all-to-all(f32[16,1,2]{2,1,0:T(1,128)S(1)} %broadcast_in_dim.14), channel_id=1, replica_groups=mesh['yh'=4,'yl'=2,'z'=8,'x'=4,'c'=2] {'yl','z'}, dimensions={0} | all-to-all | bytes 256 | tf_op jit(solution)/shard_map/all_to_all | solution.py:35
  322.1 10.6 %all-to-all-start.3 = ((f32[32,1,2]{2,1,0:T(1,128)}), f32[32,1,2]{2,1,0:T(1,128)S(1)}, u32[]{:S(2)}, u32[]{:S(2)}) async-start(f32[32,1,2]{2,1,0:T(1,128)} %broadcast_in_dim.15), calls=%async_computation.3 | async-start | bytes 32768 | tf_op jit(solution)/shard_map/all_to_all | solution.py:35
  333.4 8.6 %all-to-all-done.3 = f32[32,1,2]{2,1,0:T(1,128)S(1)} async-done(((f32[32,1,2]{2,1,0:T(1,128)}), f32[32,1,2]{2,1,0:T(1,128)S(1)}, u32[]{:S(2)}, u32[]{:S(2)}) %all-to-all-start.3) | async-done | bytes 288 | tf_op jit(solution)/shard_map/all_to_all | solution.py:35
  350.2 2.9 collective-permute-start.45
  360.8 2.9 collective-permute-start.47
  363.7 3.3 collective-permute-done.47
  369.2 3.3 collective-permute-done.48
  377.1 4.1 collective-permute-done.49
  383.0 3.1 collective-permute-start.53
  386.1 6.6 %collective-permute-done.53 = f32[512,64]{0,1:T(8,128)S(1)} collective-permute-done((f32[512,64]{0,1:T(8,128)S(1)}, f32[512,64]{0,1:T(8,128)S(1)}, u32[]{:S(2)}, u32[]{:S(2)}) %collective-permute-start.53) | collective-permute-done | bytes 131104 | tf_op jit(solution)/shard_map/ppermute | solution.py:25
  395.5 2.8 collective-permute-start.59
  398.9 10.3 %collective-permute-start.54 = (f32[256,32]{0,1:T(8,128)S(1)}, f32[256,32]{0,1:T(8,128)S(1)}, u32[]{:S(2)}, u32[]{:S(2)}) collective-permute-start(f32[256,32]{0,1:T(8,128)S(1)} %convolution_add_fusion), channel_id=1, source_target_pairs={{0,1},{1,0},{2,3},{3,2},{4,5},{5,4},{6,7},{7,6},{8,9},{9,8},{10,11... | collective-permute-start | bytes 98312 | tf_op jit(solution)/shard_map/ppermute | solution.py:25
  418.5 3.5 collective-permute-done.56
  421.9 3.8 collective-permute-start.57
  427.5 6.9 %collective-permute-start.58 = (f32[256,32]{0,1:T(8,128)S(1)}, f32[256,32]{0,1:T(8,128)S(1)}, u32[]{:S(2)}, u32[]{:S(2)}) collective-permute-start(f32[256,32]{0,1:T(8,128)S(1)} %add.459), channel_id=1, source_target_pairs={{0,256},{128,384},{256,0},{384,128},{1,257},{129,385},{257,1},{385... | collective-permute-start | bytes 98312 | tf_op jit(solution)/shard_map/ppermute | solution.py:25
  434.4 3.0 collective-permute-start.61
  438.1 3.2 collective-permute-done.61
  441.3 3.5 collective-permute-start.62
  447.4 7.7 %all-to-all-start.4 = ((f32[16,1,2]{2,1,0:T(1,128)}), f32[16,1,2]{2,1,0:T(1,128)S(1)}, u32[]{:S(2)}, u32[]{:S(2)}) async-start(f32[16,1,2]{2,1,0:T(1,128)} %broadcast_in_dim.16), calls=%async_computation.4 | async-start | bytes 16384 | tf_op jit(solution)/shard_map/all_to_all | solution.py:35
  455.0 7.2 %all-to-all-done.4 = f32[16,1,2]{2,1,0:T(1,128)S(1)} async-done(((f32[16,1,2]{2,1,0:T(1,128)}), f32[16,1,2]{2,1,0:T(1,128)S(1)}, u32[]{:S(2)}, u32[]{:S(2)}) %all-to-all-start.4) | async-done | bytes 160 | tf_op jit(solution)/shard_map/all_to_all | solution.py:35
  465.0 10.6 %all-to-all-start.5 = ((f32[32,1,2]{2,1,0:T(1,128)}), f32[32,1,2]{2,1,0:T(1,128)S(1)}, u32[]{:S(2)}, u32[]{:S(2)}) async-start(f32[32,1,2]{2,1,0:T(1,128)} %broadcast_in_dim.17), calls=%async_computation.5 | async-start | bytes 32768 | tf_op jit(solution)/shard_map/all_to_all | solution.py:35
  476.2 8.6 %all-to-all-done.5 = f32[32,1,2]{2,1,0:T(1,128)S(1)} async-done(((f32[32,1,2]{2,1,0:T(1,128)}), f32[32,1,2]{2,1,0:T(1,128)S(1)}, u32[]{:S(2)}, u32[]{:S(2)}) %all-to-all-start.5) | async-done | bytes 288 | tf_op jit(solution)/shard_map/all_to_all | solution.py:35
  (226 shorter events, 131.2 us)
Async XLA Ops:
  1.4 10.6 %collective-permute-start.5 = (f32[32,32]{0,1:T(8,128)S(1)}, f32[32,32]{0,1:T(8,128)S(1)}, u32[]{:S(2)}, u32[]{:S(2)}) collective-permute-start(f32[32,32]{0,1:T(8,128)S(1)} %copy.20), channel_id=1, source_target_pairs={{0,8},{8,0},{16,24},{24,16},{32,40},{40,32},{48,56},{56,48},{1,9},... | collective-permute-start | bytes 12296 | tf_op jit(solution)/shard_map/ppermute | solution.py:46
  6.3 33.0 %collective-permute-start = (f32[64,32]{0,1:T(8,128)S(1)}, f32[64,32]{0,1:T(8,128)S(1)}, u32[]{:S(2)}, u32[]{:S(2)}) collective-permute-start(f32[64,32]{0,1:T(8,128)S(1)} %broadcast_divide_fusion.5), channel_id=1, source_target_pairs={{0,128},{128,0},{256,384},{384,256},{1,129},{129,1},{257,385},{385... | collective-permute-start | bytes 24584 | tf_op jit(solution)/shard_map/ppermute | solution.py:46
  12.1 19.2 %collective-permute-start.6 = (f32[64,32]{0,1:T(8,128)S(1)}, f32[64,32]{0,1:T(8,128)S(1)}, u32[]{:S(2)}, u32[]{:S(2)}) collective-permute-start(f32[64,32]{0,1:T(8,128)S(1)} %maximum_select_fusion.4), channel_id=1, source_target_pairs={{0,16},{8,24},{16,0},{24,8},{32,48},{40,56},{48,32},{56,40},{1,17}... | collective-permute-start | bytes 24584 | tf_op jit(solution)/shard_map/ppermute | solution.py:46
  18.0 28.1 %collective-permute-start.2 = (f32[2,64,512]{2,1,0:T(8,128)S(1)}, f32[2,64,512]{2,1,0:T(8,128)S(1)}, u32[]{:S(2)}, u32[]{:S(2)}) collective-permute-start(f32[2,64,512]{2,1,0:T(8,128)S(1)} %get-tuple-element.47), channel_id=1, source_target_pairs={{0,128},{128,256},{256,384},{384,0},{1,129},{129,257},{257,385},{3... | collective-permute-start | bytes 786440 | tf_op jit(solution)/shard_map/ppermute | solution.py:64
  20.0 26.2 %collective-permute-start.3 = (f32[2,64,512]{2,1,0:T(8,128)S(1)}, f32[2,64,512]{2,1,0:T(8,128)S(1)}, u32[]{:S(2)}, u32[]{:S(2)}) collective-permute-start(f32[2,64,512]{2,1,0:T(8,128)S(1)} %get-tuple-element.48), channel_id=1, source_target_pairs={{0,256},{128,384},{256,0},{384,128},{1,257},{129,385},{257,1},{385... | collective-permute-start | bytes 786440 | tf_op jit(solution)/shard_map/ppermute | solution.py:64
  27.4 24.9 %collective-permute-start.4 = (f32[2,64,512]{2,1,0:T(8,128)S(1)}, f32[2,64,512]{2,1,0:T(8,128)S(1)}, u32[]{:S(2)}, u32[]{:S(2)}) collective-permute-start(f32[2,64,512]{2,1,0:T(8,128)S(1)} %get-tuple-element.49), channel_id=1, source_target_pairs={{0,384},{128,0},{256,128},{384,256},{1,385},{129,1},{257,129},{385... | collective-permute-start | bytes 786440 | tf_op jit(solution)/shard_map/ppermute | solution.py:64
  31.4 11.6 %collective-permute-start.7 = (f32[128,32]{0,1:T(8,128)S(1)}, f32[128,32]{0,1:T(8,128)S(1)}, u32[]{:S(2)}, u32[]{:S(2)}) collective-permute-start(f32[128,32]{0,1:T(8,128)S(1)} %maximum_select_fusion.5), channel_id=1, source_target_pairs={{0,32},{8,40},{16,48},{24,56},{32,0},{40,8},{48,16},{56,24},{1,33}... | collective-permute-start | bytes 49160 | tf_op jit(solution)/shard_map/ppermute | solution.py:46
  39.4 13.4 %collective-permute-start.1 = (f32[128,32]{0,1:T(8,128)S(1)}, f32[128,32]{0,1:T(8,128)S(1)}, u32[]{:S(2)}, u32[]{:S(2)}) collective-permute-start(f32[128,32]{0,1:T(8,128)S(1)} %maximum_select_fusion.3), channel_id=1, source_target_pairs={{0,256},{128,384},{256,0},{384,128},{1,257},{129,385},{257,1},{385... | collective-permute-start | bytes 49160 | tf_op jit(solution)/shard_map/ppermute | solution.py:46
  42.9 9.8 %collective-permute-start.8 = (f32[256,32]{0,1:T(8,128)S(1)}, f32[256,32]{0,1:T(8,128)S(1)}, u32[]{:S(2)}, u32[]{:S(2)}) collective-permute-start(f32[256,32]{0,1:T(8,128)S(1)} %maximum_select_fusion.2), channel_id=1, source_target_pairs={{0,64},{64,0},{1,65},{65,1},{2,66},{66,2},{3,67},{67,3},{4,68},{68... | collective-permute-start | bytes 98312 | tf_op jit(solution)/shard_map/ppermute | solution.py:46
  54.4 8.8 %collective-permute-start.14 = (f32[512,64]{0,1:T(8,128)S(1)}, f32[512,64]{0,1:T(8,128)S(1)}, u32[]{:S(2)}, u32[]{:S(2)}) collective-permute-start(f32[512,64]{0,1:T(8,128)S(1)} %pad_maximum_fusion.2), channel_id=1, source_target_pairs={{0,64},{64,0},{1,65},{65,1},{2,66},{66,2},{3,67},{67,3},{4,68},{68... | collective-permute-start | bytes 393224 | tf_op jit(solution)/shard_map/ppermute | solution.py:25
  57.4 7.7 %collective-permute-start.9 = (f32[256,32]{0,1:T(8,128)S(1)}, f32[256,32]{0,1:T(8,128)S(1)}, u32[]{:S(2)}, u32[]{:S(2)}) collective-permute-start(f32[256,32]{0,1:T(8,128)S(1)} %convolution_add_fusion.5), channel_id=1, source_target_pairs={{0,1},{1,0},{2,3},{3,2},{4,5},{5,4},{6,7},{7,6},{8,9},{9,8},{10,11... | collective-permute-start | bytes 98312 | tf_op jit(solution)/shard_map/ppermute | solution.py:25
  63.2 22.9 %collective-permute-start.15 = (f32[512,64]{0,1:T(8,128)S(1)}, f32[512,64]{0,1:T(8,128)S(1)}, u32[]{:S(2)}, u32[]{:S(2)}) collective-permute-start(f32[512,64]{0,1:T(8,128)S(1)} %fusion.53), channel_id=1, source_target_pairs={{0,8},{8,0},{16,24},{24,16},{32,40},{40,32},{48,56},{56,48},{1,9},... | collective-permute-start | bytes 393224 | tf_op jit(solution)/shard_map/ppermute | solution.py:25
  65.1 5.0 %collective-permute-start.10 = (f32[256,32]{0,1:T(8,128)S(1)}, f32[256,32]{0,1:T(8,128)S(1)}, u32[]{:S(2)}, u32[]{:S(2)}) collective-permute-start(f32[256,32]{0,1:T(8,128)S(1)} %add.387), channel_id=1, source_target_pairs={{0,2},{2,0},{4,6},{6,4},{1,3},{3,1},{5,7},{7,5},{8,10},{10,8},{12,... | collective-permute-start | bytes 98312 | tf_op jit(solution)/shard_map/ppermute | solution.py:25
  70.1 6.2 %collective-permute-start.11 = (f32[256,32]{0,1:T(8,128)S(1)}, f32[256,32]{0,1:T(8,128)S(1)}, u32[]{:S(2)}, u32[]{:S(2)}) collective-permute-start(f32[256,32]{0,1:T(8,128)S(1)} %add.388), channel_id=1, source_target_pairs={{0,4},{2,6},{4,0},{6,2},{1,5},{3,7},{5,1},{7,3},{8,12},{10,14},{12... | collective-permute-start | bytes 98312 | tf_op jit(solution)/shard_map/ppermute | solution.py:25
  76.2 5.5 %collective-permute-start.12 = (f32[256,32]{0,1:T(8,128)S(1)}, f32[256,32]{0,1:T(8,128)S(1)}, u32[]{:S(2)}, u32[]{:S(2)}) collective-permute-start(f32[256,32]{0,1:T(8,128)S(1)} %add.389), channel_id=1, source_target_pairs={{0,128},{128,0},{256,384},{384,256},{1,129},{129,1},{257,385},{385... | collective-permute-start | bytes 98312 | tf_op jit(solution)/shard_map/ppermute | solution.py:25
  81.8 8.6 %collective-permute-start.13 = (f32[256,32]{0,1:T(8,128)S(1)}, f32[256,32]{0,1:T(8,128)S(1)}, u32[]{:S(2)}, u32[]{:S(2)}) collective-permute-start(f32[256,32]{0,1:T(8,128)S(1)} %add.390), channel_id=1, source_target_pairs={{0,256},{128,384},{256,0},{384,128},{1,257},{129,385},{257,1},{385... | collective-permute-start | bytes 98312 | tf_op jit(solution)/shard_map/ppermute | solution.py:25
  86.2 8.3 %collective-permute-start.16 = (f32[512,64]{0,1:T(8,128)S(1)}, f32[512,64]{0,1:T(8,128)S(1)}, u32[]{:S(2)}, u32[]{:S(2)}) collective-permute-start(f32[512,64]{0,1:T(8,128)S(1)} %add.393), channel_id=1, source_target_pairs={{0,16},{8,24},{16,0},{24,8},{32,48},{40,56},{48,32},{56,40},{1,17}... | collective-permute-start | bytes 393224 | tf_op jit(solution)/shard_map/ppermute | solution.py:25
  94.5 9.6 %collective-permute-start.17 = (f32[512,64]{0,1:T(8,128)S(1)}, f32[512,64]{0,1:T(8,128)S(1)}, u32[]{:S(2)}, u32[]{:S(2)}) collective-permute-start(f32[512,64]{0,1:T(8,128)S(1)} %add.394), channel_id=1, source_target_pairs={{0,32},{8,40},{16,48},{24,56},{32,0},{40,8},{48,16},{56,24},{1,33}... | collective-permute-start | bytes 393224 | tf_op jit(solution)/shard_map/ppermute | solution.py:25
  106.9 12.5 %collective-permute-start.23 = (f32[512,64]{0,1:T(8,128)S(1)}, f32[512,64]{0,1:T(8,128)S(1)}, u32[]{:S(2)}, u32[]{:S(2)}) collective-permute-start(f32[512,64]{0,1:T(8,128)S(1)} %pad_maximum_fusion.3), channel_id=1, source_target_pairs={{0,64},{64,0},{1,65},{65,1},{2,66},{66,2},{3,67},{67,3},{4,68},{68... | collective-permute-start | bytes 393224 | tf_op jit(solution)/shard_map/ppermute | solution.py:25
  109.8 12.7 %collective-permute-start.18 = (f32[256,32]{0,1:T(8,128)S(1)}, f32[256,32]{0,1:T(8,128)S(1)}, u32[]{:S(2)}, u32[]{:S(2)}) collective-permute-start(f32[256,32]{0,1:T(8,128)S(1)} %convolution_add_fusion.4), channel_id=1, source_target_pairs={{0,1},{1,0},{2,3},{3,2},{4,5},{5,4},{6,7},{7,6},{8,9},{9,8},{10,11... | collective-permute-start | bytes 98312 | tf_op jit(solution)/shard_map/ppermute | solution.py:25
  119.5 24.6 %collective-permute-start.24 = (f32[512,64]{0,1:T(8,128)S(1)}, f32[512,64]{0,1:T(8,128)S(1)}, u32[]{:S(2)}, u32[]{:S(2)}) collective-permute-start(f32[512,64]{0,1:T(8,128)S(1)} %fusion.52), channel_id=1, source_target_pairs={{0,8},{8,0},{16,24},{24,16},{32,40},{40,32},{48,56},{56,48},{1,9},... | collective-permute-start | bytes 393224 | tf_op jit(solution)/shard_map/ppermute | solution.py:25
  122.5 5.0 %collective-permute-start.19 = (f32[256,32]{0,1:T(8,128)S(1)}, f32[256,32]{0,1:T(8,128)S(1)}, u32[]{:S(2)}, u32[]{:S(2)}) collective-permute-start(f32[256,32]{0,1:T(8,128)S(1)} %add.398), channel_id=1, source_target_pairs={{0,2},{2,0},{4,6},{6,4},{1,3},{3,1},{5,7},{7,5},{8,10},{10,8},{12,... | collective-permute-start | bytes 98312 | tf_op jit(solution)/shard_map/ppermute | solution.py:25
  127.5 6.2 %collective-permute-start.20 = (f32[256,32]{0,1:T(8,128)S(1)}, f32[256,32]{0,1:T(8,128)S(1)}, u32[]{:S(2)}, u32[]{:S(2)}) collective-permute-start(f32[256,32]{0,1:T(8,128)S(1)} %add.399), channel_id=1, source_target_pairs={{0,4},{2,6},{4,0},{6,2},{1,5},{3,7},{5,1},{7,3},{8,12},{10,14},{12... | collective-permute-start | bytes 98312 | tf_op jit(solution)/shard_map/ppermute | solution.py:25
  133.6 5.5 %collective-permute-start.21 = (f32[256,32]{0,1:T(8,128)S(1)}, f32[256,32]{0,1:T(8,128)S(1)}, u32[]{:S(2)}, u32[]{:S(2)}) collective-permute-start(f32[256,32]{0,1:T(8,128)S(1)} %add.400), channel_id=1, source_target_pairs={{0,128},{128,0},{256,384},{384,256},{1,129},{129,1},{257,385},{385... | collective-permute-start | bytes 98312 | tf_op jit(solution)/shard_map/ppermute | solution.py:25
  139.2 8.6 %collective-permute-start.22 = (f32[256,32]{0,1:T(8,128)S(1)}, f32[256,32]{0,1:T(8,128)S(1)}, u32[]{:S(2)}, u32[]{:S(2)}) collective-permute-start(f32[256,32]{0,1:T(8,128)S(1)} %add.401), channel_id=1, source_target_pairs={{0,256},{128,384},{256,0},{384,128},{1,257},{129,385},{257,1},{385... | collective-permute-start | bytes 98312 | tf_op jit(solution)/shard_map/ppermute | solution.py:25
  144.1 7.8 %collective-permute-start.25 = (f32[512,64]{0,1:T(8,128)S(1)}, f32[512,64]{0,1:T(8,128)S(1)}, u32[]{:S(2)}, u32[]{:S(2)}) collective-permute-start(f32[512,64]{0,1:T(8,128)S(1)} %add.405), channel_id=1, source_target_pairs={{0,16},{8,24},{16,0},{24,8},{32,48},{40,56},{48,32},{56,40},{1,17}... | collective-permute-start | bytes 393224 | tf_op jit(solution)/shard_map/ppermute | solution.py:25
  151.9 18.9 %collective-permute-start.26 = (f32[512,64]{0,1:T(8,128)S(1)}, f32[512,64]{0,1:T(8,128)S(1)}, u32[]{:S(2)}, u32[]{:S(2)}) collective-permute-start(f32[512,64]{0,1:T(8,128)S(1)} %add.406), channel_id=1, source_target_pairs={{0,32},{8,40},{16,48},{24,56},{32,0},{40,8},{48,16},{56,24},{1,33}... | collective-permute-start | bytes 393224 | tf_op jit(solution)/shard_map/ppermute | solution.py:25
  173.5 26.4 %all-to-all-start.1 = ((f32[32,1,2]{2,1,0:T(1,128)}), f32[32,1,2]{2,1,0:T(1,128)S(1)}, u32[]{:S(2)}, u32[]{:S(2)}) async-start(f32[32,1,2]{2,1,0:T(1,128)} %broadcast_in_dim.13), calls=%async_computation.1 | async-start | bytes 32768 | tf_op jit(solution)/shard_map/all_to_all | solution.py:35
  205.3 6.2 %collective-permute-start.32 = (f32[512,64]{0,1:T(8,128)S(1)}, f32[512,64]{0,1:T(8,128)S(1)}, u32[]{:S(2)}, u32[]{:S(2)}) collective-permute-start(f32[512,64]{0,1:T(8,128)S(1)} %pad_maximum_fusion.4), channel_id=1, source_target_pairs={{0,64},{64,0},{1,65},{65,1},{2,66},{66,2},{3,67},{67,3},{4,68},{68... | collective-permute-start | bytes 393224 | tf_op jit(solution)/shard_map/ppermute | solution.py:25
  208.1 5.7 %collective-permute-start.27 = (f32[256,32]{0,1:T(8,128)S(1)}, f32[256,32]{0,1:T(8,128)S(1)}, u32[]{:S(2)}, u32[]{:S(2)}) collective-permute-start(f32[256,32]{0,1:T(8,128)S(1)} %convolution_add_fusion.3), channel_id=1, source_target_pairs={{0,1},{1,0},{2,3},{3,2},{4,5},{5,4},{6,7},{7,6},{8,9},{9,8},{10,11... | collective-permute-start | bytes 98312 | tf_op jit(solution)/shard_map/ppermute | solution.py:25
  211.6 21.2 %collective-permute-start.33 = (f32[512,64]{0,1:T(8,128)S(1)}, f32[512,64]{0,1:T(8,128)S(1)}, u32[]{:S(2)}, u32[]{:S(2)}) collective-permute-start(f32[512,64]{0,1:T(8,128)S(1)} %fusion.51), channel_id=1, source_target_pairs={{0,8},{8,0},{16,24},{24,16},{32,40},{40,32},{48,56},{56,48},{1,9},... | collective-permute-start | bytes 393224 | tf_op jit(solution)/shard_map/ppermute | solution.py:25
  213.8 5.0 %collective-permute-start.28 = (f32[256,32]{0,1:T(8,128)S(1)}, f32[256,32]{0,1:T(8,128)S(1)}, u32[]{:S(2)}, u32[]{:S(2)}) collective-permute-start(f32[256,32]{0,1:T(8,128)S(1)} %add.416), channel_id=1, source_target_pairs={{0,2},{2,0},{4,6},{6,4},{1,3},{3,1},{5,7},{7,5},{8,10},{10,8},{12,... | collective-permute-start | bytes 98312 | tf_op jit(solution)/shard_map/ppermute | solution.py:25
  218.8 6.2 %collective-permute-start.29 = (f32[256,32]{0,1:T(8,128)S(1)}, f32[256,32]{0,1:T(8,128)S(1)}, u32[]{:S(2)}, u32[]{:S(2)}) collective-permute-start(f32[256,32]{0,1:T(8,128)S(1)} %add.417), channel_id=1, source_target_pairs={{0,4},{2,6},{4,0},{6,2},{1,5},{3,7},{5,1},{7,3},{8,12},{10,14},{12... | collective-permute-start | bytes 98312 | tf_op jit(solution)/shard_map/ppermute | solution.py:25
  224.9 5.5 %collective-permute-start.30 = (f32[256,32]{0,1:T(8,128)S(1)}, f32[256,32]{0,1:T(8,128)S(1)}, u32[]{:S(2)}, u32[]{:S(2)}) collective-permute-start(f32[256,32]{0,1:T(8,128)S(1)} %add.418), channel_id=1, source_target_pairs={{0,128},{128,0},{256,384},{384,256},{1,129},{129,1},{257,385},{385... | collective-permute-start | bytes 98312 | tf_op jit(solution)/shard_map/ppermute | solution.py:25
  230.5 8.6 %collective-permute-start.31 = (f32[256,32]{0,1:T(8,128)S(1)}, f32[256,32]{0,1:T(8,128)S(1)}, u32[]{:S(2)}, u32[]{:S(2)}) collective-permute-start(f32[256,32]{0,1:T(8,128)S(1)} %add.419), channel_id=1, source_target_pairs={{0,256},{128,384},{256,0},{384,128},{1,257},{129,385},{257,1},{385... | collective-permute-start | bytes 98312 | tf_op jit(solution)/shard_map/ppermute | solution.py:25
  232.8 8.0 %collective-permute-start.34 = (f32[512,64]{0,1:T(8,128)S(1)}, f32[512,64]{0,1:T(8,128)S(1)}, u32[]{:S(2)}, u32[]{:S(2)}) collective-permute-start(f32[512,64]{0,1:T(8,128)S(1)} %add.422), channel_id=1, source_target_pairs={{0,16},{8,24},{16,0},{24,8},{32,48},{40,56},{48,32},{56,40},{1,17}... | collective-permute-start | bytes 393224 | tf_op jit(solution)/shard_map/ppermute | solution.py:25
  240.8 9.7 %collective-permute-start.35 = (f32[512,64]{0,1:T(8,128)S(1)}, f32[512,64]{0,1:T(8,128)S(1)}, u32[]{:S(2)}, u32[]{:S(2)}) collective-permute-start(f32[512,64]{0,1:T(8,128)S(1)} %add.423), channel_id=1, source_target_pairs={{0,32},{8,40},{16,48},{24,56},{32,0},{40,8},{48,16},{56,24},{1,33}... | collective-permute-start | bytes 393224 | tf_op jit(solution)/shard_map/ppermute | solution.py:25
  253.4 13.6 %collective-permute-start.41 = (f32[512,64]{0,1:T(8,128)S(1)}, f32[512,64]{0,1:T(8,128)S(1)}, u32[]{:S(2)}, u32[]{:S(2)}) collective-permute-start(f32[512,64]{0,1:T(8,128)S(1)} %pad_maximum_fusion.5), channel_id=1, source_target_pairs={{0,64},{64,0},{1,65},{65,1},{2,66},{66,2},{3,67},{67,3},{4,68},{68... | collective-permute-start | bytes 393224 | tf_op jit(solution)/shard_map/ppermute | solution.py:25
  256.8 12.2 %collective-permute-start.36 = (f32[256,32]{0,1:T(8,128)S(1)}, f32[256,32]{0,1:T(8,128)S(1)}, u32[]{:S(2)}, u32[]{:S(2)}) collective-permute-start(f32[256,32]{0,1:T(8,128)S(1)} %convolution_add_fusion.2), channel_id=1, source_target_pairs={{0,1},{1,0},{2,3},{3,2},{4,5},{5,4},{6,7},{7,6},{8,9},{9,8},{10,11... | collective-permute-start | bytes 98312 | tf_op jit(solution)/shard_map/ppermute | solution.py:25
  267.1 25.2 %collective-permute-start.42 = (f32[512,64]{0,1:T(8,128)S(1)}, f32[512,64]{0,1:T(8,128)S(1)}, u32[]{:S(2)}, u32[]{:S(2)}) collective-permute-start(f32[512,64]{0,1:T(8,128)S(1)} %fusion.50), channel_id=1, source_target_pairs={{0,8},{8,0},{16,24},{24,16},{32,40},{40,32},{48,56},{56,48},{1,9},... | collective-permute-start | bytes 393224 | tf_op jit(solution)/shard_map/ppermute | solution.py:25
  273.7 6.2 %collective-permute-start.38 = (f32[256,32]{0,1:T(8,128)S(1)}, f32[256,32]{0,1:T(8,128)S(1)}, u32[]{:S(2)}, u32[]{:S(2)}) collective-permute-start(f32[256,32]{0,1:T(8,128)S(1)} %add.428), channel_id=1, source_target_pairs={{0,4},{2,6},{4,0},{6,2},{1,5},{3,7},{5,1},{7,3},{8,12},{10,14},{12... | collective-permute-start | bytes 98312 | tf_op jit(solution)/shard_map/ppermute | solution.py:25
  279.8 5.5 %collective-permute-start.39 = (f32[256,32]{0,1:T(8,128)S(1)}, f32[256,32]{0,1:T(8,128)S(1)}, u32[]{:S(2)}, u32[]{:S(2)}) collective-permute-start(f32[256,32]{0,1:T(8,128)S(1)} %add.429), channel_id=1, source_target_pairs={{0,128},{128,0},{256,384},{384,256},{1,129},{129,1},{257,385},{385... | collective-permute-start | bytes 98312 | tf_op jit(solution)/shard_map/ppermute | solution.py:25
  285.4 10.0 %collective-permute-start.40 = (f32[256,32]{0,1:T(8,128)S(1)}, f32[256,32]{0,1:T(8,128)S(1)}, u32[]{:S(2)}, u32[]{:S(2)}) collective-permute-start(f32[256,32]{0,1:T(8,128)S(1)} %add.430), channel_id=1, source_target_pairs={{0,256},{128,384},{256,0},{384,128},{1,257},{129,385},{257,1},{385... | collective-permute-start | bytes 98312 | tf_op jit(solution)/shard_map/ppermute | solution.py:25
  292.3 6.9 %collective-permute-start.43 = (f32[512,64]{0,1:T(8,128)S(1)}, f32[512,64]{0,1:T(8,128)S(1)}, u32[]{:S(2)}, u32[]{:S(2)}) collective-permute-start(f32[512,64]{0,1:T(8,128)S(1)} %add.434), channel_id=1, source_target_pairs={{0,16},{8,24},{16,0},{24,8},{32,48},{40,56},{48,32},{56,40},{1,17}... | collective-permute-start | bytes 393224 | tf_op jit(solution)/shard_map/ppermute | solution.py:25
  299.3 20.2 %collective-permute-start.44 = (f32[512,64]{0,1:T(8,128)S(1)}, f32[512,64]{0,1:T(8,128)S(1)}, u32[]{:S(2)}, u32[]{:S(2)}) collective-permute-start(f32[512,64]{0,1:T(8,128)S(1)} %add.435), channel_id=1, source_target_pairs={{0,32},{8,40},{16,48},{24,56},{32,0},{40,8},{48,16},{56,24},{1,33}... | collective-permute-start | bytes 393224 | tf_op jit(solution)/shard_map/ppermute | solution.py:25
  322.1 19.8 %all-to-all-start.3 = ((f32[32,1,2]{2,1,0:T(1,128)}), f32[32,1,2]{2,1,0:T(1,128)S(1)}, u32[]{:S(2)}, u32[]{:S(2)}) async-start(f32[32,1,2]{2,1,0:T(1,128)} %broadcast_in_dim.15), calls=%async_computation.3 | async-start | bytes 32768 | tf_op jit(solution)/shard_map/all_to_all | solution.py:35
  347.4 6.2 %collective-permute-start.50 = (f32[512,64]{0,1:T(8,128)S(1)}, f32[512,64]{0,1:T(8,128)S(1)}, u32[]{:S(2)}, u32[]{:S(2)}) collective-permute-start(f32[512,64]{0,1:T(8,128)S(1)} %pad_maximum_fusion.6), channel_id=1, source_target_pairs={{0,64},{64,0},{1,65},{65,1},{2,66},{66,2},{3,67},{67,3},{4,68},{68... | collective-permute-start | bytes 393224 | tf_op jit(solution)/shard_map/ppermute | solution.py:25
  350.2 5.7 %collective-permute-start.45 = (f32[256,32]{0,1:T(8,128)S(1)}, f32[256,32]{0,1:T(8,128)S(1)}, u32[]{:S(2)}, u32[]{:S(2)}) collective-permute-start(f32[256,32]{0,1:T(8,128)S(1)} %convolution_add_fusion.1), channel_id=1, source_target_pairs={{0,1},{1,0},{2,3},{3,2},{4,5},{5,4},{6,7},{7,6},{8,9},{9,8},{10,11... | collective-permute-start | bytes 98312 | tf_op jit(solution)/shard_map/ppermute | solution.py:25
  353.6 21.2 %collective-permute-start.51 = (f32[512,64]{0,1:T(8,128)S(1)}, f32[512,64]{0,1:T(8,128)S(1)}, u32[]{:S(2)}, u32[]{:S(2)}) collective-permute-start(f32[512,64]{0,1:T(8,128)S(1)} %fusion.49), channel_id=1, source_target_pairs={{0,8},{8,0},{16,24},{24,16},{32,40},{40,32},{48,56},{56,48},{1,9},... | collective-permute-start | bytes 393224 | tf_op jit(solution)/shard_map/ppermute | solution.py:25
  360.8 6.2 %collective-permute-start.47 = (f32[256,32]{0,1:T(8,128)S(1)}, f32[256,32]{0,1:T(8,128)S(1)}, u32[]{:S(2)}, u32[]{:S(2)}) collective-permute-start(f32[256,32]{0,1:T(8,128)S(1)} %add.446), channel_id=1, source_target_pairs={{0,4},{2,6},{4,0},{6,2},{1,5},{3,7},{5,1},{7,3},{8,12},{10,14},{12... | collective-permute-start | bytes 98312 | tf_op jit(solution)/shard_map/ppermute | solution.py:25
  367.0 5.5 %collective-permute-start.48 = (f32[256,32]{0,1:T(8,128)S(1)}, f32[256,32]{0,1:T(8,128)S(1)}, u32[]{:S(2)}, u32[]{:S(2)}) collective-permute-start(f32[256,32]{0,1:T(8,128)S(1)} %add.447), channel_id=1, source_target_pairs={{0,128},{128,0},{256,384},{384,256},{1,129},{129,1},{257,385},{385... | collective-permute-start | bytes 98312 | tf_op jit(solution)/shard_map/ppermute | solution.py:25
  372.6 8.7 %collective-permute-start.49 = (f32[256,32]{0,1:T(8,128)S(1)}, f32[256,32]{0,1:T(8,128)S(1)}, u32[]{:S(2)}, u32[]{:S(2)}) collective-permute-start(f32[256,32]{0,1:T(8,128)S(1)} %add.448), channel_id=1, source_target_pairs={{0,256},{128,384},{256,0},{384,128},{1,257},{129,385},{257,1},{385... | collective-permute-start | bytes 98312 | tf_op jit(solution)/shard_map/ppermute | solution.py:25
  374.9 8.0 %collective-permute-start.52 = (f32[512,64]{0,1:T(8,128)S(1)}, f32[512,64]{0,1:T(8,128)S(1)}, u32[]{:S(2)}, u32[]{:S(2)}) collective-permute-start(f32[512,64]{0,1:T(8,128)S(1)} %add.451), channel_id=1, source_target_pairs={{0,16},{8,24},{16,0},{24,8},{32,48},{40,56},{48,32},{56,40},{1,17}... | collective-permute-start | bytes 393224 | tf_op jit(solution)/shard_map/ppermute | solution.py:25
  383.0 9.7 %collective-permute-start.53 = (f32[512,64]{0,1:T(8,128)S(1)}, f32[512,64]{0,1:T(8,128)S(1)}, u32[]{:S(2)}, u32[]{:S(2)}) collective-permute-start(f32[512,64]{0,1:T(8,128)S(1)} %add.452), channel_id=1, source_target_pairs={{0,32},{8,40},{16,48},{24,56},{32,0},{40,8},{48,16},{56,24},{1,33}... | collective-permute-start | bytes 393224 | tf_op jit(solution)/shard_map/ppermute | solution.py:25
  395.5 13.6 %collective-permute-start.59 = (f32[512,64]{0,1:T(8,128)S(1)}, f32[512,64]{0,1:T(8,128)S(1)}, u32[]{:S(2)}, u32[]{:S(2)}) collective-permute-start(f32[512,64]{0,1:T(8,128)S(1)} %pad_maximum_fusion.7), channel_id=1, source_target_pairs={{0,64},{64,0},{1,65},{65,1},{2,66},{66,2},{3,67},{67,3},{4,68},{68... | collective-permute-start | bytes 393224 | tf_op jit(solution)/shard_map/ppermute | solution.py:25
  398.9 12.2 %collective-permute-start.54 = (f32[256,32]{0,1:T(8,128)S(1)}, f32[256,32]{0,1:T(8,128)S(1)}, u32[]{:S(2)}, u32[]{:S(2)}) collective-permute-start(f32[256,32]{0,1:T(8,128)S(1)} %convolution_add_fusion), channel_id=1, source_target_pairs={{0,1},{1,0},{2,3},{3,2},{4,5},{5,4},{6,7},{7,6},{8,9},{9,8},{10,11... | collective-permute-start | bytes 98312 | tf_op jit(solution)/shard_map/ppermute | solution.py:25
  409.1 25.2 %collective-permute-start.60 = (f32[512,64]{0,1:T(8,128)S(1)}, f32[512,64]{0,1:T(8,128)S(1)}, u32[]{:S(2)}, u32[]{:S(2)}) collective-permute-start(f32[512,64]{0,1:T(8,128)S(1)} %fusion.48), channel_id=1, source_target_pairs={{0,8},{8,0},{16,24},{24,16},{32,40},{40,32},{48,56},{56,48},{1,9},... | collective-permute-start | bytes 393224 | tf_op jit(solution)/shard_map/ppermute | solution.py:25
  415.8 6.2 %collective-permute-start.56 = (f32[256,32]{0,1:T(8,128)S(1)}, f32[256,32]{0,1:T(8,128)S(1)}, u32[]{:S(2)}, u32[]{:S(2)}) collective-permute-start(f32[256,32]{0,1:T(8,128)S(1)} %add.457), channel_id=1, source_target_pairs={{0,4},{2,6},{4,0},{6,2},{1,5},{3,7},{5,1},{7,3},{8,12},{10,14},{12... | collective-permute-start | bytes 98312 | tf_op jit(solution)/shard_map/ppermute | solution.py:25
  421.9 5.5 %collective-permute-start.57 = (f32[256,32]{0,1:T(8,128)S(1)}, f32[256,32]{0,1:T(8,128)S(1)}, u32[]{:S(2)}, u32[]{:S(2)}) collective-permute-start(f32[256,32]{0,1:T(8,128)S(1)} %add.458), channel_id=1, source_target_pairs={{0,128},{128,0},{256,384},{384,256},{1,129},{129,1},{257,385},{385... | collective-permute-start | bytes 98312 | tf_op jit(solution)/shard_map/ppermute | solution.py:25
  427.5 10.0 %collective-permute-start.58 = (f32[256,32]{0,1:T(8,128)S(1)}, f32[256,32]{0,1:T(8,128)S(1)}, u32[]{:S(2)}, u32[]{:S(2)}) collective-permute-start(f32[256,32]{0,1:T(8,128)S(1)} %add.459), channel_id=1, source_target_pairs={{0,256},{128,384},{256,0},{384,128},{1,257},{129,385},{257,1},{385... | collective-permute-start | bytes 98312 | tf_op jit(solution)/shard_map/ppermute | solution.py:25
  434.4 6.9 %collective-permute-start.61 = (f32[512,64]{0,1:T(8,128)S(1)}, f32[512,64]{0,1:T(8,128)S(1)}, u32[]{:S(2)}, u32[]{:S(2)}) collective-permute-start(f32[512,64]{0,1:T(8,128)S(1)} %add.463), channel_id=1, source_target_pairs={{0,16},{8,24},{16,0},{24,8},{32,48},{40,56},{48,32},{56,40},{1,17}... | collective-permute-start | bytes 393224 | tf_op jit(solution)/shard_map/ppermute | solution.py:25
  441.3 21.0 %collective-permute-start.62 = (f32[512,64]{0,1:T(8,128)S(1)}, f32[512,64]{0,1:T(8,128)S(1)}, u32[]{:S(2)}, u32[]{:S(2)}) collective-permute-start(f32[512,64]{0,1:T(8,128)S(1)} %add.464), channel_id=1, source_target_pairs={{0,32},{8,40},{16,48},{24,56},{32,0},{40,8},{48,16},{56,24},{1,33}... | collective-permute-start | bytes 393224 | tf_op jit(solution)/shard_map/ppermute | solution.py:25
  447.4 14.9 %all-to-all-start.4 = ((f32[16,1,2]{2,1,0:T(1,128)}), f32[16,1,2]{2,1,0:T(1,128)S(1)}, u32[]{:S(2)}, u32[]{:S(2)}) async-start(f32[16,1,2]{2,1,0:T(1,128)} %broadcast_in_dim.16), calls=%async_computation.4 | async-start | bytes 16384 | tf_op jit(solution)/shard_map/all_to_all | solution.py:35
  465.0 19.8 %all-to-all-start.5 = ((f32[32,1,2]{2,1,0:T(1,128)}), f32[32,1,2]{2,1,0:T(1,128)S(1)}, u32[]{:S(2)}, u32[]{:S(2)}) async-start(f32[32,1,2]{2,1,0:T(1,128)} %broadcast_in_dim.17), calls=%async_computation.5 | async-start | bytes 32768 | tf_op jit(solution)/shard_map/all_to_all | solution.py:35
  (5 other events, 25.4 us)

commit v7 on v5

--- a/solution.py
+++ b/solution.py
@@ -93,7 +93,7 @@
         rf = f_one - f_zero
         vq = q_two - 2.0 * q_one + q_zero
         vf = f_two - 2.0 * f_one + f_zero
-        q_parts = group_total(jnp.stack([jnp.sum(rq * rq), jnp.sum(vq * vq)]), ROW_GROUP)
+        q_parts = doubling_sum(jnp.stack([jnp.sum(rq * rq), jnp.sum(vq * vq)]), ROW_GROUP)
         f_parts = group_total(jnp.stack([jnp.sum(rf * rf), jnp.sum(vf * vf)]), COL_GROUP)
         first = q_parts[0] + f_parts[0]
         second = q_parts[1] + f_parts[1]

time: 493 us -> 525 us (1.065)
  starting transfers between devices: 283 us -> 331 us
  blocking collectives: 26.2 us -> 0 us
  other arithmetic: 19.9 us -> 28.1 us
    ppermute x54 -> x66, starting transfers between devices: 202 us -> 246 us  [doubling_sum(): value = value + lax.ppermute(value, name, pairs)]
    all_to_all x2 -> x0, blocking collectives: 26.2 us -> none  [group_total(): gathered = lax.all_to_all(spread, axes, 0, 0, tiled=True)]
    ppermute x54 -> x66, waiting for transfers between devices: 85.6 us -> 95.8 us  [doubling_sum(): value = value + lax.ppermute(value, name, pairs)]
    add x48 -> x60, other arithmetic: 0.61 us -> 9.03 us  [doubling_sum(): value = value + lax.ppermute(value, name, pairs)]
    all_to_all x4 -> x3, waiting for transfers between devices: 32.9 us -> 25.8 us  [group_total(): gathered = lax.all_to_all(spread, axes, 0, 0, tiled=True)]
    all_to_all x4 -> x3, starting transfers between devices: 43.9 us -> 47.6 us  [group_total(): gathered = lax.all_to_all(spread, axes, 0, 0, tiled=True)]
  transfers between devices with their start and end apart: 65 -> 76, of which waited for: 39 -> 42; matrix products, arithmetic and copies ran while one was open for 3% -> 4% of each run, Pallas kernels for 0% -> 0%
where the time goes in v7:
time: 525 us; the launch traced here: 522 us
  starting transfers between devices  331 us (63%)
  waiting for transfers between devices  128 us (24%)
  other arithmetic  28.1 us (5%)
  matrix products  16.2 us (3%)
  between operations  10.1 us (2%)
  local copies, waits for them, and re-layouts  8.94 us (2%)
    ppermute x66, starting transfers between devices, doubling_sum(): value = value + lax.ppermute(value, name, pairs)  246 us
    ppermute x66, waiting for transfers between devices, doubling_sum(): value = value + lax.ppermute(value, name, pairs)  95.8 us
    all_to_all x3, starting transfers between devices, group_total(): gathered = lax.all_to_all(spread, axes, 0, 0, tiled=True)  47.6 us
    ppermute x6, starting transfers between devices, doubling_gather(): other = lax.ppermute(value, name, pairs)  29.1 us
    all_to_all x3, waiting for transfers between devices, group_total(): gathered = lax.all_to_all(spread, axes, 0, 0, tiled=True)  25.8 us
  transfers between devices with their start and end apart: 76, of which 42 were waited for; matrix products, arithmetic and copies ran while one was open for 4% of the time, Pallas kernels for 0%

profile of v7, /device:TPU:1, one launch (start us, length us, event | category | flops | bytes accessed | tf_op | source)
XLA Modules:
  0.0 522.4 jit_solution(1404910421370668063)
XLA Ops:
  4.9 7.8 %all-to-all-start = ((f32[4,2,64,512]{3,2,1,0:T(8,128)}), f32[4,2,64,512]{3,2,1,0:T(8,128)S(1)}, u32[]{:S(2)}, u32[]{:S(2)}) async-start(f32[4,2,64,512]{3,2,1,0:T(8,128)} %copy.27), calls=%async_computation | async-start | bytes 2097152 | tf_op jit(solution)/shard_map/all_to_all | solution.py:59
  12.8 4.1 collective-permute-start.2
  18.1 5.8 %collective-permute-start.3 = (f32[64,32]{0,1:T(8,128)S(1)}, f32[64,32]{0,1:T(8,128)S(1)}, u32[]{:S(2)}, u32[]{:S(2)}) collective-permute-start(f32[64,32]{0,1:T(8,128)S(1)} %maximum_select_fusion.4), channel_id=1, source_target_pairs={{0,16},{8,24},{16,0},{24,8},{32,48},{40,56},{48,32},{56,40},{1,17}... | collective-permute-start | bytes 24584 | tf_op jit(solution)/shard_map/ppermute | solution.py:46
  23.9 4.6 collective-permute-start
  28.7 8.2 %collective-permute-start.4 = (f32[128,32]{0,1:T(8,128)S(1)}, f32[128,32]{0,1:T(8,128)S(1)}, u32[]{:S(2)}, u32[]{:S(2)}) collective-permute-start(f32[128,32]{0,1:T(8,128)S(1)} %maximum_select_fusion.5), channel_id=1, source_target_pairs={{0,32},{8,40},{16,48},{24,56},{32,0},{40,8},{48,16},{56,24},{1,33}... | collective-permute-start | bytes 49160 | tf_op jit(solution)/shard_map/ppermute | solution.py:46
  39.5 4.5 collective-permute-start.1
  53.7 4.7 collective-permute-start.6
  58.5 3.8 collective-permute-start.12
  62.4 3.1 collective-permute-start.7
  67.0 4.6 collective-permute-start.8
  73.2 4.4 collective-permute-start.9
  78.9 3.7 collective-permute-start.10
  82.6 5.7 %collective-permute-start.13 = (f32[512,64]{0,1:T(8,128)S(1)}, f32[512,64]{0,1:T(8,128)S(1)}, u32[]{:S(2)}, u32[]{:S(2)}) collective-permute-start(f32[512,64]{0,1:T(8,128)S(1)} %add.353), channel_id=1, source_target_pairs={{0,16},{8,24},{16,0},{24,8},{32,48},{40,56},{48,32},{56,40},{1,17}... | collective-permute-start | bytes 393224 | tf_op jit(solution)/shard_map/ppermute | solution.py:25
  88.4 3.6 collective-permute-done.13
  92.0 8.6 %collective-permute-start.14 = (f32[512,64]{0,1:T(8,128)S(1)}, f32[512,64]{0,1:T(8,128)S(1)}, u32[]{:S(2)}, u32[]{:S(2)}) collective-permute-start(f32[512,64]{0,1:T(8,128)S(1)} %add.354), channel_id=1, source_target_pairs={{0,32},{8,40},{16,48},{24,56},{32,0},{40,8},{48,16},{56,24},{1,33}... | collective-permute-start | bytes 393224 | tf_op jit(solution)/shard_map/ppermute | solution.py:25
  100.6 3.8 collective-permute-done.14
  107.8 9.5 %collective-permute-start.15 = (f32[256,32]{0,1:T(8,128)S(1)}, f32[256,32]{0,1:T(8,128)S(1)}, u32[]{:S(2)}, u32[]{:S(2)}) collective-permute-start(f32[256,32]{0,1:T(8,128)S(1)} %convolution_add_fusion.4), channel_id=1, source_target_pairs={{0,1},{1,0},{2,3},{3,2},{4,5},{5,4},{6,7},{7,6},{8,9},{9,8},{10,11... | collective-permute-start | bytes 98312 | tf_op jit(solution)/shard_map/ppermute | solution.py:25
  119.3 3.1 collective-permute-start.16
  124.3 4.6 collective-permute-start.17
  130.4 3.5 collective-permute-start.18
  136.0 5.3 %collective-permute-start.19 = (f32[256,32]{0,1:T(8,128)S(1)}, f32[256,32]{0,1:T(8,128)S(1)}, u32[]{:S(2)}, u32[]{:S(2)}) collective-permute-start(f32[256,32]{0,1:T(8,128)S(1)} %add.361), channel_id=1, source_target_pairs={{0,256},{128,384},{256,0},{384,128},{1,257},{129,385},{257,1},{385... | collective-permute-start | bytes 98312 | tf_op jit(solution)/shard_map/ppermute | solution.py:25
  147.2 3.1 collective-permute-start.20
  150.3 3.0 collective-permute-start.26
  154.8 3.5 collective-permute-start.21
  158.3 7.5 %collective-permute-start.27 = (f32[512,64]{0,1:T(8,128)S(1)}, f32[512,64]{0,1:T(8,128)S(1)}, u32[]{:S(2)}, u32[]{:S(2)}) collective-permute-start(f32[512,64]{0,1:T(8,128)S(1)} %add.370), channel_id=1, source_target_pairs={{0,32},{8,40},{16,48},{24,56},{32,0},{40,8},{48,16},{56,24},{1,33}... | collective-permute-start | bytes 393224 | tf_op jit(solution)/shard_map/ppermute | solution.py:25
  169.2 3.3 collective-permute-done.22
  174.4 6.2 %collective-permute-done.23 = f32[2]{0:T(128)S(1)} collective-permute-done((f32[2]{0:T(128)S(1)}, f32[2]{0:T(128)S(1)}, u32[]{:S(2)}, u32[]{:S(2)}) %collective-permute-start.23) | collective-permute-done | bytes 40 | tf_op jit(solution)/shard_map/ppermute | solution.py:25
  183.3 17.6 %all-to-all-start.1 = ((f32[32,1,2]{2,1,0:T(1,128)}), f32[32,1,2]{2,1,0:T(1,128)S(1)}, u32[]{:S(2)}, u32[]{:S(2)}) async-start(f32[32,1,2]{2,1,0:T(1,128)} %broadcast_in_dim.6), calls=%async_computation.1 | async-start | bytes 32768 | tf_op jit(solution)/shard_map/all_to_all | solution.py:35
  201.4 8.6 %all-to-all-done.1 = f32[32,1,2]{2,1,0:T(1,128)S(1)} async-done(((f32[32,1,2]{2,1,0:T(1,128)}), f32[32,1,2]{2,1,0:T(1,128)S(1)}, u32[]{:S(2)}, u32[]{:S(2)}) %all-to-all-start.1) | async-done | bytes 288 | tf_op jit(solution)/shard_map/all_to_all | solution.py:35
  218.4 2.9 collective-permute-start.28
  228.7 2.8 collective-permute-start.30
  231.5 3.3 collective-permute-done.30
  237.1 3.3 collective-permute-done.31
  242.7 3.8 collective-permute-start.35
  252.9 8.5 %collective-permute-done.36 = f32[512,64]{0,1:T(8,128)S(1)} collective-permute-done((f32[512,64]{0,1:T(8,128)S(1)}, f32[512,64]{0,1:T(8,128)S(1)}, u32[]{:S(2)}, u32[]{:S(2)}) %collective-permute-start.36) | collective-permute-done | bytes 131104 | tf_op jit(solution)/shard_map/ppermute | solution.py:25
  264.8 9.2 %collective-permute-start.37 = (f32[256,32]{0,1:T(8,128)S(1)}, f32[256,32]{0,1:T(8,128)S(1)}, u32[]{:S(2)}, u32[]{:S(2)}) collective-permute-start(f32[256,32]{0,1:T(8,128)S(1)} %convolution_add_fusion.2), channel_id=1, source_target_pairs={{0,1},{1,0},{2,3},{3,2},{4,5},{5,4},{6,7},{7,6},{8,9},{9,8},{10,11... | collective-permute-start | bytes 98312 | tf_op jit(solution)/shard_map/ppermute | solution.py:25
  283.5 3.6 collective-permute-done.39
  287.1 3.6 collective-permute-start.40
  292.7 6.9 %collective-permute-start.41 = (f32[256,32]{0,1:T(8,128)S(1)}, f32[256,32]{0,1:T(8,128)S(1)}, u32[]{:S(2)}, u32[]{:S(2)}) collective-permute-start(f32[256,32]{0,1:T(8,128)S(1)} %add.394), channel_id=1, source_target_pairs={{0,256},{128,384},{256,0},{384,128},{1,257},{129,385},{257,1},{385... | collective-permute-start | bytes 98312 | tf_op jit(solution)/shard_map/ppermute | solution.py:25
  299.6 2.8 collective-permute-start.47
  305.1 3.0 collective-permute-start.42
  308.1 4.1 collective-permute-start.48
  324.7 7.3 %collective-permute-start.45 = (f32[2]{0:T(128)S(1)}, f32[2]{0:T(128)S(1)}, u32[]{:S(2)}, u32[]{:S(2)}) collective-permute-start(f32[2]{0:T(128)S(1)} %add.399), channel_id=1, source_target_pairs={{0,32},{8,40},{16,48},{24,56},{32,0},{40,8},{48,16},{56,24},{1,33}... | collective-permute-start | bytes 32 | tf_op jit(solution)/shard_map/ppermute | solution.py:25
  335.7 14.9 %all-to-all-start.2 = ((f32[32,1,2]{2,1,0:T(1,128)}), f32[32,1,2]{2,1,0:T(1,128)S(1)}, u32[]{:S(2)}, u32[]{:S(2)}) async-start(f32[32,1,2]{2,1,0:T(1,128)} %broadcast_in_dim.7), calls=%async_computation.2 | async-start | bytes 32768 | tf_op jit(solution)/shard_map/all_to_all | solution.py:35
  351.2 8.6 %all-to-all-done.2 = f32[32,1,2]{2,1,0:T(1,128)S(1)} async-done(((f32[32,1,2]{2,1,0:T(1,128)}), f32[32,1,2]{2,1,0:T(1,128)S(1)}, u32[]{:S(2)}, u32[]{:S(2)}) %all-to-all-start.2) | async-done | bytes 288 | tf_op jit(solution)/shard_map/all_to_all | solution.py:35
  371.5 3.7 collective-permute-start.56
  380.0 2.8 collective-permute-start.52
  382.8 3.3 collective-permute-done.52
  388.3 3.3 collective-permute-done.53
  394.0 4.5 collective-permute-start.57
  402.3 7.5 %collective-permute-start.58 = (f32[512,64]{0,1:T(8,128)S(1)}, f32[512,64]{0,1:T(8,128)S(1)}, u32[]{:S(2)}, u32[]{:S(2)}) collective-permute-start(f32[512,64]{0,1:T(8,128)S(1)} %add.420), channel_id=1, source_target_pairs={{0,32},{8,40},{16,48},{24,56},{32,0},{40,8},{48,16},{56,24},{1,33}... | collective-permute-start | bytes 393224 | tf_op jit(solution)/shard_map/ppermute | solution.py:25
  409.8 3.5 collective-permute-done.58
  416.7 8.7 %collective-permute-start.59 = (f32[256,32]{0,1:T(8,128)S(1)}, f32[256,32]{0,1:T(8,128)S(1)}, u32[]{:S(2)}, u32[]{:S(2)}) collective-permute-start(f32[256,32]{0,1:T(8,128)S(1)} %convolution_add_fusion), channel_id=1, source_target_pairs={{0,1},{1,0},{2,3},{3,2},{4,5},{5,4},{6,7},{7,6},{8,9},{9,8},{10,11... | collective-permute-start | bytes 98312 | tf_op jit(solution)/shard_map/ppermute | solution.py:25
  432.3 2.8 collective-permute-start.61
  435.1 3.3 collective-permute-done.61
  438.5 3.9 collective-permute-start.62
  444.0 7.5 %collective-permute-start.63 = (f32[256,32]{0,1:T(8,128)S(1)}, f32[256,32]{0,1:T(8,128)S(1)}, u32[]{:S(2)}, u32[]{:S(2)}) collective-permute-start(f32[256,32]{0,1:T(8,128)S(1)} %add.427), channel_id=1, source_target_pairs={{0,256},{128,384},{256,0},{384,128},{1,257},{129,385},{257,1},{385... | collective-permute-start | bytes 98312 | tf_op jit(solution)/shard_map/ppermute | solution.py:25
  456.2 3.1 collective-permute-start.64
  459.3 4.7 collective-permute-start.70
  465.3 3.4 collective-permute-start.65
  468.7 7.1 %collective-permute-start.71 = (f32[512,64]{0,1:T(8,128)S(1)}, f32[512,64]{0,1:T(8,128)S(1)}, u32[]{:S(2)}, u32[]{:S(2)}) collective-permute-start(f32[512,64]{0,1:T(8,128)S(1)} %add.436), channel_id=1, source_target_pairs={{0,32},{8,40},{16,48},{24,56},{32,0},{40,8},{48,16},{56,24},{1,33}... | collective-permute-start | bytes 393224 | tf_op jit(solution)/shard_map/ppermute | solution.py:25
  484.6 6.0 %collective-permute-done.67 = f32[2]{0:T(128)S(1)} collective-permute-done((f32[2]{0:T(128)S(1)}, f32[2]{0:T(128)S(1)}, u32[]{:S(2)}, u32[]{:S(2)}) %collective-permute-start.67) | collective-permute-done | bytes 40 | tf_op jit(solution)/shard_map/ppermute | solution.py:25
  493.2 15.1 %all-to-all-start.3 = ((f32[32,1,2]{2,1,0:T(1,128)}), f32[32,1,2]{2,1,0:T(1,128)S(1)}, u32[]{:S(2)}, u32[]{:S(2)}) async-start(f32[32,1,2]{2,1,0:T(1,128)} %broadcast_in_dim.8), calls=%async_computation.3 | async-start | bytes 32768 | tf_op jit(solution)/shard_map/all_to_all | solution.py:35
  508.9 8.6 %all-to-all-done.3 = f32[32,1,2]{2,1,0:T(1,128)S(1)} async-done(((f32[32,1,2]{2,1,0:T(1,128)}), f32[32,1,2]{2,1,0:T(1,128)S(1)}, u32[]{:S(2)}, u32[]{:S(2)}) %all-to-all-start.3) | async-done | bytes 288 | tf_op jit(solution)/shard_map/all_to_all | solution.py:35
  (250 shorter events, 161.0 us)
Async XLA Ops:
  4.9 41.1 %all-to-all-start = ((f32[4,2,64,512]{3,2,1,0:T(8,128)}), f32[4,2,64,512]{3,2,1,0:T(8,128)S(1)}, u32[]{:S(2)}, u32[]{:S(2)}) async-start(f32[4,2,64,512]{3,2,1,0:T(8,128)} %copy.27), calls=%async_computation | async-start | bytes 2097152 | tf_op jit(solution)/shard_map/all_to_all | solution.py:59
  18.1 10.5 %collective-permute-start.3 = (f32[64,32]{0,1:T(8,128)S(1)}, f32[64,32]{0,1:T(8,128)S(1)}, u32[]{:S(2)}, u32[]{:S(2)}) collective-permute-start(f32[64,32]{0,1:T(8,128)S(1)} %maximum_select_fusion.4), channel_id=1, source_target_pairs={{0,16},{8,24},{16,0},{24,8},{32,48},{40,56},{48,32},{56,40},{1,17}... | collective-permute-start | bytes 24584 | tf_op jit(solution)/shard_map/ppermute | solution.py:46
  23.9 15.5 %collective-permute-start = (f32[64,32]{0,1:T(8,128)S(1)}, f32[64,32]{0,1:T(8,128)S(1)}, u32[]{:S(2)}, u32[]{:S(2)}) collective-permute-start(f32[64,32]{0,1:T(8,128)S(1)} %broadcast_divide_fusion.5), channel_id=1, source_target_pairs={{0,128},{128,0},{256,384},{384,256},{1,129},{129,1},{257,385},{385... | collective-permute-start | bytes 24584 | tf_op jit(solution)/shard_map/ppermute | solution.py:46
  28.7 15.4 %collective-permute-start.4 = (f32[128,32]{0,1:T(8,128)S(1)}, f32[128,32]{0,1:T(8,128)S(1)}, u32[]{:S(2)}, u32[]{:S(2)}) collective-permute-start(f32[128,32]{0,1:T(8,128)S(1)} %maximum_select_fusion.5), channel_id=1, source_target_pairs={{0,32},{8,40},{16,48},{24,56},{32,0},{40,8},{48,16},{56,24},{1,33}... | collective-permute-start | bytes 49160 | tf_op jit(solution)/shard_map/ppermute | solution.py:46
  39.5 8.4 %collective-permute-start.1 = (f32[128,32]{0,1:T(8,128)S(1)}, f32[128,32]{0,1:T(8,128)S(1)}, u32[]{:S(2)}, u32[]{:S(2)}) collective-permute-start(f32[128,32]{0,1:T(8,128)S(1)} %maximum_select_fusion.3), channel_id=1, source_target_pairs={{0,256},{128,384},{256,0},{384,128},{1,257},{129,385},{257,1},{385... | collective-permute-start | bytes 49160 | tf_op jit(solution)/shard_map/ppermute | solution.py:46
  50.7 7.8 %collective-permute-start.11 = (f32[512,64]{0,1:T(8,128)S(1)}, f32[512,64]{0,1:T(8,128)S(1)}, u32[]{:S(2)}, u32[]{:S(2)}) collective-permute-start(f32[512,64]{0,1:T(8,128)S(1)} %pad_maximum_fusion.1), channel_id=1, source_target_pairs={{0,64},{64,0},{1,65},{65,1},{2,66},{66,2},{3,67},{67,3},{4,68},{68... | collective-permute-start | bytes 393224 | tf_op jit(solution)/shard_map/ppermute | solution.py:25
  53.7 8.6 %collective-permute-start.6 = (f32[256,32]{0,1:T(8,128)S(1)}, f32[256,32]{0,1:T(8,128)S(1)}, u32[]{:S(2)}, u32[]{:S(2)}) collective-permute-start(f32[256,32]{0,1:T(8,128)S(1)} %convolution_add_fusion.5), channel_id=1, source_target_pairs={{0,1},{1,0},{2,3},{3,2},{4,5},{5,4},{6,7},{7,6},{8,9},{9,8},{10,11... | collective-permute-start | bytes 98312 | tf_op jit(solution)/shard_map/ppermute | solution.py:25
  58.5 24.1 %collective-permute-start.12 = (f32[512,64]{0,1:T(8,128)S(1)}, f32[512,64]{0,1:T(8,128)S(1)}, u32[]{:S(2)}, u32[]{:S(2)}) collective-permute-start(f32[512,64]{0,1:T(8,128)S(1)} %fusion.44), channel_id=1, source_target_pairs={{0,8},{8,0},{16,24},{24,16},{32,40},{40,32},{48,56},{56,48},{1,9},... | collective-permute-start | bytes 393224 | tf_op jit(solution)/shard_map/ppermute | solution.py:25
  67.0 6.2 %collective-permute-start.8 = (f32[256,32]{0,1:T(8,128)S(1)}, f32[256,32]{0,1:T(8,128)S(1)}, u32[]{:S(2)}, u32[]{:S(2)}) collective-permute-start(f32[256,32]{0,1:T(8,128)S(1)} %add.348), channel_id=1, source_target_pairs={{0,4},{2,6},{4,0},{6,2},{1,5},{3,7},{5,1},{7,3},{8,12},{10,14},{12... | collective-permute-start | bytes 98312 | tf_op jit(solution)/shard_map/ppermute | solution.py:25
  73.2 5.7 %collective-permute-start.9 = (f32[256,32]{0,1:T(8,128)S(1)}, f32[256,32]{0,1:T(8,128)S(1)}, u32[]{:S(2)}, u32[]{:S(2)}) collective-permute-start(f32[256,32]{0,1:T(8,128)S(1)} %add.349), channel_id=1, source_target_pairs={{0,128},{128,0},{256,384},{384,256},{1,129},{129,1},{257,385},{385... | collective-permute-start | bytes 98312 | tf_op jit(solution)/shard_map/ppermute | solution.py:25
  78.9 9.4 %collective-permute-start.10 = (f32[256,32]{0,1:T(8,128)S(1)}, f32[256,32]{0,1:T(8,128)S(1)}, u32[]{:S(2)}, u32[]{:S(2)}) collective-permute-start(f32[256,32]{0,1:T(8,128)S(1)} %add.350), channel_id=1, source_target_pairs={{0,256},{128,384},{256,0},{384,128},{1,257},{129,385},{257,1},{385... | collective-permute-start | bytes 98312 | tf_op jit(solution)/shard_map/ppermute | solution.py:25
  82.6 9.3 %collective-permute-start.13 = (f32[512,64]{0,1:T(8,128)S(1)}, f32[512,64]{0,1:T(8,128)S(1)}, u32[]{:S(2)}, u32[]{:S(2)}) collective-permute-start(f32[512,64]{0,1:T(8,128)S(1)} %add.353), channel_id=1, source_target_pairs={{0,16},{8,24},{16,0},{24,8},{32,48},{40,56},{48,32},{56,40},{1,17}... | collective-permute-start | bytes 393224 | tf_op jit(solution)/shard_map/ppermute | solution.py:25
  92.0 12.4 %collective-permute-start.14 = (f32[512,64]{0,1:T(8,128)S(1)}, f32[512,64]{0,1:T(8,128)S(1)}, u32[]{:S(2)}, u32[]{:S(2)}) collective-permute-start(f32[512,64]{0,1:T(8,128)S(1)} %add.354), channel_id=1, source_target_pairs={{0,32},{8,40},{16,48},{24,56},{32,0},{40,8},{48,16},{56,24},{1,33}... | collective-permute-start | bytes 393224 | tf_op jit(solution)/shard_map/ppermute | solution.py:25
  107.8 11.5 %collective-permute-start.15 = (f32[256,32]{0,1:T(8,128)S(1)}, f32[256,32]{0,1:T(8,128)S(1)}, u32[]{:S(2)}, u32[]{:S(2)}) collective-permute-start(f32[256,32]{0,1:T(8,128)S(1)} %convolution_add_fusion.4), channel_id=1, source_target_pairs={{0,1},{1,0},{2,3},{3,2},{4,5},{5,4},{6,7},{7,6},{8,9},{9,8},{10,11... | collective-permute-start | bytes 98312 | tf_op jit(solution)/shard_map/ppermute | solution.py:25
  117.3 24.0 %collective-permute-start.24 = (f32[512,64]{0,1:T(8,128)S(1)}, f32[512,64]{0,1:T(8,128)S(1)}, u32[]{:S(2)}, u32[]{:S(2)}) collective-permute-start(f32[512,64]{0,1:T(8,128)S(1)} %pad_maximum_fusion.2), channel_id=1, source_target_pairs={{0,64},{64,0},{1,65},{65,1},{2,66},{66,2},{3,67},{67,3},{4,68},{68... | collective-permute-start | bytes 393224 | tf_op jit(solution)/shard_map/ppermute | solution.py:25
  124.3 6.2 %collective-permute-start.17 = (f32[256,32]{0,1:T(8,128)S(1)}, f32[256,32]{0,1:T(8,128)S(1)}, u32[]{:S(2)}, u32[]{:S(2)}) collective-permute-start(f32[256,32]{0,1:T(8,128)S(1)} %add.359), channel_id=1, source_target_pairs={{0,4},{2,6},{4,0},{6,2},{1,5},{3,7},{5,1},{7,3},{8,12},{10,14},{12... | collective-permute-start | bytes 98312 | tf_op jit(solution)/shard_map/ppermute | solution.py:25
  130.4 5.5 %collective-permute-start.18 = (f32[256,32]{0,1:T(8,128)S(1)}, f32[256,32]{0,1:T(8,128)S(1)}, u32[]{:S(2)}, u32[]{:S(2)}) collective-permute-start(f32[256,32]{0,1:T(8,128)S(1)} %add.360), channel_id=1, source_target_pairs={{0,128},{128,0},{256,384},{384,256},{1,129},{129,1},{257,385},{385... | collective-permute-start | bytes 98312 | tf_op jit(solution)/shard_map/ppermute | solution.py:25
  136.0 8.6 %collective-permute-start.19 = (f32[256,32]{0,1:T(8,128)S(1)}, f32[256,32]{0,1:T(8,128)S(1)}, u32[]{:S(2)}, u32[]{:S(2)}) collective-permute-start(f32[256,32]{0,1:T(8,128)S(1)} %add.361), channel_id=1, source_target_pairs={{0,256},{128,384},{256,0},{384,128},{1,257},{129,385},{257,1},{385... | collective-permute-start | bytes 98312 | tf_op jit(solution)/shard_map/ppermute | solution.py:25
  141.3 8.9 %collective-permute-start.25 = (f32[512,64]{0,1:T(8,128)S(1)}, f32[512,64]{0,1:T(8,128)S(1)}, u32[]{:S(2)}, u32[]{:S(2)}) collective-permute-start(f32[512,64]{0,1:T(8,128)S(1)} %fusion.43), channel_id=1, source_target_pairs={{0,8},{8,0},{16,24},{24,16},{32,40},{40,32},{48,56},{56,48},{1,9},... | collective-permute-start | bytes 393224 | tf_op jit(solution)/shard_map/ppermute | solution.py:25
  147.2 6.2 %collective-permute-start.20 = (f32[2]{0:T(128)S(1)}, f32[2]{0:T(128)S(1)}, u32[]{:S(2)}, u32[]{:S(2)}) collective-permute-start(f32[2]{0:T(128)S(1)} %pad_maximum_fusion.7), channel_id=1, source_target_pairs={{0,64},{64,0},{1,65},{65,1},{2,66},{66,2},{3,67},{67,3},{4,68},{68... | collective-permute-start | bytes 32 | tf_op jit(solution)/shard_map/ppermute | solution.py:25
  150.3 8.0 %collective-permute-start.26 = (f32[512,64]{0,1:T(8,128)S(1)}, f32[512,64]{0,1:T(8,128)S(1)}, u32[]{:S(2)}, u32[]{:S(2)}) collective-permute-start(f32[512,64]{0,1:T(8,128)S(1)} %add.369), channel_id=1, source_target_pairs={{0,16},{8,24},{16,0},{24,8},{32,48},{40,56},{48,32},{56,40},{1,17}... | collective-permute-start | bytes 393224 | tf_op jit(solution)/shard_map/ppermute | solution.py:25
  154.8 11.1 %collective-permute-start.21 = (f32[2]{0:T(128)S(1)}, f32[2]{0:T(128)S(1)}, u32[]{:S(2)}, u32[]{:S(2)}) collective-permute-start(f32[2]{0:T(128)S(1)} %fusion.124), channel_id=1, source_target_pairs={{0,8},{8,0},{16,24},{24,16},{32,40},{40,32},{48,56},{56,48},{1,9},... | collective-permute-start | bytes 32 | tf_op jit(solution)/shard_map/ppermute | solution.py:25
  158.3 22.3 %collective-permute-start.27 = (f32[512,64]{0,1:T(8,128)S(1)}, f32[512,64]{0,1:T(8,128)S(1)}, u32[]{:S(2)}, u32[]{:S(2)}) collective-permute-start(f32[512,64]{0,1:T(8,128)S(1)} %add.370), channel_id=1, source_target_pairs={{0,32},{8,40},{16,48},{24,56},{32,0},{40,8},{48,16},{56,24},{1,33}... | collective-permute-start | bytes 393224 | tf_op jit(solution)/shard_map/ppermute | solution.py:25
  172.4 8.2 %collective-permute-start.23 = (f32[2]{0:T(128)S(1)}, f32[2]{0:T(128)S(1)}, u32[]{:S(2)}, u32[]{:S(2)}) collective-permute-start(f32[2]{0:T(128)S(1)} %add.366), channel_id=1, source_target_pairs={{0,32},{8,40},{16,48},{24,56},{32,0},{40,8},{48,16},{56,24},{1,33}... | collective-permute-start | bytes 32 | tf_op jit(solution)/shard_map/ppermute | solution.py:25
  183.3 26.7 %all-to-all-start.1 = ((f32[32,1,2]{2,1,0:T(1,128)}), f32[32,1,2]{2,1,0:T(1,128)S(1)}, u32[]{:S(2)}, u32[]{:S(2)}) async-start(f32[32,1,2]{2,1,0:T(1,128)} %broadcast_in_dim.6), calls=%async_computation.1 | async-start | bytes 32768 | tf_op jit(solution)/shard_map/all_to_all | solution.py:35
  215.5 6.2 %collective-permute-start.33 = (f32[512,64]{0,1:T(8,128)S(1)}, f32[512,64]{0,1:T(8,128)S(1)}, u32[]{:S(2)}, u32[]{:S(2)}) collective-permute-start(f32[512,64]{0,1:T(8,128)S(1)} %pad_maximum_fusion.3), channel_id=1, source_target_pairs={{0,64},{64,0},{1,65},{65,1},{2,66},{66,2},{3,67},{67,3},{4,68},{68... | collective-permute-start | bytes 393224 | tf_op jit(solution)/shard_map/ppermute | solution.py:25
  218.4 5.3 %collective-permute-start.28 = (f32[256,32]{0,1:T(8,128)S(1)}, f32[256,32]{0,1:T(8,128)S(1)}, u32[]{:S(2)}, u32[]{:S(2)}) collective-permute-start(f32[256,32]{0,1:T(8,128)S(1)} %convolution_add_fusion.3), channel_id=1, source_target_pairs={{0,1},{1,0},{2,3},{3,2},{4,5},{5,4},{6,7},{7,6},{8,9},{9,8},{10,11... | collective-permute-start | bytes 98312 | tf_op jit(solution)/shard_map/ppermute | solution.py:25
  221.8 20.9 %collective-permute-start.34 = (f32[512,64]{0,1:T(8,128)S(1)}, f32[512,64]{0,1:T(8,128)S(1)}, u32[]{:S(2)}, u32[]{:S(2)}) collective-permute-start(f32[512,64]{0,1:T(8,128)S(1)} %fusion.42), channel_id=1, source_target_pairs={{0,8},{8,0},{16,24},{24,16},{32,40},{40,32},{48,56},{56,48},{1,9},... | collective-permute-start | bytes 393224 | tf_op jit(solution)/shard_map/ppermute | solution.py:25
  228.7 6.2 %collective-permute-start.30 = (f32[256,32]{0,1:T(8,128)S(1)}, f32[256,32]{0,1:T(8,128)S(1)}, u32[]{:S(2)}, u32[]{:S(2)}) collective-permute-start(f32[256,32]{0,1:T(8,128)S(1)} %add.381), channel_id=1, source_target_pairs={{0,4},{2,6},{4,0},{6,2},{1,5},{3,7},{5,1},{7,3},{8,12},{10,14},{12... | collective-permute-start | bytes 98312 | tf_op jit(solution)/shard_map/ppermute | solution.py:25
  234.8 5.5 %collective-permute-start.31 = (f32[256,32]{0,1:T(8,128)S(1)}, f32[256,32]{0,1:T(8,128)S(1)}, u32[]{:S(2)}, u32[]{:S(2)}) collective-permute-start(f32[256,32]{0,1:T(8,128)S(1)} %add.382), channel_id=1, source_target_pairs={{0,128},{128,0},{256,384},{384,256},{1,129},{129,1},{257,385},{385... | collective-permute-start | bytes 98312 | tf_op jit(solution)/shard_map/ppermute | solution.py:25
  240.4 8.7 %collective-permute-start.32 = (f32[256,32]{0,1:T(8,128)S(1)}, f32[256,32]{0,1:T(8,128)S(1)}, u32[]{:S(2)}, u32[]{:S(2)}) collective-permute-start(f32[256,32]{0,1:T(8,128)S(1)} %add.383), channel_id=1, source_target_pairs={{0,256},{128,384},{256,0},{384,128},{1,257},{129,385},{257,1},{385... | collective-permute-start | bytes 98312 | tf_op jit(solution)/shard_map/ppermute | solution.py:25
  242.7 8.0 %collective-permute-start.35 = (f32[512,64]{0,1:T(8,128)S(1)}, f32[512,64]{0,1:T(8,128)S(1)}, u32[]{:S(2)}, u32[]{:S(2)}) collective-permute-start(f32[512,64]{0,1:T(8,128)S(1)} %add.386), channel_id=1, source_target_pairs={{0,16},{8,24},{16,0},{24,8},{32,48},{40,56},{48,32},{56,40},{1,17}... | collective-permute-start | bytes 393224 | tf_op jit(solution)/shard_map/ppermute | solution.py:25
  250.8 10.7 %collective-permute-start.36 = (f32[512,64]{0,1:T(8,128)S(1)}, f32[512,64]{0,1:T(8,128)S(1)}, u32[]{:S(2)}, u32[]{:S(2)}) collective-permute-start(f32[512,64]{0,1:T(8,128)S(1)} %add.387), channel_id=1, source_target_pairs={{0,32},{8,40},{16,48},{24,56},{32,0},{40,8},{48,16},{56,24},{1,33}... | collective-permute-start | bytes 393224 | tf_op jit(solution)/shard_map/ppermute | solution.py:25
  264.8 11.1 %collective-permute-start.37 = (f32[256,32]{0,1:T(8,128)S(1)}, f32[256,32]{0,1:T(8,128)S(1)}, u32[]{:S(2)}, u32[]{:S(2)}) collective-permute-start(f32[256,32]{0,1:T(8,128)S(1)} %convolution_add_fusion.2), channel_id=1, source_target_pairs={{0,1},{1,0},{2,3},{3,2},{4,5},{5,4},{6,7},{7,6},{8,9},{9,8},{10,11... | collective-permute-start | bytes 98312 | tf_op jit(solution)/shard_map/ppermute | solution.py:25
  274.0 25.5 %collective-permute-start.46 = (f32[512,64]{0,1:T(8,128)S(1)}, f32[512,64]{0,1:T(8,128)S(1)}, u32[]{:S(2)}, u32[]{:S(2)}) collective-permute-start(f32[512,64]{0,1:T(8,128)S(1)} %pad_maximum_fusion.4), channel_id=1, source_target_pairs={{0,64},{64,0},{1,65},{65,1},{2,66},{66,2},{3,67},{67,3},{4,68},{68... | collective-permute-start | bytes 393224 | tf_op jit(solution)/shard_map/ppermute | solution.py:25
  281.0 6.2 %collective-permute-start.39 = (f32[256,32]{0,1:T(8,128)S(1)}, f32[256,32]{0,1:T(8,128)S(1)}, u32[]{:S(2)}, u32[]{:S(2)}) collective-permute-start(f32[256,32]{0,1:T(8,128)S(1)} %add.392), channel_id=1, source_target_pairs={{0,4},{2,6},{4,0},{6,2},{1,5},{3,7},{5,1},{7,3},{8,12},{10,14},{12... | collective-permute-start | bytes 98312 | tf_op jit(solution)/shard_map/ppermute | solution.py:25
  287.1 5.5 %collective-permute-start.40 = (f32[256,32]{0,1:T(8,128)S(1)}, f32[256,32]{0,1:T(8,128)S(1)}, u32[]{:S(2)}, u32[]{:S(2)}) collective-permute-start(f32[256,32]{0,1:T(8,128)S(1)} %add.393), channel_id=1, source_target_pairs={{0,128},{128,0},{256,384},{384,256},{1,129},{129,1},{257,385},{385... | collective-permute-start | bytes 98312 | tf_op jit(solution)/shard_map/ppermute | solution.py:25
  292.7 9.7 %collective-permute-start.41 = (f32[256,32]{0,1:T(8,128)S(1)}, f32[256,32]{0,1:T(8,128)S(1)}, u32[]{:S(2)}, u32[]{:S(2)}) collective-permute-start(f32[256,32]{0,1:T(8,128)S(1)} %add.394), channel_id=1, source_target_pairs={{0,256},{128,384},{256,0},{384,128},{1,257},{129,385},{257,1},{385... | collective-permute-start | bytes 98312 | tf_op jit(solution)/shard_map/ppermute | solution.py:25
  299.6 8.5 %collective-permute-start.47 = (f32[512,64]{0,1:T(8,128)S(1)}, f32[512,64]{0,1:T(8,128)S(1)}, u32[]{:S(2)}, u32[]{:S(2)}) collective-permute-start(f32[512,64]{0,1:T(8,128)S(1)} %fusion.41), channel_id=1, source_target_pairs={{0,8},{8,0},{16,24},{24,16},{32,40},{40,32},{48,56},{56,48},{1,9},... | collective-permute-start | bytes 393224 | tf_op jit(solution)/shard_map/ppermute | solution.py:25
  305.1 7.2 %collective-permute-start.42 = (f32[2]{0:T(128)S(1)}, f32[2]{0:T(128)S(1)}, u32[]{:S(2)}, u32[]{:S(2)}) collective-permute-start(f32[2]{0:T(128)S(1)} %pad_maximum_fusion.9), channel_id=1, source_target_pairs={{0,64},{64,0},{1,65},{65,1},{2,66},{66,2},{3,67},{67,3},{4,68},{68... | collective-permute-start | bytes 32 | tf_op jit(solution)/shard_map/ppermute | solution.py:25
  308.1 8.0 %collective-permute-start.48 = (f32[512,64]{0,1:T(8,128)S(1)}, f32[512,64]{0,1:T(8,128)S(1)}, u32[]{:S(2)}, u32[]{:S(2)}) collective-permute-start(f32[512,64]{0,1:T(8,128)S(1)} %add.402), channel_id=1, source_target_pairs={{0,16},{8,24},{16,0},{24,8},{32,48},{40,56},{48,32},{56,40},{1,17}... | collective-permute-start | bytes 393224 | tf_op jit(solution)/shard_map/ppermute | solution.py:25
  316.2 16.8 %collective-permute-start.49 = (f32[512,64]{0,1:T(8,128)S(1)}, f32[512,64]{0,1:T(8,128)S(1)}, u32[]{:S(2)}, u32[]{:S(2)}) collective-permute-start(f32[512,64]{0,1:T(8,128)S(1)} %add.403), channel_id=1, source_target_pairs={{0,32},{8,40},{16,48},{24,56},{32,0},{40,8},{48,16},{56,24},{1,33}... | collective-permute-start | bytes 393224 | tf_op jit(solution)/shard_map/ppermute | solution.py:25
  324.7 8.3 %collective-permute-start.45 = (f32[2]{0:T(128)S(1)}, f32[2]{0:T(128)S(1)}, u32[]{:S(2)}, u32[]{:S(2)}) collective-permute-start(f32[2]{0:T(128)S(1)} %add.399), channel_id=1, source_target_pairs={{0,32},{8,40},{16,48},{24,56},{32,0},{40,8},{48,16},{56,24},{1,33}... | collective-permute-start | bytes 32 | tf_op jit(solution)/shard_map/ppermute | solution.py:25
  335.7 24.1 %all-to-all-start.2 = ((f32[32,1,2]{2,1,0:T(1,128)}), f32[32,1,2]{2,1,0:T(1,128)S(1)}, u32[]{:S(2)}, u32[]{:S(2)}) async-start(f32[32,1,2]{2,1,0:T(1,128)} %broadcast_in_dim.7), calls=%async_computation.2 | async-start | bytes 32768 | tf_op jit(solution)/shard_map/all_to_all | solution.py:35
  365.3 6.2 %collective-permute-start.55 = (f32[512,64]{0,1:T(8,128)S(1)}, f32[512,64]{0,1:T(8,128)S(1)}, u32[]{:S(2)}, u32[]{:S(2)}) collective-permute-start(f32[512,64]{0,1:T(8,128)S(1)} %pad_maximum_fusion.5), channel_id=1, source_target_pairs={{0,64},{64,0},{1,65},{65,1},{2,66},{66,2},{3,67},{67,3},{4,68},{68... | collective-permute-start | bytes 393224 | tf_op jit(solution)/shard_map/ppermute | solution.py:25
  367.8 7.5 %collective-permute-start.50 = (f32[256,32]{0,1:T(8,128)S(1)}, f32[256,32]{0,1:T(8,128)S(1)}, u32[]{:S(2)}, u32[]{:S(2)}) collective-permute-start(f32[256,32]{0,1:T(8,128)S(1)} %convolution_add_fusion.1), channel_id=1, source_target_pairs={{0,1},{1,0},{2,3},{3,2},{4,5},{5,4},{6,7},{7,6},{8,9},{9,8},{10,11... | collective-permute-start | bytes 98312 | tf_op jit(solution)/shard_map/ppermute | solution.py:25
  371.5 22.5 %collective-permute-start.56 = (f32[512,64]{0,1:T(8,128)S(1)}, f32[512,64]{0,1:T(8,128)S(1)}, u32[]{:S(2)}, u32[]{:S(2)}) collective-permute-start(f32[512,64]{0,1:T(8,128)S(1)} %fusion.40), channel_id=1, source_target_pairs={{0,8},{8,0},{16,24},{24,16},{32,40},{40,32},{48,56},{56,48},{1,9},... | collective-permute-start | bytes 393224 | tf_op jit(solution)/shard_map/ppermute | solution.py:25
  380.0 6.2 %collective-permute-start.52 = (f32[256,32]{0,1:T(8,128)S(1)}, f32[256,32]{0,1:T(8,128)S(1)}, u32[]{:S(2)}, u32[]{:S(2)}) collective-permute-start(f32[256,32]{0,1:T(8,128)S(1)} %add.414), channel_id=1, source_target_pairs={{0,4},{2,6},{4,0},{6,2},{1,5},{3,7},{5,1},{7,3},{8,12},{10,14},{12... | collective-permute-start | bytes 98312 | tf_op jit(solution)/shard_map/ppermute | solution.py:25
  386.1 5.5 %collective-permute-start.53 = (f32[256,32]{0,1:T(8,128)S(1)}, f32[256,32]{0,1:T(8,128)S(1)}, u32[]{:S(2)}, u32[]{:S(2)}) collective-permute-start(f32[256,32]{0,1:T(8,128)S(1)} %add.415), channel_id=1, source_target_pairs={{0,128},{128,0},{256,384},{384,256},{1,129},{129,1},{257,385},{385... | collective-permute-start | bytes 98312 | tf_op jit(solution)/shard_map/ppermute | solution.py:25
  391.7 8.7 %collective-permute-start.54 = (f32[256,32]{0,1:T(8,128)S(1)}, f32[256,32]{0,1:T(8,128)S(1)}, u32[]{:S(2)}, u32[]{:S(2)}) collective-permute-start(f32[256,32]{0,1:T(8,128)S(1)} %add.416), channel_id=1, source_target_pairs={{0,256},{128,384},{256,0},{384,128},{1,257},{129,385},{257,1},{385... | collective-permute-start | bytes 98312 | tf_op jit(solution)/shard_map/ppermute | solution.py:25
  394.0 8.3 %collective-permute-start.57 = (f32[512,64]{0,1:T(8,128)S(1)}, f32[512,64]{0,1:T(8,128)S(1)}, u32[]{:S(2)}, u32[]{:S(2)}) collective-permute-start(f32[512,64]{0,1:T(8,128)S(1)} %add.419), channel_id=1, source_target_pairs={{0,16},{8,24},{16,0},{24,8},{32,48},{40,56},{48,32},{56,40},{1,17}... | collective-permute-start | bytes 393224 | tf_op jit(solution)/shard_map/ppermute | solution.py:25
  402.3 11.0 %collective-permute-start.58 = (f32[512,64]{0,1:T(8,128)S(1)}, f32[512,64]{0,1:T(8,128)S(1)}, u32[]{:S(2)}, u32[]{:S(2)}) collective-permute-start(f32[512,64]{0,1:T(8,128)S(1)} %add.420), channel_id=1, source_target_pairs={{0,32},{8,40},{16,48},{24,56},{32,0},{40,8},{48,16},{56,24},{1,33}... | collective-permute-start | bytes 393224 | tf_op jit(solution)/shard_map/ppermute | solution.py:25
  416.7 10.6 %collective-permute-start.59 = (f32[256,32]{0,1:T(8,128)S(1)}, f32[256,32]{0,1:T(8,128)S(1)}, u32[]{:S(2)}, u32[]{:S(2)}) collective-permute-start(f32[256,32]{0,1:T(8,128)S(1)} %convolution_add_fusion), channel_id=1, source_target_pairs={{0,1},{1,0},{2,3},{3,2},{4,5},{5,4},{6,7},{7,6},{8,9},{9,8},{10,11... | collective-permute-start | bytes 98312 | tf_op jit(solution)/shard_map/ppermute | solution.py:25
  425.4 26.1 %collective-permute-start.68 = (f32[512,64]{0,1:T(8,128)S(1)}, f32[512,64]{0,1:T(8,128)S(1)}, u32[]{:S(2)}, u32[]{:S(2)}) collective-permute-start(f32[512,64]{0,1:T(8,128)S(1)} %pad_maximum_fusion.6), channel_id=1, source_target_pairs={{0,64},{64,0},{1,65},{65,1},{2,66},{66,2},{3,67},{67,3},{4,68},{68... | collective-permute-start | bytes 393224 | tf_op jit(solution)/shard_map/ppermute | solution.py:25
  432.3 6.2 %collective-permute-start.61 = (f32[256,32]{0,1:T(8,128)S(1)}, f32[256,32]{0,1:T(8,128)S(1)}, u32[]{:S(2)}, u32[]{:S(2)}) collective-permute-start(f32[256,32]{0,1:T(8,128)S(1)} %add.425), channel_id=1, source_target_pairs={{0,4},{2,6},{4,0},{6,2},{1,5},{3,7},{5,1},{7,3},{8,12},{10,14},{12... | collective-permute-start | bytes 98312 | tf_op jit(solution)/shard_map/ppermute | solution.py:25
  438.5 5.5 %collective-permute-start.62 = (f32[256,32]{0,1:T(8,128)S(1)}, f32[256,32]{0,1:T(8,128)S(1)}, u32[]{:S(2)}, u32[]{:S(2)}) collective-permute-start(f32[256,32]{0,1:T(8,128)S(1)} %add.426), channel_id=1, source_target_pairs={{0,128},{128,0},{256,384},{384,256},{1,129},{129,1},{257,385},{385... | collective-permute-start | bytes 98312 | tf_op jit(solution)/shard_map/ppermute | solution.py:25
  444.0 9.4 %collective-permute-start.63 = (f32[256,32]{0,1:T(8,128)S(1)}, f32[256,32]{0,1:T(8,128)S(1)}, u32[]{:S(2)}, u32[]{:S(2)}) collective-permute-start(f32[256,32]{0,1:T(8,128)S(1)} %add.427), channel_id=1, source_target_pairs={{0,256},{128,384},{256,0},{384,128},{1,257},{129,385},{257,1},{385... | collective-permute-start | bytes 98312 | tf_op jit(solution)/shard_map/ppermute | solution.py:25
  451.5 7.7 %collective-permute-start.69 = (f32[512,64]{0,1:T(8,128)S(1)}, f32[512,64]{0,1:T(8,128)S(1)}, u32[]{:S(2)}, u32[]{:S(2)}) collective-permute-start(f32[512,64]{0,1:T(8,128)S(1)} %fusion.39), channel_id=1, source_target_pairs={{0,8},{8,0},{16,24},{24,16},{32,40},{40,32},{48,56},{56,48},{1,9},... | collective-permute-start | bytes 393224 | tf_op jit(solution)/shard_map/ppermute | solution.py:25
  456.2 7.8 %collective-permute-start.64 = (f32[2]{0:T(128)S(1)}, f32[2]{0:T(128)S(1)}, u32[]{:S(2)}, u32[]{:S(2)}) collective-permute-start(f32[2]{0:T(128)S(1)} %pad_maximum_fusion.11), channel_id=1, source_target_pairs={{0,64},{64,0},{1,65},{65,1},{2,66},{66,2},{3,67},{67,3},{4,68},{68... | collective-permute-start | bytes 32 | tf_op jit(solution)/shard_map/ppermute | solution.py:25
  459.3 9.4 %collective-permute-start.70 = (f32[512,64]{0,1:T(8,128)S(1)}, f32[512,64]{0,1:T(8,128)S(1)}, u32[]{:S(2)}, u32[]{:S(2)}) collective-permute-start(f32[512,64]{0,1:T(8,128)S(1)} %add.435), channel_id=1, source_target_pairs={{0,16},{8,24},{16,0},{24,8},{32,48},{40,56},{48,32},{56,40},{1,17}... | collective-permute-start | bytes 393224 | tf_op jit(solution)/shard_map/ppermute | solution.py:25
  465.3 10.5 %collective-permute-start.65 = (f32[2]{0:T(128)S(1)}, f32[2]{0:T(128)S(1)}, u32[]{:S(2)}, u32[]{:S(2)}) collective-permute-start(f32[2]{0:T(128)S(1)} %fusion.122), channel_id=1, source_target_pairs={{0,8},{8,0},{16,24},{24,16},{32,40},{40,32},{48,56},{56,48},{1,9},... | collective-permute-start | bytes 32 | tf_op jit(solution)/shard_map/ppermute | solution.py:25
  468.7 21.9 %collective-permute-start.71 = (f32[512,64]{0,1:T(8,128)S(1)}, f32[512,64]{0,1:T(8,128)S(1)}, u32[]{:S(2)}, u32[]{:S(2)}) collective-permute-start(f32[512,64]{0,1:T(8,128)S(1)} %add.436), channel_id=1, source_target_pairs={{0,32},{8,40},{16,48},{24,56},{32,0},{40,8},{48,16},{56,24},{1,33}... | collective-permute-start | bytes 393224 | tf_op jit(solution)/shard_map/ppermute | solution.py:25
  482.4 8.2 %collective-permute-start.67 = (f32[2]{0:T(128)S(1)}, f32[2]{0:T(128)S(1)}, u32[]{:S(2)}, u32[]{:S(2)}) collective-permute-start(f32[2]{0:T(128)S(1)} %add.432), channel_id=1, source_target_pairs={{0,32},{8,40},{16,48},{24,56},{32,0},{40,8},{48,16},{56,24},{1,33}... | collective-permute-start | bytes 32 | tf_op jit(solution)/shard_map/ppermute | solution.py:25
  493.2 24.3 %all-to-all-start.3 = ((f32[32,1,2]{2,1,0:T(1,128)}), f32[32,1,2]{2,1,0:T(1,128)S(1)}, u32[]{:S(2)}, u32[]{:S(2)}) async-start(f32[32,1,2]{2,1,0:T(1,128)} %broadcast_in_dim.8), calls=%async_computation.3 | async-start | bytes 32768 | tf_op jit(solution)/shard_map/all_to_all | solution.py:35
  (15 other events, 72.3 us)
